TPU v7x, 128 devices: a whole 4x4x4 slice. The times are simulated.
128 devices in a mesh: lat: 32 (over z, y, core), chan: 4 (over x).
Axes of the slice: x: 4, y: 4, z: 4, core: 2. Of those that a mesh axis runs over, the one named last changes fastest.
Arguments:
- field: bfloat16 [32, 3, 2, 512, 4096], P('chan', None, None, 'lat'), may hold values from -6 to 6
- mix_weight: bfloat16 [32, 32], replicated, may hold values from -1 to 1
- spectral_gain: float32 [32, 2048], P('chan'), may hold values from 0.05 to 1
- legendre: bfloat16 [2, 512, 512, 1024], P(None, 'lat'), may hold values from -0.25 to 0.25
- slot_mode: int32 [512], replicated, may hold values from 0 to 511, as said below
Outputs:
- layered: bfloat16 [32, 3, 2, 512, 4096], P('chan', None, None, 'lat')
Inputs may be any that keep to these rules, and one draw needn't show every extreme that they name: `slot_mode`: A permutation of the mode indices; slots 2 j and 2 j + 1 carry the modes k and 511 - k for some k, so the slots of every index of lat carry whole such pairs.
All inputs are finite; a program needn't handle non-finite values.
Results may differ from a plain program's by a relative error of at most 0.0085.
Values may be sent and summed in bfloat16 or wider, within the bound.
No kernel may reach another device: no remote copies, remote signals or barrier semaphores. Data moves between devices by JAX's collectives and lax.ppermute only.
A program may use at most 192 MiB of HBM per device.

v0:
```python
import math

import jax
import jax.numpy as jnp
from jax import lax
from jax.sharding import PartitionSpec as P


def local(field, mix_weight, spectral_gain, legendre, slot_mode, n_lat, n_chan):
    chans = field.shape[0]
    fields = field.shape[1]
    cycles = field.shape[3]
    points = field.shape[4]
    total_modes = slot_mode.shape[0]
    degrees = spectral_gain.shape[1]
    half_deg = degrees // 2
    step_size = degrees // total_modes
    period = points // math.gcd(points, step_size)
    devices = n_lat * n_chan
    per_dev = total_modes // devices
    lat_index = lax.axis_index("lat")
    chan_index = lax.axis_index("chan")
    row_count = chans * fields * 2 * cycles

    modes = (slot_mode * step_size).reshape(n_lat, n_chan, per_dev)
    modes = jnp.transpose(modes, (1, 0, 2)).reshape(devices, 1, per_dev)
    quarter = jnp.array([0, points // 4], jnp.int32).reshape(1, 2, 1)
    places = lax.iota(jnp.int32, period)
    turns = (modes[..., None] * places + quarter[..., None]) % points
    basis = jnp.cos(turns.astype(jnp.float32) * (2.0 * math.pi / points)).reshape(-1, period)
    fwd = (basis * math.sqrt(2.0 / points)).astype(jnp.bfloat16)
    ratio = math.sqrt(points / (2.0 * total_modes))
    if ratio == 2.0 ** round(math.log2(ratio)):
        fwd = lax.optimization_barrier(fwd)
        inv = fwd
    else:
        inv = (basis * math.sqrt(1.0 / total_modes)).astype(jnp.bfloat16)
        ratio = 1.0

    flat = field.reshape(-1, points)
    summed = flat[:, :period].astype(jnp.float32)
    for n in range(1, points // period):
        summed = summed + flat[:, n * period : (n + 1) * period].astype(jnp.float32)
    high = summed.astype(jnp.bfloat16)
    low = (summed - high.astype(jnp.float32)).astype(jnp.bfloat16)
    rows = jnp.concatenate([high, low], axis=1)
    spec_t = lax.dot_general(
        jnp.concatenate([fwd, fwd], axis=1), rows, (((1,), (1,)), ((), ())),
        preferred_element_type=jnp.float32,
    ).astype(jnp.bfloat16)

    sent = spec_t.reshape(devices, 2 * per_dev, row_count)
    got = lax.all_to_all(sent, ("chan", "lat"), 0, 0, tiled=True)
    got = got.reshape(n_chan, n_lat, 2, per_dev, chans, fields, 2, cycles)
    sign = jnp.array([[1.0, 1.0], [1.0, -1.0]], jnp.float32)
    weight = mix_weight.astype(jnp.float32).reshape(-1, n_chan, chans)
    mix_fold = (sign[:, None, None, :, None] * jnp.transpose(weight, (0, 2, 1))[None, :, :, None, :])
    mix_fold = mix_fold.astype(jnp.bfloat16)
    folded = jnp.einsum(
        "pokhC,CLqskthr->sptqoLr", mix_fold, got, preferred_element_type=jnp.float32
    ).astype(jnp.bfloat16)
    folded = folded.reshape(per_dev, 2, fields, 2, -1, n_lat * cycles)

    leg = lax.dynamic_slice_in_dim(legendre, chan_index * per_dev, per_dev, 1)
    coefficients = jnp.einsum(
        "sptqor,psri->sptqoi", folded, leg, preferred_element_type=jnp.float32
    )
    all_gain = lax.all_gather(spectral_gain, "chan", axis=0, tiled=True)
    gain_par = jnp.transpose(all_gain.reshape(-1, half_deg, 2), (2, 0, 1))
    own_modes = lax.dynamic_slice_in_dim(
        modes.reshape(-1), (chan_index * n_lat + lat_index) * per_dev, per_dev, 0
    )
    degree = 2 * lax.iota(jnp.int32, half_deg)[None, :] + lax.iota(jnp.int32, 2)[:, None]
    allowed = degree[None, :, :] >= own_modes[:, None, None]
    filtered = jnp.where(
        allowed[:, :, None, None, None, :],
        gain_par[None, :, None, None, :, :] * coefficients,
        0.0,
    ).astype(jnp.bfloat16)
    synthesis = jnp.einsum(
        "sptqoi,psri->sptqor", filtered, leg, preferred_element_type=jnp.float32
    )
    back = jnp.stack(
        [synthesis[:, 0] + synthesis[:, 1], synthesis[:, 0] - synthesis[:, 1]], axis=1
    ).astype(jnp.bfloat16)
    back = back.reshape(per_dev, 2, fields, 2, n_chan, chans, n_lat, cycles)
    leaving = jnp.transpose(back, (4, 6, 3, 0, 5, 2, 1, 7)).reshape(devices, 2 * per_dev, row_count)
    returned = lax.all_to_all(leaving, ("chan", "lat"), 0, 0, tiled=True)
    returned = returned.reshape(2 * total_modes, row_count)

    waveform = lax.dot_general(
        returned, inv, (((0,), (0,)), ((), ())), preferred_element_type=jnp.float32
    ) * ratio
    waveform = waveform.reshape(chans, fields, -1, period)
    primal_h = waveform[:, 0]
    sigmoid_h = jax.nn.sigmoid(primal_h)
    slope_h = sigmoid_h * (1.0 + primal_h * (1.0 - sigmoid_h))
    gain_h = primal_h * sigmoid_h
    flat = field.reshape(chans, fields, -1, points)
    pieces = []
    for n in range(points // period):
        initial = flat[:, :, :, n * period : (n + 1) * period].astype(jnp.float32)
        primal = initial[:, 0] + gain_h
        tangents = initial[:, 1:] + slope_h[:, None] * waveform[:, 1:]
        pieces.append(jnp.concatenate([primal[:, None], tangents], axis=1).astype(jnp.bfloat16))
    out = jnp.concatenate(pieces, axis=3)
    return out.reshape(field.shape)


def solution(mesh):
    n_lat = mesh.shape["lat"]
    n_chan = mesh.shape["chan"]
    placed = (
        P("chan", None, None, "lat", None),
        P(),
        P("chan", None),
        P(None, "lat", None, None),
        P(),
    )

    def body(field, mix_weight, spectral_gain, legendre, slot_mode):
        return local(field, mix_weight, spectral_gain, legendre, slot_mode, n_lat, n_chan)

    return jax.shard_map(
        body,
        mesh=mesh,
        in_specs=placed,
        out_specs=P("chan", None, None, "lat", None),
        check_vma=False,
    )
```

profile of v0, /device:TPU:0, one launch (start us, length us, event | category | flops | bytes accessed | tf_op | source)
XLA Modules:
  0.0 207.4 jit_solution(11617352371418357159)
XLA Ops:
  1.5 3.1 %add.111 = s32[128,2,4,1024]{3,2,1,0:T(4,128)} broadcast(s32[128,4,1024]{2,1,0:T(4,128)S(1)} %iota_multiply_fusion), dimensions={0,2,3} | broadcast | bytes 6291456 | tf_op jit(solution)/shard_map/add | solution.py:29
  4.6 5.3 %add.112 = s32[1024,1024]{1,0:T(8,128)} reshape(s32[128,2,4,1024]{3,2,1,0:T(4,128)} %add.111) | data formatting | bytes 8388608 | tf_op jit(solution)/shard_map/add | solution.py:29
  9.9 17.8 %fusion.10 = bf16[1024,1024]{1,0:T(8,128)(2,1)S(1)} fusion(s32[1024,1024]{1,0:T(8,128)} %add.112, s32[1024]{0:T(1024)S(1)} %add.114), kind=kLoop, calls=%fused_computation.18 | loop fusion | flops 16777216 | bytes 6295552 | tf_op jit(solution)/shard_map/convert_element_type | solution.py:31
  27.7 5.1 %subtract_convert_fusion = (bf16[768,1024]{1,0:T(8,128)(2,1)S(1)}, bf16[768,1024]{1,0:T(8,128)(2,1)S(1)}) fusion(bf16[768,4096]{1,0:T(8,128)(2,1)} %bitcast.68), kind=kLoop, calls=%fused_computation.27 | loop fusion | flops 8650752 | bytes 9437184 | tf_op jit(solution)/shard_map/convert_element_type | solution.py:45
  32.8 4.6 %fusion.33 = bf16[128,8,768]{2,1,0:T(8,128)(2,1)} fusion(bf16[768,1024]{1,0:T(8,128)(2,1)S(1)} %get-tuple-element.5, bf16[768,1024]{1,0:T(8,128)(2,1)S(1)} %get-tuple-element.6, bf16[1024,1024]{1,0:T(8,128)(2,1)S(1)} %fusion.10), kind=kOutput, calls=%fused_computation.50 | convolution fusion | flops 3236691968 | bytes 6815744 | tf_op jit(solution)/shard_map/dot_general | solution.py:47
  37.4 11.1 %all-to-all-start = ((bf16[128,8,768]{2,1,0:T(8,128)(2,1)}), bf16[128,8,768]{2,1,0:T(8,128)(2,1)S(1)}, u32[]{:S(2)}, u32[]{:S(2)}) async-start(bf16[128,8,768]{2,1,0:T(8,128)(2,1)} %fusion.33), calls=%async_computation | async-start | bytes 3145728 | tf_op jit(solution)/shard_map/all_to_all | solution.py:53
  48.8 26.3 %all_gather.3 = f32[32,2048]{1,0:T(8,128)S(1)} all-gather(f32[8,2048]{1,0:T(8,128)S(1)} %copy-done.4), channel_id=1, replica_groups=mesh['lat'=32,'chan'=4] {'chan'}, dimensions={0}, use_global_device_ids=true | all-gather | bytes 327680 | tf_op jit(solution)/shard_map/all_gather | solution.py:68
  77.3 4.6 %reshape.107 = bf16[4,32,2,4,8,3,2,16]{1,0,7,6,5,4,3,2:T(4,128)(2,1)} reshape(bf16[128,8,768]{0,2,1:T(8,128)(2,1)S(1)} %copy.41) | data formatting | bytes 3145728 | tf_op jit(solution)/shard_map/reshape | solution.py:54
  81.9 6.9 %fusion.2 = bf16[4,2,3,2,32,32,16]{4,5,1,6,2,0,3:T(8,128)(2,1)S(1)} fusion(f32[32,8,4]{0,2,1:T(4,128)S(1)} %copy.43, f32[2,2]{1,0:T(2,128)S(1)} %copy-done.6, bf16[4,32,2,4,8,3,2,16]{1,0,7,6,5,4,3,2:T(4,128)(2,1)} %reshape.107), kind=kOutput, calls=%fused_computation.5 | convolution fusion | flops 101457920 | bytes 3149840 | tf_op jit(solution)/shard_map/pokhC,CLqskthr->sptqoLr/dot_general | solution.py:59
  88.8 10.0 %copy.45 = bf16[4,2,3,2,32,32,16]{4,6,5,3,2,1,0:T(8,128)(2,1)} copy(bf16[4,2,3,2,32,32,16]{4,5,1,6,2,0,3:T(8,128)(2,1)S(1)} %fusion.2) | data formatting | bytes 3145728 | tf_op jit(solution)/shard_map/convert_element_type | solution.py:61
  98.8 11.3 %fusion = f32[4,2,3,2,32,512]{5,4,3,2,1,0:T(8,128)} fusion(bf16[4,2,3,2,32,512]{4,5,3,2,1,0:T(8,128)(2,1)} %bitcast.72, f32[2,32,1024]{2,1,0:T(8,128)S(1)} %copy.38, pred[4,2,1024]{2,1,0:T(4,128)(4,1)S(1)} %broadcast_compare_fusion, bf16[2,16,512,1024]{3,2,1,0:T(8,128)(2,1)} %param.10, s32[]{:T(128)S(6)} %select_n.20), kind=kOutput, calls=%fused_computation.3 | convolution fusion | flops 3225944064 | bytes 26485760 | tf_op jit(solution)/shard_map/sptqoi,psri->sptqor/dot_general | solution.py:80
  110.1 2.4 %add_convert_fusion = (bf16[4,1,3,2,32,512]{5,4,3,2,1,0:T(8,128)(2,1)S(1)}, bf16[4,1,3,2,32,512]{5,4,3,2,1,0:T(8,128)(2,1)S(1)}) fusion(f32[4,2,3,2,32,512]{5,4,3,2,1,0:T(8,128)} %fusion), kind=kLoop, calls=%fused_computation.49 | loop fusion | flops 1572864 | bytes 4718592 | tf_op jit(solution)/shard_map/convert.21
  112.5 6.4 %stack.9 = bf16[4,1,3,2,4,8,32,16]{7,6,5,4,3,2,0,1:T(8,128)(2,1)} reshape(bf16[4,1,3,2,32,512]{5,4,3,2,1,0:T(8,128)(2,1)S(1)} %get-tuple-element.20) | data formatting | bytes 1572864 | tf_op jit(solution)/shard_map/stack | solution.py:83
  118.9 6.2 %stack.10 = bf16[4,1,3,2,4,8,32,16]{7,6,5,4,3,2,0,1:T(8,128)(2,1)} reshape(bf16[4,1,3,2,32,512]{5,4,3,2,1,0:T(8,128)(2,1)S(1)} %get-tuple-element.21) | data formatting | bytes 1572864 | tf_op jit(solution)/shard_map/stack | solution.py:83
  125.1 11.2 %maximum_bitcast_fusion = bf16[4,32,2,4,8,3,2,16]{7,1,4,0,2,5,3,6:T(8,128)(2,1)} fusion(bf16[4,1,3,2,4,8,32,16]{7,6,5,4,3,2,0,1:T(8,128)(2,1)} %stack.10, bf16[4,1,3,2,4,8,32,16]{7,6,5,4,3,2,0,1:T(8,128)(2,1)} %stack.9), kind=kLoop, calls=%fused_computation | loop fusion | flops 786432 | bytes 3145728 | tf_op jit(solution)/shard_map/transpose | solution.py:87
  136.3 14.3 %copy.48 = bf16[4,32,2,4,8,3,2,16]{1,0,7,6,5,4,3,2:T(4,128)(2,1)} copy(bf16[4,32,2,4,8,3,2,16]{7,1,4,0,2,5,3,6:T(8,128)(2,1)} %maximum_bitcast_fusion) | data formatting | bytes 3145728 | tf_op jit(solution)/shard_map/transpose | solution.py:87
  150.6 7.3 %reshape.110 = bf16[128,8,768]{0,2,1:T(8,128)(2,1)S(1)} reshape(bf16[4,32,2,4,8,3,2,16]{1,0,7,6,5,4,3,2:T(4,128)(2,1)} %copy.48) | data formatting | bytes 3145728 | tf_op jit(solution)/shard_map/reshape | solution.py:87
  157.9 2.0 copy.49
  159.9 9.9 %all-to-all-start.1 = ((bf16[128,8,768]{2,1,0:T(8,128)(2,1)}), bf16[128,8,768]{2,1,0:T(8,128)(2,1)}, u32[]{:S(2)}, u32[]{:S(2)}) async-start(bf16[128,8,768]{2,1,0:T(8,128)(2,1)} %copy.49), calls=%async_computation.1 | async-start | bytes 3145728 | tf_op jit(solution)/shard_map/all_to_all | solution.py:88
  169.8 7.2 %slice_convert_fusion.3 = (f32[8,3,32,1024]{3,2,1,0:T(8,128)S(1)}, f32[8,3,32,1024]{3,2,1,0:T(8,128)}, f32[8,3,32,1024]{3,2,1,0:T(8,128)}, f32[8,3,32,1024]{3,2,1,0:T(8,128)}) fusion(bf16[8,3,32,4096]{3,2,1,0:T(8,128)(2,1)} %bitcast.69), kind=kLoop, calls=%fused_computation.46 | loop fusion | flops 3145728 | bytes 18874368 | tf_op jit(solution)/shard_map/convert_element_type | solution.py:102
  177.0 17.0 %all-to-all-done.1 = bf16[128,8,768]{2,1,0:T(8,128)(2,1)} async-done(((bf16[128,8,768]{2,1,0:T(8,128)(2,1)}), bf16[128,8,768]{2,1,0:T(8,128)(2,1)}, u32[]{:S(2)}, u32[]{:S(2)}) %all-to-all-start.1) | async-done | bytes 1572896 | tf_op jit(solution)/shard_map/all_to_all | solution.py:88
  194.0 4.1 %convolution_multiply_fusion = f32[768,1024]{1,0:T(8,128)S(1)} fusion(bf16[1024,1024]{1,0:T(8,128)(2,1)} %copy-done.3, bf16[128,8,768]{2,1,0:T(8,128)(2,1)} %all-to-all-done.1), kind=kOutput, calls=%fused_computation.41 | convolution fusion | flops 1611399168 | bytes 6815744 | tf_op jit(solution)/shard_map/dot_general | solution.py:91
  198.1 3.1 %fusion.41 = (bf16[8,1,32,1024]{3,2,1,0:T(8,128)(2,1)S(1)}, bf16[8,1,32,1024]{3,2,1,0:T(8,128)(2,1)S(1)}, bf16[8,1,32,1024]{3,2,1,0:T(8,128)(2,1)}, bf16[8,1,32,1024]{3,2,1,0:T(8,128)(2,1)}, f32[8,32,1024]{2,1,0:T(8,128)S(1)}) fusion(f32[8,3,32,1024]{3,2,1,0:T(8,128)S(1)} %get-tuple-element.7, f32[8,3,32,1024]{3,2,1,0:T(8,128)S(1)} %bitcast.70, ...), kind=kLoop, calls=%fused_computation.58 | loop fusion | flops 4194304 | bytes 8388608 | tf_op jit(solution)/shard_map/convert.17
  202.9 4.6 %maximum_maximum_fusion = bf16[8,3,2,16,4096]{4,3,2,1,0:T(8,128)(2,1)} fusion(bf16[8,2,2,16,1024]{4,3,2,1,0:T(8,128)(2,1)S(1)} %bitcast.77, bf16[8,1,2,16,1024]{4,3,2,1,0:T(8,128)(2,1)} %bitcast.81, bf16[8,2,2,16,1024]{4,3,2,1,0:T(8,128)(2,1)S(1)} %bitcast.76, bf16[8,1,2,16,1024]{4,3,2,1,0:T(8,128)(2,1)} %bitcast.80, ...), kind=kLoop, calls=%fused_computation.6 | loop fusion | flops 50331648 | bytes 12582912 | tf_op jit(solution)/shard_map/concatenate | solution.py:106
  (34 shorter events, 5.5 us)
Async XLA Ops:
  27.7 5.1 %copy-start.3 = (bf16[1024,1024]{1,0:T(8,128)(2,1)}, bf16[1024,1024]{1,0:T(8,128)(2,1)S(1)}, u32[]{:S(2)}) copy-start(bf16[1024,1024]{1,0:T(8,128)(2,1)S(1)} %fusion.10) | copy-start | bytes 6291460
  32.8 15.9 %copy-start.5 = (bf16[32,32]{1,0:T(8,128)(2,1)S(1)}, bf16[32,32]{1,0:T(8,128)(2,1)}, u32[]{:S(2)}) copy-start(bf16[32,32]{1,0:T(8,128)(2,1)} %param.8) | copy-start | bytes 6148
  32.8 16.0 %copy-start.4 = (f32[8,2048]{1,0:T(8,128)S(1)}, f32[8,2048]{1,0:T(8,128)}, u32[]{:S(2)}) copy-start(f32[8,2048]{1,0:T(8,128)} %param.9) | copy-start | bytes 196612
  37.4 38.7 %all-to-all-start = ((bf16[128,8,768]{2,1,0:T(8,128)(2,1)}), bf16[128,8,768]{2,1,0:T(8,128)(2,1)S(1)}, u32[]{:S(2)}, u32[]{:S(2)}) async-start(bf16[128,8,768]{2,1,0:T(8,128)(2,1)} %fusion.33), calls=%async_computation | async-start | bytes 3145728 | tf_op jit(solution)/shard_map/all_to_all | solution.py:53
  77.3 4.6 %copy-start.6 = (f32[2,2]{1,0:T(2,128)S(1)}, f32[2,2]{1,0:T(2,128)}, u32[]{:S(2)}) copy-start(f32[2,2]{1,0:T(2,128)} %constant.52.clone) | copy-start | bytes 52
  159.9 34.1 %all-to-all-start.1 = ((bf16[128,8,768]{2,1,0:T(8,128)(2,1)}), bf16[128,8,768]{2,1,0:T(8,128)(2,1)}, u32[]{:S(2)}, u32[]{:S(2)}) async-start(bf16[128,8,768]{2,1,0:T(8,128)(2,1)} %copy.49), calls=%async_computation.1 | async-start | bytes 3145728 | tf_op jit(solution)/shard_map/all_to_all | solution.py:88
  194.0 4.1 %copy-start = (f32[8,3,32,1024]{3,2,1,0:T(8,128)S(1)}, f32[8,3,32,1024]{3,2,1,0:T(8,128)}, u32[]{:S(2)}) copy-start(f32[8,3,32,1024]{3,2,1,0:T(8,128)} %get-tuple-element.8) | copy-start | bytes 9437188
  194.0 4.1 %copy-start.1 = (f32[8,3,32,1024]{3,2,1,0:T(8,128)S(1)}, f32[8,3,32,1024]{3,2,1,0:T(8,128)}, u32[]{:S(2)}) copy-start(f32[8,3,32,1024]{3,2,1,0:T(8,128)} %get-tuple-element.9) | copy-start | bytes 9437188
  198.1 3.1 %copy-start.2 = (f32[8,3,32,1024]{3,2,1,0:T(8,128)S(1)}, f32[8,3,32,1024]{3,2,1,0:T(8,128)}, u32[]{:S(2)}) copy-start(f32[8,3,32,1024]{3,2,1,0:T(8,128)} %get-tuple-element.10) | copy-start | bytes 9437188
where the time goes:
time: 209 us; the launch traced here: 207 us
  local copies, waits for them, and re-layouts  61.9 us (30%)
  other arithmetic  54.1 us (26%)
  matrix products  26.9 us (13%)
  blocking collectives  26.3 us (13%)
  starting transfers between devices  21 us (10%)
  waiting for transfers between devices  17 us (8%)
    all_gather x1, blocking collectives, local(): all_gain = lax.all_gather(spectral_gain, 'chan', axis=0, tiled=True)  26.3 us
    convert_element_type x1, other arithmetic, local(): fwd = (basis * math.sqrt(2.0 / points)).astype(jnp.bfloat16)  17.8 us
    all_to_all x1, waiting for transfers between devices, local(): returned = lax.all_to_all(leaving, ('chan', 'lat'), 0, 0, tiled=True)  17 us
    transpose x1, local copies, waits for them, and re-layouts, local(): jnp.transpose(back, (4, 6, 3, 0, 5, 2, 1, 7))  14.3 us
    another operation x2, local copies, waits for them, and re-layouts, local(): jnp.stack([synthesis[:, 0] + synthesis[:, 1], synthesis[:, 0] - synthesis...  12.6 us
    dot_general x1, matrix products, local(): jnp.einsum('sptqoi,psri->sptqor', filtered, leg, preferred_element_type=j...  11.3 us
    transpose x1, other arithmetic, local(): jnp.transpose(back, (4, 6, 3, 0, 5, 2, 1, 7))  11.2 us
    all_to_all x1, starting transfers between devices, local(): got = lax.all_to_all(sent, ('chan', 'lat'), 0, 0, tiled=True)  11.1 us
  transfers between devices with their start and end apart: 2, of which 1 were waited for; matrix products, arithmetic and copies ran while one was open for 4% of the time, Pallas kernels for 0%

commit v1 on v0

--- a/solution.py
+++ b/solution.py
@@ -25,9 +25,16 @@
     modes = (slot_mode * step_size).reshape(n_lat, n_chan, per_dev)
     modes = jnp.transpose(modes, (1, 0, 2)).reshape(devices, 1, per_dev)
     quarter = jnp.array([0, points // 4], jnp.int32).reshape(1, 2, 1)
-    places = lax.iota(jnp.int32, period)
-    turns = (modes[..., None] * places + quarter[..., None]) % points
-    basis = jnp.cos(turns.astype(jnp.float32) * (2.0 * math.pi / points)).reshape(-1, period)
+    lanes = min(128, period)
+    blocks = period // lanes
+    scale = 2.0 * math.pi / points
+    hi_turns = (modes[..., None] * (lax.iota(jnp.int32, blocks) * lanes) + quarter[..., None]) % points
+    lo_turns = (modes[..., None] * lax.iota(jnp.int32, lanes)) % points
+    hi_angle = hi_turns.astype(jnp.float32) * scale
+    lo_angle = lo_turns.astype(jnp.float32) * scale
+    ca, sa = jnp.cos(hi_angle)[..., None], jnp.sin(hi_angle)[..., None]
+    cb, sb = jnp.cos(lo_angle)[..., None, :], jnp.sin(lo_angle)[..., None, :]
+    basis = (ca * cb - sa * sb).reshape(-1, period)
     fwd = (basis * math.sqrt(2.0 / points)).astype(jnp.bfloat16)
     ratio = math.sqrt(points / (2.0 * total_modes))
     if ratio == 2.0 ** round(math.log2(ratio)):
@@ -72,16 +79,13 @@
     )
     degree = 2 * lax.iota(jnp.int32, half_deg)[None, :] + lax.iota(jnp.int32, 2)[:, None]
     allowed = degree[None, :, :] >= own_modes[:, None, None]
+    sign = jnp.array([[1.0, 1.0], [1.0, -1.0]], jnp.float32).reshape(1, 2, 2, 1, 1, 1, 1)
+    scaled = gain_par[None, :, None, None, :, :] * coefficients
     filtered = jnp.where(
-        allowed[:, :, None, None, None, :],
-        gain_par[None, :, None, None, :, :] * coefficients,
-        0.0,
+        allowed[:, None, :, None, None, None, :], sign * scaled[:, None], 0.0
     ).astype(jnp.bfloat16)
-    synthesis = jnp.einsum(
-        "sptqoi,psri->sptqor", filtered, leg, preferred_element_type=jnp.float32
-    )
-    back = jnp.stack(
-        [synthesis[:, 0] + synthesis[:, 1], synthesis[:, 0] - synthesis[:, 1]], axis=1
+    back = jnp.einsum(
+        "shptqoi,psri->shtqor", filtered, leg, preferred_element_type=jnp.float32
     ).astype(jnp.bfloat16)
     back = back.reshape(per_dev, 2, fields, 2, n_chan, chans, n_lat, cycles)
     leaving = jnp.transpose(back, (4, 6, 3, 0, 5, 2, 1, 7)).reshape(devices, 2 * per_dev, row_count)

time: 209 us -> 179 us (0.86)
  other arithmetic: 54.1 us -> 24.1 us
  matrix products: 26.9 us -> 35.5 us
  local copies, waits for them, and re-layouts: 61.9 us -> 54.3 us
    convert_element_type x1, other arithmetic: 17.8 us -> 2.48 us  [local(): fwd = (basis * math.sqrt(2.0 / points)).astype(jnp.bfloat16)]
    another operation x2 -> x0, local copies, waits for them, and re-layouts: 12.6 us -> none  [local(): jnp.stack([synthesis[:, 0] + synthesis[:, 1], synthesis[:, 0] - synthesis...]
    reshape x0 -> x1, local copies, waits for them, and re-layouts: none -> 11.9 us  [local(): back = back.reshape(per_dev, 2, fields, 2, n_chan, chans, n_lat, cycles)]
    transpose x1 -> x0, other arithmetic: 11.2 us -> none  [local(): jnp.transpose(back, (4, 6, 3, 0, 5, 2, 1, 7))]
    add x4 -> x0, local copies, waits for them, and re-layouts: 8.67 us -> none  [local(): turns = (modes[..., None] * places + quarter[..., None]) % points]
    dot_general x1 -> x2, matrix products: 11.3 us -> 17.2 us  [the longest x1 8.65 us: local(): jnp.einsum('shptqoi,psri->shtqor', filtered, leg, preferred_element_type=...]
    convert_element_type x1, other arithmetic: 5.1 us -> 1.57 us  [local(): low = (summed - high.astype(jnp.float32)).astype(jnp.bfloat16)]
    dot_general x1, matrix products: 6.87 us -> 9.56 us  [local(): jnp.einsum('pokhC,CLqskthr->sptqoLr', mix_fold, got, preferred_element_ty...]
  transfers between devices with their start and end apart: 2 -> 2, of which waited for: 1 -> 1; matrix products, arithmetic and copies ran while one was open for 4% -> 5% of each run, Pallas kernels for 0% -> 0%
where the time goes in v1:
time: 179 us; the launch traced here: 178 us
  local copies, waits for them, and re-layouts  54.3 us (30%)
  matrix products  35.5 us (20%)
  blocking collectives  26.3 us (15%)
  other arithmetic  24.1 us (13%)
  starting transfers between devices  20.8 us (12%)
  waiting for transfers between devices  17 us (9%)
    all_gather x1, blocking collectives, local(): all_gain = lax.all_gather(spectral_gain, 'chan', axis=0, tiled=True)  26.3 us
    all_to_all x1, waiting for transfers between devices, local(): returned = lax.all_to_all(leaving, ('chan', 'lat'), 0, 0, tiled=True)  17 us
    transpose x1, local copies, waits for them, and re-layouts, local(): jnp.transpose(back, (4, 6, 3, 0, 5, 2, 1, 7))  14.5 us
    reshape x1, local copies, waits for them, and re-layouts, local(): back = back.reshape(per_dev, 2, fields, 2, n_chan, chans, n_lat, cycles)  11.9 us
    all_to_all x1, starting transfers between devices, local(): got = lax.all_to_all(sent, ('chan', 'lat'), 0, 0, tiled=True)  11.1 us
    convert_element_type x1, local copies, waits for them, and re-layouts, local(): folded = jnp.einsum('pokhC,CLqskthr->sptqoLr', mix_fold, got, preferred_e...  10.1 us
    all_to_all x1, starting transfers between devices, local(): returned = lax.all_to_all(leaving, ('chan', 'lat'), 0, 0, tiled=True)  9.68 us
    dot_general x1, matrix products, local(): jnp.einsum('pokhC,CLqskthr->sptqoLr', mix_fold, got, preferred_element_ty...  9.56 us
  transfers between devices with their start and end apart: 2, of which 1 were waited for; matrix products, arithmetic and copies ran while one was open for 5% of the time, Pallas kernels for 0%

profile of v1, /device:TPU:0, one launch (start us, length us, event | category | flops | bytes accessed | tf_op | source)
XLA Modules:
  0.0 178.2 jit_solution(10418024160867076549)
XLA Ops:
  0.0 0.7 broadcast_multiply_fusion.2
  1.2 2.4 %fusion.54 = (f32[128,4,128]{2,1,0:T(4,128)S(1)}, f32[128,4,128]{2,1,0:T(4,128)S(1)}) fusion(s32[128,4]{1,0:T(8,128)S(1)} %copy.59), kind=kLoop, calls=%fused_computation.66 | loop fusion | flops 917504 | bytes 526336 | tf_op jit(solution)/shard_map/cos | solution.py:36
  4.4 2.5 %multiply_convert_fusion = bf16[128,2,4,8,128]{4,3,2,1,0:T(8,128)(2,1)S(1)} fusion(f32[128,4,128]{2,1,0:T(4,128)S(1)} %get-tuple-element.21, f32[128,2,4,8]{3,2,1,0:T(4,128)S(1)} %copy.60, f32[128,4,128]{2,1,0:T(4,128)S(1)} %get-tuple-element.20, f32[128,2,4,8]{3,2,1,0:T(4,128)S(1)} %copy.58), kind=kLoop, calls=%fused_computation.21 | loop fusion | flops 5242880 | bytes 2686976 | tf_op jit(solution)/shard_map/convert_element_type | solution.py:38
  7.5 1.6 subtract_convert_fusion
  9.3 4.6 %fusion.39 = bf16[128,8,768]{2,1,0:T(8,128)(2,1)} fusion(bf16[768,1024]{1,0:T(8,128)(2,1)S(1)} %get-tuple-element.5, bf16[768,1024]{1,0:T(8,128)(2,1)S(1)} %get-tuple-element.6, bf16[1024,1024]{1,0:T(8,128)(2,1)S(1)} %bitcast.84), kind=kOutput, calls=%fused_computation.46 | convolution fusion | flops 3236691968 | bytes 6815744 | tf_op jit(solution)/shard_map/dot_general | solution.py:54
  13.9 11.1 %all-to-all-start = ((bf16[128,8,768]{2,1,0:T(8,128)(2,1)}), bf16[128,8,768]{2,1,0:T(8,128)(2,1)S(1)}, u32[]{:S(2)}, u32[]{:S(2)}) async-start(bf16[128,8,768]{2,1,0:T(8,128)(2,1)} %fusion.39), calls=%async_computation | async-start | bytes 3145728 | tf_op jit(solution)/shard_map/all_to_all | solution.py:60
  25.3 26.3 %all_gather.3 = f32[32,2048]{1,0:T(8,128)S(1)} all-gather(f32[8,2048]{1,0:T(8,128)S(1)} %copy-done.5), channel_id=1, replica_groups=mesh['lat'=32,'chan'=4] {'chan'}, dimensions={0}, use_global_device_ids=true | all-gather | bytes 327680 | tf_op jit(solution)/shard_map/all_gather | solution.py:75
  52.6 1.2 copy.61
  53.8 4.6 %reshape.168 = bf16[4,32,2,4,8,3,2,16]{1,0,7,6,5,4,3,2:T(4,128)(2,1)} reshape(bf16[128,8,768]{0,2,1:T(8,128)(2,1)S(1)} %copy.61) | data formatting | bytes 3145728 | tf_op jit(solution)/shard_map/reshape | solution.py:61
  58.4 9.6 %fusion.6 = bf16[4,2,3,2,32,32,16]{4,5,1,6,2,0,3:T(8,128)(2,1)} fusion(f32[32,8,4]{0,2,1:T(4,128)S(1)} %copy.63, f32[2,2]{1,0:T(2,128)S(1)} %copy-done.7, bf16[4,32,2,4,8,3,2,16]{1,0,7,6,5,4,3,2:T(4,128)(2,1)} %reshape.168), kind=kOutput, calls=%fused_computation.8 | convolution fusion | flops 101457920 | bytes 3149840 | tf_op jit(solution)/shard_map/pokhC,CLqskthr->sptqoLr/dot_general | solution.py:66
  68.0 10.1 %copy.65 = bf16[4,2,3,2,32,32,16]{4,6,5,3,2,1,0:T(8,128)(2,1)S(1)} copy(bf16[4,2,3,2,32,32,16]{4,5,1,6,2,0,3:T(8,128)(2,1)} %fusion.6) | data formatting | bytes 3145728 | tf_op jit(solution)/shard_map/convert_element_type | solution.py:68
  78.0 8.6 %broadcast_multiply_fusion = f32[4,2,3,2,32,1024]{5,4,1,3,2,0:T(8,128)} fusion(f32[2,32,1024]{2,1,0:T(8,128)S(1)} %copy.56, bf16[4,2,3,2,32,512]{4,5,3,2,1,0:T(8,128)(2,1)S(1)} %bitcast.80, bf16[2,16,512,1024]{3,2,1,0:T(8,128)(2,1)} %param.11, s32[]{:T(128)S(6)} %select_n.43), kind=kOutput, calls=%fused_computation.28 | convolution fusion | flops 1612185600 | bytes 16515076 | tf_op jit(solution)/shard_map/sptqor,psri->sptqoi/dot_general | solution.py:72
  86.6 8.7 %bitcast_convert_fusion.1 = bf16[4,2,3,2,32,512]{5,4,3,2,1,0:T(8,128)(2,1)S(1)} fusion(f32[4,2,3,2,32,1024]{5,4,1,3,2,0:T(8,128)} %broadcast_multiply_fusion, f32[2,2]{1,0:T(2,128)S(1)} %copy-done.7, pred[4,2,1024]{2,1,0:T(4,128)(4,1)S(1)} %broadcast_compare_fusion, bf16[2,16,512,1024]{3,2,1,0:T(8,128)(2,1)} %param.11, s32[]{:T(128)S(6)} %select_n.43), kind=kOutput, calls=%fused_computation.25 | convolution fusion | flops 3231449088 | bytes 16261140 | tf_op jit(solution)/shard_map/shptqoi,psri->shtqor/dot_general | solution.py:87
  95.3 11.9 %reshape.171 = bf16[4,2,3,2,4,8,32,16]{7,6,5,4,3,2,1,0:T(8,128)(2,1)} reshape(bf16[4,2,3,2,32,512]{5,4,3,2,1,0:T(8,128)(2,1)S(1)} %bitcast_convert_fusion.1) | data formatting | bytes 3145728 | tf_op jit(solution)/shard_map/reshape | solution.py:90
  107.1 14.5 %copy.68 = bf16[4,32,2,4,8,3,2,16]{1,0,7,6,5,4,3,2:T(4,128)(2,1)} copy(bf16[4,32,2,4,8,3,2,16]{7,1,4,0,2,5,6,3:T(8,128)(2,1)} %bitcast.77) | data formatting | bytes 3145728 | tf_op jit(solution)/shard_map/transpose | solution.py:91
  121.6 7.3 %reshape.172 = bf16[128,8,768]{0,2,1:T(8,128)(2,1)S(1)} reshape(bf16[4,32,2,4,8,3,2,16]{1,0,7,6,5,4,3,2:T(4,128)(2,1)} %copy.68) | data formatting | bytes 3145728 | tf_op jit(solution)/shard_map/reshape | solution.py:91
  128.9 2.0 %copy.69 = bf16[128,8,768]{2,1,0:T(8,128)(2,1)} copy(bf16[128,8,768]{0,2,1:T(8,128)(2,1)S(1)} %reshape.172) | data formatting | bytes 3145728 | tf_op jit(solution)/shard_map/reshape | solution.py:91
  130.9 9.7 %all-to-all-start.1 = ((bf16[128,8,768]{2,1,0:T(8,128)(2,1)}), bf16[128,8,768]{2,1,0:T(8,128)(2,1)}, u32[]{:S(2)}, u32[]{:S(2)}) async-start(bf16[128,8,768]{2,1,0:T(8,128)(2,1)} %copy.69), calls=%async_computation.1 | async-start | bytes 3145728 | tf_op jit(solution)/shard_map/all_to_all | solution.py:92
  140.6 7.2 %slice_convert_fusion.3 = (f32[8,3,32,1024]{3,2,1,0:T(8,128)S(1)}, f32[8,3,32,1024]{3,2,1,0:T(8,128)}, f32[8,3,32,1024]{3,2,1,0:T(8,128)}, f32[8,3,32,1024]{3,2,1,0:T(8,128)}) fusion(bf16[8,3,32,4096]{3,2,1,0:T(8,128)(2,1)} %bitcast.78), kind=kLoop, calls=%fused_computation.44 | loop fusion | flops 3145728 | bytes 18874368 | tf_op jit(solution)/shard_map/convert_element_type | solution.py:106
  147.8 17.0 %all-to-all-done.1 = bf16[128,8,768]{2,1,0:T(8,128)(2,1)} async-done(((bf16[128,8,768]{2,1,0:T(8,128)(2,1)}), bf16[128,8,768]{2,1,0:T(8,128)(2,1)}, u32[]{:S(2)}, u32[]{:S(2)}) %all-to-all-start.1) | async-done | bytes 1572896 | tf_op jit(solution)/shard_map/all_to_all | solution.py:92
  164.8 4.1 %convolution_multiply_fusion = f32[768,1024]{1,0:T(8,128)S(1)} fusion(bf16[1024,1024]{1,0:T(8,128)(2,1)} %bitcast.85, bf16[128,8,768]{2,1,0:T(8,128)(2,1)} %all-to-all-done.1), kind=kOutput, calls=%fused_computation.39 | convolution fusion | flops 1611399168 | bytes 6815744 | tf_op jit(solution)/shard_map/dot_general | solution.py:95
  168.9 3.1 %fusion.47 = (bf16[8,1,32,1024]{3,2,1,0:T(8,128)(2,1)S(1)}, bf16[8,1,32,1024]{3,2,1,0:T(8,128)(2,1)S(1)}, bf16[8,1,32,1024]{3,2,1,0:T(8,128)(2,1)}, bf16[8,1,32,1024]{3,2,1,0:T(8,128)(2,1)}, f32[8,32,1024]{2,1,0:T(8,128)S(1)}) fusion(f32[8,3,32,1024]{3,2,1,0:T(8,128)S(1)} %get-tuple-element.7, f32[8,3,32,1024]{3,2,1,0:T(8,128)S(1)} %bitcast.81, ...), kind=kLoop, calls=%fused_computation.54 | loop fusion | flops 4194304 | bytes 8388608 | tf_op jit(solution)/shard_map/convert.17
  172.0 1.7 fusion.30
  173.7 4.6 %maximum_maximum_fusion = bf16[8,3,2,16,4096]{4,3,2,1,0:T(8,128)(2,1)} fusion(bf16[8,2,2,16,1024]{4,3,2,1,0:T(8,128)(2,1)S(1)} %bitcast.90, bf16[8,1,2,16,1024]{4,3,2,1,0:T(8,128)(2,1)} %bitcast.94, bf16[8,2,2,16,1024]{4,3,2,1,0:T(8,128)(2,1)S(1)} %bitcast.89, bf16[8,1,2,16,1024]{4,3,2,1,0:T(8,128)(2,1)} %bitcast.93, ...), kind=kLoop, calls=%fused_computation.9 | loop fusion | flops 50331648 | bytes 12582912 | tf_op jit(solution)/shard_map/concatenate | solution.py:110
  (39 shorter events, 3.3 us)
Async XLA Ops:
  4.4 3.1 %copy-start = (bf16[8,3,2,16,4096]{4,3,2,1,0:T(8,128)(2,1)S(1)}, bf16[8,3,2,16,4096]{4,3,2,1,0:T(8,128)(2,1)}, u32[]{:S(2)}) copy-start(bf16[8,3,2,16,4096]{4,3,2,1,0:T(8,128)(2,1)} %param.8) | copy-start | bytes 18874372
  7.5 1.8 %copy-start.4 = (bf16[128,8,8,128]{3,1,2,0:T(8,128)(2,1)}, bf16[128,8,8,128]{3,1,2,0:T(8,128)(2,1)S(1)}, u32[]{:S(2)}) copy-start(bf16[128,8,8,128]{3,1,2,0:T(8,128)(2,1)S(1)} %copy.103) | copy-start | bytes 6291460
  9.3 15.8 %copy-start.6 = (bf16[32,32]{1,0:T(8,128)(2,1)S(1)}, bf16[32,32]{1,0:T(8,128)(2,1)}, u32[]{:S(2)}) copy-start(bf16[32,32]{1,0:T(8,128)(2,1)} %param.9) | copy-start | bytes 6148
  9.3 16.0 %copy-start.5 = (f32[8,2048]{1,0:T(8,128)S(1)}, f32[8,2048]{1,0:T(8,128)}, u32[]{:S(2)}) copy-start(f32[8,2048]{1,0:T(8,128)} %param.10) | copy-start | bytes 196612
  13.9 38.7 %all-to-all-start = ((bf16[128,8,768]{2,1,0:T(8,128)(2,1)}), bf16[128,8,768]{2,1,0:T(8,128)(2,1)S(1)}, u32[]{:S(2)}, u32[]{:S(2)}) async-start(bf16[128,8,768]{2,1,0:T(8,128)(2,1)} %fusion.39), calls=%async_computation | async-start | bytes 3145728 | tf_op jit(solution)/shard_map/all_to_all | solution.py:60
  53.8 4.6 %copy-start.7 = (f32[2,2]{1,0:T(2,128)S(1)}, f32[2,2]{1,0:T(2,128)}, u32[]{:S(2)}) copy-start(f32[2,2]{1,0:T(2,128)} %constant.63.clone) | copy-start | bytes 52
  130.9 33.9 %all-to-all-start.1 = ((bf16[128,8,768]{2,1,0:T(8,128)(2,1)}), bf16[128,8,768]{2,1,0:T(8,128)(2,1)}, u32[]{:S(2)}, u32[]{:S(2)}) async-start(bf16[128,8,768]{2,1,0:T(8,128)(2,1)} %copy.69), calls=%async_computation.1 | async-start | bytes 3145728 | tf_op jit(solution)/shard_map/all_to_all | solution.py:92
  164.8 4.1 %copy-start.1 = (f32[8,3,32,1024]{3,2,1,0:T(8,128)S(1)}, f32[8,3,32,1024]{3,2,1,0:T(8,128)}, u32[]{:S(2)}) copy-start(f32[8,3,32,1024]{3,2,1,0:T(8,128)} %get-tuple-element.8) | copy-start | bytes 9437188
  164.8 4.1 %copy-start.2 = (f32[8,3,32,1024]{3,2,1,0:T(8,128)S(1)}, f32[8,3,32,1024]{3,2,1,0:T(8,128)}, u32[]{:S(2)}) copy-start(f32[8,3,32,1024]{3,2,1,0:T(8,128)} %get-tuple-element.9) | copy-start | bytes 9437188
  168.8 3.2 %copy-start.3 = (f32[8,3,32,1024]{3,2,1,0:T(8,128)S(1)}, f32[8,3,32,1024]{3,2,1,0:T(8,128)}, u32[]{:S(2)}) copy-start(f32[8,3,32,1024]{3,2,1,0:T(8,128)} %get-tuple-element.10) | copy-start | bytes 9437188

commit v2 on v1

--- a/solution.py
+++ b/solution.py
@@ -1,9 +1,66 @@
+import functools
 import math
 
 import jax
 import jax.numpy as jnp
 from jax import lax
+from jax.experimental import pallas as pl
+from jax.experimental.pallas import tpu as pltpu
 from jax.sharding import PartitionSpec as P
+
+
+def legendre_kernel(modes_ref, base_ref, folded_ref, leg_ref, gain_ref, out_ref, *, block):
+    s = pl.program_id(0)
+    mode = modes_ref[s]
+    half_deg = leg_ref.shape[-1]
+    rows = folded_ref.shape[-2]
+    north = folded_ref.shape[-1]
+    syn = []
+    for p in range(2):
+        lhs = folded_ref[0, p]
+        acc = jnp.zeros((rows, north), jnp.float32)
+        for b in range(half_deg // block):
+            def step(acc, p=p, b=b):
+                table = leg_ref[p, 0, :, b * block : (b + 1) * block]
+                coef = jnp.dot(lhs, table, preferred_element_type=jnp.float32)
+                degree = 2 * (b * block + lax.broadcasted_iota(jnp.int32, (1, block), 1)) + p
+                kept = jnp.where(
+                    degree >= mode, gain_ref[p, :, b * block : (b + 1) * block] * coef, 0.0
+                ).astype(jnp.bfloat16)
+                return acc + lax.dot_general(
+                    kept, table, (((1,), (1,)), ((), ())), preferred_element_type=jnp.float32
+                )
+            top = 2 * ((b + 1) * block - 1) + p
+            acc = lax.cond(top >= mode, step, lambda a: a, acc)
+        syn.append(acc)
+    out_ref[0, 0] = (syn[0] + syn[1]).astype(out_ref.dtype)
+    out_ref[0, 1] = (syn[0] - syn[1]).astype(out_ref.dtype)
+
+
+def legendre_stage(folded, legendre, gain_rows, own_modes, base, block=256):
+    per_dev, _, rows, north = folded.shape
+    half_deg = legendre.shape[-1]
+    grid_spec = pltpu.PrefetchScalarGridSpec(
+        num_scalar_prefetch=2,
+        grid=(per_dev,),
+        in_specs=[
+            pl.BlockSpec((1, 2, rows, north), lambda s, m, b: (s, 0, 0, 0)),
+            pl.BlockSpec((2, 1, north, half_deg), lambda s, m, b: (0, b[0] + s, 0, 0)),
+            pl.BlockSpec((2, rows, half_deg), lambda s, m, b: (0, 0, 0)),
+        ],
+        out_specs=pl.BlockSpec((1, 2, rows, north), lambda s, m, b: (s, 0, 0, 0)),
+    )
+    flops = 8 * per_dev * rows * north * half_deg
+    return pl.pallas_call(
+        functools.partial(legendre_kernel, block=block),
+        grid_spec=grid_spec,
+        out_shape=jax.ShapeDtypeStruct((per_dev, 2, rows, north), jnp.bfloat16),
+        compiler_params=pltpu.CompilerParams(vmem_limit_bytes=48 * 1024 * 1024),
+        cost_estimate=pl.CostEstimate(
+            flops=flops, transcendentals=0,
+            bytes_accessed=2 * per_dev * north * half_deg * 2 + 4 * folded.size + 4 * gain_rows.size,
+        ),
+    )(own_modes, base, folded, legendre, gain_rows)
 
 
 def local(field, mix_weight, spectral_gain, legendre, slot_mode, n_lat, n_chan):
@@ -68,25 +125,17 @@
     ).astype(jnp.bfloat16)
     folded = folded.reshape(per_dev, 2, fields, 2, -1, n_lat * cycles)
 
-    leg = lax.dynamic_slice_in_dim(legendre, chan_index * per_dev, per_dev, 1)
-    coefficients = jnp.einsum(
-        "sptqor,psri->sptqoi", folded, leg, preferred_element_type=jnp.float32
-    )
     all_gain = lax.all_gather(spectral_gain, "chan", axis=0, tiled=True)
     gain_par = jnp.transpose(all_gain.reshape(-1, half_deg, 2), (2, 0, 1))
     own_modes = lax.dynamic_slice_in_dim(
         modes.reshape(-1), (chan_index * n_lat + lat_index) * per_dev, per_dev, 0
     )
-    degree = 2 * lax.iota(jnp.int32, half_deg)[None, :] + lax.iota(jnp.int32, 2)[:, None]
-    allowed = degree[None, :, :] >= own_modes[:, None, None]
-    sign = jnp.array([[1.0, 1.0], [1.0, -1.0]], jnp.float32).reshape(1, 2, 2, 1, 1, 1, 1)
-    scaled = gain_par[None, :, None, None, :, :] * coefficients
-    filtered = jnp.where(
-        allowed[:, None, :, None, None, None, :], sign * scaled[:, None], 0.0
-    ).astype(jnp.bfloat16)
-    back = jnp.einsum(
-        "shptqoi,psri->shtqor", filtered, leg, preferred_element_type=jnp.float32
-    ).astype(jnp.bfloat16)
+    rows_x = folded.shape[2] * folded.shape[3] * folded.shape[4]
+    gain_rows = jnp.tile(gain_par, (1, rows_x // gain_par.shape[1], 1))
+    base = (chan_index * per_dev).astype(jnp.int32).reshape(1)
+    back = legendre_stage(
+        folded.reshape(per_dev, 2, rows_x, -1), legendre, gain_rows, own_modes, base
+    )
     back = back.reshape(per_dev, 2, fields, 2, n_chan, chans, n_lat, cycles)
     leaving = jnp.transpose(back, (4, 6, 3, 0, 5, 2, 1, 7)).reshape(devices, 2 * per_dev, row_count)
     returned = lax.all_to_all(leaving, ("chan", "lat"), 0, 0, tiled=True)

time: 179 us -> 189 us (1.056)
  matrix products: 35.5 us -> 18.2 us
  local copies, waits for them, and re-layouts: 54.3 us -> 68.6 us
  Pallas kernels: 0 us -> 12.8 us
    dot_general x2 -> x0, matrix products: 17.2 us -> none  [the longest x1 8.65 us: local(): jnp.einsum('shptqoi,psri->shtqor', filtered, leg, preferred_element_type=...]
    pallas_call x0 -> x1, Pallas kernels: none -> 12.8 us  [legendre_stage(): pl.pallas_call(functools.partial(legendre_kernel, block=block), grid_spec...]
    another operation x0 -> x3, local copies, waits for them, and re-layouts: none -> 11.7 us  [the longest x2 11.5 us: local(): folded.reshape(per_dev, 2, rows_x, -1)]
    convert_element_type x1, local copies, waits for them, and re-layouts: 10.1 us -> 12.7 us  [local(): folded = jnp.einsum('pokhC,CLqskthr->sptqoLr', mix_fold, got, preferred_e...]
  transfers between devices with their start and end apart: 2 -> 2, of which waited for: 1 -> 1; matrix products, arithmetic and copies ran while one was open for 5% -> 4% of each run, Pallas kernels for 0% -> 0%
where the time goes in v2:
time: 189 us; the launch traced here: 188 us
  local copies, waits for them, and re-layouts  68.6 us (36%)
  blocking collectives  26.3 us (14%)
  other arithmetic  24 us (13%)
  starting transfers between devices  20.9 us (11%)
  matrix products  18.2 us (10%)
  waiting for transfers between devices  17 us (9%)
  Pallas kernels  12.8 us (7%)
    all_gather x1, blocking collectives, local(): all_gain = lax.all_gather(spectral_gain, 'chan', axis=0, tiled=True)  26.3 us
    all_to_all x1, waiting for transfers between devices, local(): returned = lax.all_to_all(leaving, ('chan', 'lat'), 0, 0, tiled=True)  17 us
    transpose x1, local copies, waits for them, and re-layouts, local(): jnp.transpose(back, (4, 6, 3, 0, 5, 2, 1, 7))  14.5 us
    pallas_call x1, Pallas kernels, legendre_stage(): pl.pallas_call(functools.partial(legendre_kernel, block=block), grid_spec...  12.8 us
    convert_element_type x1, local copies, waits for them, and re-layouts, local(): folded = jnp.einsum('pokhC,CLqskthr->sptqoLr', mix_fold, got, preferred_e...  12.7 us
    reshape x1, local copies, waits for them, and re-layouts, local(): back = back.reshape(per_dev, 2, fields, 2, n_chan, chans, n_lat, cycles)  11.9 us
    another operation x2, local copies, waits for them, and re-layouts, local(): folded.reshape(per_dev, 2, rows_x, -1)  11.5 us
    all_to_all x1, starting transfers between devices, local(): got = lax.all_to_all(sent, ('chan', 'lat'), 0, 0, tiled=True)  11.1 us
  transfers between devices with their start and end apart: 2, of which 1 were waited for; matrix products, arithmetic and copies ran while one was open for 4% of the time, Pallas kernels for 0%

profile of v2, /device:TPU:0, one launch (start us, length us, event | category | flops | bytes accessed | tf_op | source)
XLA Modules:
  0.0 188.2 jit_solution(5889828789074874861)
XLA Ops:
  1.2 2.4 %fusion.37 = (f32[128,4,128]{2,1,0:T(4,128)S(1)}, f32[128,4,128]{2,1,0:T(4,128)S(1)}) fusion(s32[128,4]{1,0:T(8,128)S(1)} %copy.54), kind=kLoop, calls=%fused_computation.52 | loop fusion | flops 917504 | bytes 526336 | tf_op jit(solution)/shard_map/cos | solution.py:93
  4.4 2.5 %multiply_convert_fusion = bf16[128,2,4,8,128]{4,3,2,1,0:T(8,128)(2,1)S(1)} fusion(f32[128,4,128]{2,1,0:T(4,128)S(1)} %get-tuple-element.21, f32[128,2,4,8]{3,2,1,0:T(4,128)S(1)} %copy.55, f32[128,4,128]{2,1,0:T(4,128)S(1)} %get-tuple-element.20, f32[128,2,4,8]{3,2,1,0:T(4,128)S(1)} %copy.53), kind=kLoop, calls=%fused_computation.9 | loop fusion | flops 5242880 | bytes 2686976 | tf_op jit(solution)/shard_map/convert_element_type | solution.py:95
  7.5 1.6 subtract_convert_fusion
  9.3 4.6 %fusion.22 = bf16[128,8,768]{2,1,0:T(8,128)(2,1)} fusion(bf16[768,1024]{1,0:T(8,128)(2,1)S(1)} %get-tuple-element.5, bf16[768,1024]{1,0:T(8,128)(2,1)S(1)} %get-tuple-element.6, bf16[1024,1024]{1,0:T(8,128)(2,1)S(1)} %bitcast.70), kind=kOutput, calls=%fused_computation.32 | convolution fusion | flops 3236691968 | bytes 6815744 | tf_op jit(solution)/shard_map/dot_general | solution.py:111
  13.9 11.1 %all-to-all-start = ((bf16[128,8,768]{2,1,0:T(8,128)(2,1)}), bf16[128,8,768]{2,1,0:T(8,128)(2,1)S(1)}, u32[]{:S(2)}, u32[]{:S(2)}) async-start(bf16[128,8,768]{2,1,0:T(8,128)(2,1)} %fusion.22), calls=%async_computation | async-start | bytes 3145728 | tf_op jit(solution)/shard_map/all_to_all | solution.py:117
  25.3 26.3 %all_gather.3 = f32[32,2048]{1,0:T(8,128)S(1)} all-gather(f32[8,2048]{1,0:T(8,128)S(1)} %copy-done.5), channel_id=1, replica_groups=mesh['lat'=32,'chan'=4] {'chan'}, dimensions={0}, use_global_device_ids=true | all-gather | bytes 327680 | tf_op jit(solution)/shard_map/all_gather | solution.py:128
  52.5 1.2 copy.56
  53.7 4.6 %reshape.141 = bf16[4,32,2,4,8,3,2,16]{1,0,7,6,5,4,3,2:T(4,128)(2,1)} reshape(bf16[128,8,768]{0,2,1:T(8,128)(2,1)S(1)} %copy.56) | data formatting | bytes 3145728 | tf_op jit(solution)/shard_map/reshape | solution.py:118
  58.3 9.6 %fusion = bf16[4,2,3,2,32,32,16]{4,5,1,6,2,0,3:T(8,128)(2,1)} fusion(f32[32,8,4]{0,2,1:T(4,128)S(1)} %copy.58, f32[2,2]{1,0:T(2,128)S(1)} %copy-done.7, bf16[4,32,2,4,8,3,2,16]{1,0,7,6,5,4,3,2:T(4,128)(2,1)} %reshape.141), kind=kOutput, calls=%fused_computation.1 | convolution fusion | flops 101457920 | bytes 3149840 | tf_op jit(solution)/shard_map/pokhC,CLqskthr->sptqoLr/dot_general | solution.py:123
  67.8 12.7 %copy.60 = bf16[4,2,3,2,32,32,16]{4,3,2,6,5,1,0:T(2,128)(2,1)} copy(bf16[4,2,3,2,32,32,16]{4,5,1,6,2,0,3:T(8,128)(2,1)} %fusion) | data formatting | bytes 3145728 | tf_op jit(solution)/shard_map/convert_element_type | solution.py:125
  80.5 8.8 %reshape_reshape.7 = bf16[4,2,192,512]{2,3,1,0:T(8,128)(2,1)} reshape(bf16[4,2,3,2,32,32,16]{4,3,2,6,5,1,0:T(2,128)(2,1)} %copy.60) | data formatting | bytes 3145728 | tf_op jit(solution)/shard_map/reshape;reshape | solution.py:137
  89.3 2.7 %copy.63.folded_ref = bf16[4,2,192,512]{3,2,1,0:T(8,128)(2,1)S(1)} copy(bf16[4,2,192,512]{2,3,1,0:T(8,128)(2,1)} %reshape_reshape.7) | data formatting | bytes 3145728 | tf_op jit(solution)/shard_map/reshape;reshape | solution.py:137
  92.2 12.8 %shard_map.73 = bf16[4,2,192,512]{3,2,1,0:T(8,128)(2,1)S(1)} custom-call(s32[4]{0:T(128)S(1)} %dynamic_slice.3.modes_ref, s32[1]{0:T(128)} %bitcast.2.base_ref, bf16[4,2,192,512]{3,2,1,0:T(8,128)(2,1)S(1)} %copy.63.folded_ref, bf16[2,16,512,1024]{3,2,1,0:T(8,128)(2,1)} %leg_ref.1, f32[2,192,1024]{2,1,0:T(8,128)S(1)} %bitcast.63), custom_call_target="tpu_custom_call" | custom-call | flops 3221225472 | bytes 13107200 | tf_op jit(solution)/shard_map/pallas_call | solution.py:54
  105.1 11.9 %reshape.144 = bf16[4,2,3,2,4,8,32,16]{7,6,5,4,3,2,1,0:T(8,128)(2,1)} reshape(bf16[4,2,192,512]{3,2,1,0:T(8,128)(2,1)S(1)} %shard_map.73) | data formatting | bytes 3145728 | tf_op jit(solution)/shard_map/reshape | solution.py:139
  117.0 14.5 %copy.64 = bf16[4,32,2,4,8,3,2,16]{1,0,7,6,5,4,3,2:T(4,128)(2,1)} copy(bf16[4,32,2,4,8,3,2,16]{7,1,4,0,2,5,6,3:T(8,128)(2,1)} %bitcast.64) | data formatting | bytes 3145728 | tf_op jit(solution)/shard_map/transpose | solution.py:140
  131.4 7.3 %reshape.145 = bf16[128,8,768]{0,2,1:T(8,128)(2,1)S(1)} reshape(bf16[4,32,2,4,8,3,2,16]{1,0,7,6,5,4,3,2:T(4,128)(2,1)} %copy.64) | data formatting | bytes 3145728 | tf_op jit(solution)/shard_map/reshape | solution.py:140
  138.8 2.0 %copy.65 = bf16[128,8,768]{2,1,0:T(8,128)(2,1)} copy(bf16[128,8,768]{0,2,1:T(8,128)(2,1)S(1)} %reshape.145) | data formatting | bytes 3145728 | tf_op jit(solution)/shard_map/reshape | solution.py:140
  140.7 9.8 %all-to-all-start.1 = ((bf16[128,8,768]{2,1,0:T(8,128)(2,1)}), bf16[128,8,768]{2,1,0:T(8,128)(2,1)}, u32[]{:S(2)}, u32[]{:S(2)}) async-start(bf16[128,8,768]{2,1,0:T(8,128)(2,1)} %copy.65), calls=%async_computation.1 | async-start | bytes 3145728 | tf_op jit(solution)/shard_map/all_to_all | solution.py:141
  150.5 7.2 %slice_convert_fusion.3 = (f32[8,3,32,1024]{3,2,1,0:T(8,128)S(1)}, f32[8,3,32,1024]{3,2,1,0:T(8,128)}, f32[8,3,32,1024]{3,2,1,0:T(8,128)}, f32[8,3,32,1024]{3,2,1,0:T(8,128)}) fusion(bf16[8,3,32,4096]{3,2,1,0:T(8,128)(2,1)} %bitcast.65), kind=kLoop, calls=%fused_computation.30 | loop fusion | flops 3145728 | bytes 18874368 | tf_op jit(solution)/shard_map/convert_element_type | solution.py:155
  157.7 17.0 %all-to-all-done.1 = bf16[128,8,768]{2,1,0:T(8,128)(2,1)} async-done(((bf16[128,8,768]{2,1,0:T(8,128)(2,1)}), bf16[128,8,768]{2,1,0:T(8,128)(2,1)}, u32[]{:S(2)}, u32[]{:S(2)}) %all-to-all-start.1) | async-done | bytes 1572896 | tf_op jit(solution)/shard_map/all_to_all | solution.py:141
  174.7 4.1 %convolution_multiply_fusion = f32[768,1024]{1,0:T(8,128)S(1)} fusion(bf16[1024,1024]{1,0:T(8,128)(2,1)} %bitcast.71, bf16[128,8,768]{2,1,0:T(8,128)(2,1)} %all-to-all-done.1), kind=kOutput, calls=%fused_computation.25 | convolution fusion | flops 1611399168 | bytes 6815744 | tf_op jit(solution)/shard_map/dot_general | solution.py:144
  178.8 3.1 %fusion.30 = (bf16[8,1,32,1024]{3,2,1,0:T(8,128)(2,1)S(1)}, bf16[8,1,32,1024]{3,2,1,0:T(8,128)(2,1)S(1)}, bf16[8,1,32,1024]{3,2,1,0:T(8,128)(2,1)}, bf16[8,1,32,1024]{3,2,1,0:T(8,128)(2,1)}, f32[8,32,1024]{2,1,0:T(8,128)S(1)}) fusion(f32[8,3,32,1024]{3,2,1,0:T(8,128)S(1)} %get-tuple-element.7, f32[8,3,32,1024]{3,2,1,0:T(8,128)S(1)} %bitcast.67, ...), kind=kLoop, calls=%fused_computation.40 | loop fusion | flops 4194304 | bytes 8388608 | tf_op jit(solution)/shard_map/convert.17
  181.9 1.7 fusion.15
  183.6 4.6 %maximum_maximum_fusion = bf16[8,3,2,16,4096]{4,3,2,1,0:T(8,128)(2,1)} fusion(bf16[8,2,2,16,1024]{4,3,2,1,0:T(8,128)(2,1)S(1)} %bitcast.76, bf16[8,1,2,16,1024]{4,3,2,1,0:T(8,128)(2,1)} %bitcast.80, bf16[8,2,2,16,1024]{4,3,2,1,0:T(8,128)(2,1)S(1)} %bitcast.75, bf16[8,1,2,16,1024]{4,3,2,1,0:T(8,128)(2,1)} %bitcast.79, ...), kind=kLoop, calls=%fused_computation.2 | loop fusion | flops 50331648 | bytes 12582912 | tf_op jit(solution)/shard_map/concatenate | solution.py:159
  (38 shorter events, 4.0 us)
Async XLA Ops:
  4.4 3.1 %copy-start = (bf16[8,3,2,16,4096]{4,3,2,1,0:T(8,128)(2,1)S(1)}, bf16[8,3,2,16,4096]{4,3,2,1,0:T(8,128)(2,1)}, u32[]{:S(2)}) copy-start(bf16[8,3,2,16,4096]{4,3,2,1,0:T(8,128)(2,1)} %param.7) | copy-start | bytes 18874372
  7.5 1.8 copy-start.4
  13.9 11.2 %copy-start.6 = (bf16[32,32]{1,0:T(8,128)(2,1)S(1)}, bf16[32,32]{1,0:T(8,128)(2,1)}, u32[]{:S(2)}) copy-start(bf16[32,32]{1,0:T(8,128)(2,1)} %param.8) | copy-start | bytes 6148
  13.9 11.4 %copy-start.5 = (f32[8,2048]{1,0:T(8,128)S(1)}, f32[8,2048]{1,0:T(8,128)}, u32[]{:S(2)}) copy-start(f32[8,2048]{1,0:T(8,128)} %param.9) | copy-start | bytes 196612
  13.9 38.6 %all-to-all-start = ((bf16[128,8,768]{2,1,0:T(8,128)(2,1)}), bf16[128,8,768]{2,1,0:T(8,128)(2,1)S(1)}, u32[]{:S(2)}, u32[]{:S(2)}) async-start(bf16[128,8,768]{2,1,0:T(8,128)(2,1)} %fusion.22), calls=%async_computation | async-start | bytes 3145728 | tf_op jit(solution)/shard_map/all_to_all | solution.py:117
  53.7 4.6 %copy-start.7 = (f32[2,2]{1,0:T(2,128)S(1)}, f32[2,2]{1,0:T(2,128)}, u32[]{:S(2)}) copy-start(f32[2,2]{1,0:T(2,128)} %constant.57.clone) | copy-start | bytes 52
  140.7 34.0 %all-to-all-start.1 = ((bf16[128,8,768]{2,1,0:T(8,128)(2,1)}), bf16[128,8,768]{2,1,0:T(8,128)(2,1)}, u32[]{:S(2)}, u32[]{:S(2)}) async-start(bf16[128,8,768]{2,1,0:T(8,128)(2,1)} %copy.65), calls=%async_computation.1 | async-start | bytes 3145728 | tf_op jit(solution)/shard_map/all_to_all | solution.py:141
  174.7 4.1 %copy-start.1 = (f32[8,3,32,1024]{3,2,1,0:T(8,128)S(1)}, f32[8,3,32,1024]{3,2,1,0:T(8,128)}, u32[]{:S(2)}) copy-start(f32[8,3,32,1024]{3,2,1,0:T(8,128)} %get-tuple-element.8) | copy-start | bytes 9437188
  174.7 4.1 %copy-start.2 = (f32[8,3,32,1024]{3,2,1,0:T(8,128)S(1)}, f32[8,3,32,1024]{3,2,1,0:T(8,128)}, u32[]{:S(2)}) copy-start(f32[8,3,32,1024]{3,2,1,0:T(8,128)} %get-tuple-element.9) | copy-start | bytes 9437188
  178.8 3.2 %copy-start.3 = (f32[8,3,32,1024]{3,2,1,0:T(8,128)S(1)}, f32[8,3,32,1024]{3,2,1,0:T(8,128)}, u32[]{:S(2)}) copy-start(f32[8,3,32,1024]{3,2,1,0:T(8,128)} %get-tuple-element.10) | copy-start | bytes 9437188

commit v3 on v2

--- a/solution.py
+++ b/solution.py
@@ -7,6 +7,76 @@
 from jax.experimental import pallas as pl
 from jax.experimental.pallas import tpu as pltpu
 from jax.sharding import PartitionSpec as P
+
+
+def block_swap(x, piece):
+    rows, width = x.shape
+    group = 128 // piece
+    row = lax.broadcasted_iota(jnp.int32, x.shape, 0) % group
+    blk = (lax.broadcasted_iota(jnp.int32, x.shape, 1) % 128) // piece
+    out = jnp.zeros_like(x)
+    for d in range(1 - group, group):
+        moved = x if d == 0 else pltpu.roll(x, (-piece * d) % width, 1)
+        keep = (blk == row) & (row + d >= 0) & (row + d < group)
+        moved = jnp.where(keep, moved, 0.0)
+        out = out + (moved if d == 0 else pltpu.roll(moved, d % rows, 0))
+    return out
+
+
+def gather_kernel(got_ref, mix_ref, out_ref, stage_ref, *, piece, per_dev, pairs):
+    n_chan = got_ref.shape[0]
+    lat_rows = got_ref.shape[2]
+    group = 128 // piece
+
+    def one(qs, carry):
+        for c in range(n_chan):
+            swapped = block_swap(got_ref[c, qs].astype(jnp.float32), piece)
+            for th in range(pairs):
+                for tile in range(lat_rows // group):
+                    stage_ref[qs, th // 2, c, th % 2, :, tile * 128 : (tile + 1) * 128] = swapped[
+                        tile * group : (tile + 1) * group, th * 128 : (th + 1) * 128
+                    ]
+        q = qs // per_dev
+        s = qs % per_dev
+        for t in range(pairs // 2):
+            block = stage_ref[qs, t]
+            block = block.reshape(-1, block.shape[-1]).astype(jnp.bfloat16)
+            mixed = jnp.dot(mix_ref[...], block, preferred_element_type=jnp.float32)
+            half = mixed.shape[0] // 2
+            for p in range(2):
+                out_ref[s, p, t, q] = mixed[p * half : (p + 1) * half].astype(out_ref.dtype)
+        return carry
+
+    lax.fori_loop(0, got_ref.shape[1], one, 0)
+
+
+def scatter_kernel(back_ref, out_ref, *, piece, per_dev, fields):
+    n_chan = out_ref.shape[0]
+    lat_rows = out_ref.shape[2]
+    group = 128 // piece
+    chans = back_ref.shape[2] // (fields * 2)
+
+    def one(qs, carry):
+        q = qs // per_dev
+        s = qs % per_dev
+        for t in range(fields):
+            for h in range(2):
+                start = (t * 2 + q) * chans
+                part = back_ref[s, h, pl.ds(pl.multiple_of(start, 8), chans)].astype(jnp.float32)
+                swapped = block_swap(part, piece)
+                th = t * 2 + h
+                for c in range(n_chan):
+                    column = jnp.concatenate(
+                        [
+                            swapped[c * group : (c + 1) * group, tile * 128 : (tile + 1) * 128]
+                            for tile in range(lat_rows // group)
+                        ],
+                        axis=0,
+                    )
+                    out_ref[c, qs, :, th * 128 : (th + 1) * 128] = column.astype(out_ref.dtype)
+        return carry
+
+    lax.fori_loop(0, out_ref.shape[1], one, 0)
 
 
 def legendre_kernel(modes_ref, base_ref, folded_ref, leg_ref, gain_ref, out_ref, *, block):
@@ -101,7 +171,7 @@
         inv = (basis * math.sqrt(1.0 / total_modes)).astype(jnp.bfloat16)
         ratio = 1.0
 
-    flat = field.reshape(-1, points)
+    flat = jnp.transpose(field, (1, 2, 0, 3, 4)).reshape(-1, points)
     summed = flat[:, :period].astype(jnp.float32)
     for n in range(1, points // period):
         summed = summed + flat[:, n * period : (n + 1) * period].astype(jnp.float32)
@@ -115,15 +185,20 @@
 
     sent = spec_t.reshape(devices, 2 * per_dev, row_count)
     got = lax.all_to_all(sent, ("chan", "lat"), 0, 0, tiled=True)
-    got = got.reshape(n_chan, n_lat, 2, per_dev, chans, fields, 2, cycles)
+    got = jnp.transpose(got.reshape(n_chan, n_lat, 2 * per_dev, row_count), (0, 2, 1, 3))
     sign = jnp.array([[1.0, 1.0], [1.0, -1.0]], jnp.float32)
     weight = mix_weight.astype(jnp.float32).reshape(-1, n_chan, chans)
-    mix_fold = (sign[:, None, None, :, None] * jnp.transpose(weight, (0, 2, 1))[None, :, :, None, :])
-    mix_fold = mix_fold.astype(jnp.bfloat16)
-    folded = jnp.einsum(
-        "pokhC,CLqskthr->sptqoLr", mix_fold, got, preferred_element_type=jnp.float32
-    ).astype(jnp.bfloat16)
-    folded = folded.reshape(per_dev, 2, fields, 2, -1, n_lat * cycles)
+    mix_fold = sign[:, None, None, :, None] * weight[None, :, :, None, :]
+    mix_fold = mix_fold.reshape(2 * weight.shape[0], -1).astype(jnp.bfloat16)
+    piece = cycles
+    folded = pl.pallas_call(
+        functools.partial(gather_kernel, piece=piece, per_dev=per_dev, pairs=2 * fields),
+        out_shape=jax.ShapeDtypeStruct(
+            (per_dev, 2, fields, 2, weight.shape[0], n_lat * cycles), jnp.bfloat16
+        ),
+        scratch_shapes=[pltpu.VMEM((2 * per_dev, fields, n_chan, 2, chans, n_lat * cycles), jnp.float32)],
+        compiler_params=pltpu.CompilerParams(vmem_limit_bytes=48 * 1024 * 1024),
+    )(got, mix_fold)
 
     all_gain = lax.all_gather(spectral_gain, "chan", axis=0, tiled=True)
     gain_par = jnp.transpose(all_gain.reshape(-1, half_deg, 2), (2, 0, 1))
@@ -136,14 +211,19 @@
     back = legendre_stage(
         folded.reshape(per_dev, 2, rows_x, -1), legendre, gain_rows, own_modes, base
     )
-    back = back.reshape(per_dev, 2, fields, 2, n_chan, chans, n_lat, cycles)
-    leaving = jnp.transpose(back, (4, 6, 3, 0, 5, 2, 1, 7)).reshape(devices, 2 * per_dev, row_count)
+    spread = pl.pallas_call(
+        functools.partial(scatter_kernel, piece=piece, per_dev=per_dev, fields=fields),
+        out_shape=jax.ShapeDtypeStruct((n_chan, 2 * per_dev, n_lat, row_count), jnp.bfloat16),
+        compiler_params=pltpu.CompilerParams(vmem_limit_bytes=48 * 1024 * 1024),
+    )(back)
+    leaving = jnp.transpose(spread, (0, 2, 1, 3)).reshape(devices, 2 * per_dev, row_count)
     returned = lax.all_to_all(leaving, ("chan", "lat"), 0, 0, tiled=True)
     returned = returned.reshape(2 * total_modes, row_count)
 
     waveform = lax.dot_general(
         returned, inv, (((0,), (0,)), ((), ())), preferred_element_type=jnp.float32
     ) * ratio
+    waveform = jnp.transpose(waveform.reshape(fields, 2, chans, cycles, period), (2, 0, 1, 3, 4))
     waveform = waveform.reshape(chans, fields, -1, period)
     primal_h = waveform[:, 0]
     sigmoid_h = jax.nn.sigmoid(primal_h)

time: 189 us -> 142 us (0.75)
  local copies, waits for them, and re-layouts: 68.6 us -> 8.99 us
  Pallas kernels: 12.8 us -> 37.6 us
  matrix products: 18.2 us -> 8.66 us
    reshape x4 -> x2, local copies, waits for them, and re-layouts: 25.8 us -> 0.72 us  [the longest x1 0.38 us: local(): waveform.reshape(fields, 2, chans, cycles, period)]
    pallas_call x0 -> x2, Pallas kernels: none -> 24.5 us  [the longest x1 13 us: local(): pl.pallas_call(functools.partial(gather_kernel, piece=piece, per_dev=per_...]
    convert_element_type x1 -> x2, local copies, waits for them, and re-layouts: 12.7 us -> 0.18 us  [local(): mix_fold = mix_fold.reshape(2 * weight.shape[0], -1).astype(jnp.bfloat16)]
    transpose x2 -> x1, local copies, waits for them, and re-layouts: 14.5 us -> 2.03 us  [local(): jnp.transpose(spread, (0, 2, 1, 3)).reshape(devices, 2 * per_dev, row_count)]
    another operation x2 -> x0, local copies, waits for them, and re-layouts: 11.5 us -> none  [local(): folded.reshape(per_dev, 2, rows_x, -1)]
    dot_general x1 -> x0, matrix products: 9.57 us -> none  [local(): jnp.einsum('pokhC,CLqskthr->sptqoLr', mix_fold, got, preferred_element_ty...]
    unnamed x18 -> x19, local copies, waits for them, and re-layouts: 0.95 us -> 3.95 us
  transfers between devices with their start and end apart: 2 -> 2, of which waited for: 1 -> 1; matrix products, arithmetic and copies ran while one was open for 4% -> 6% of each run, Pallas kernels for 0% -> 0%
where the time goes in v3:
time: 142 us
  Pallas kernels  37.6 us (26%)
  blocking collectives  26 us (18%)
  other arithmetic  22.7 us (16%)
  starting transfers between devices  20.7 us (15%)
  waiting for transfers between devices  17 us (12%)
  local copies, waits for them, and re-layouts  8.99 us (6%)
  matrix products  8.66 us (6%)
    all_gather x1, blocking collectives, local(): all_gain = lax.all_gather(spectral_gain, 'chan', axis=0, tiled=True)  26 us
    all_to_all x1, waiting for transfers between devices, local(): returned = lax.all_to_all(leaving, ('chan', 'lat'), 0, 0, tiled=True)  17 us
    pallas_call x1, Pallas kernels, legendre_stage(): pl.pallas_call(functools.partial(legendre_kernel, block=block), grid_spec...  13 us
    pallas_call x1, Pallas kernels, local(): pl.pallas_call(functools.partial(gather_kernel, piece=piece, per_dev=per_...  13 us
    pallas_call x1, Pallas kernels, local(): pl.pallas_call(functools.partial(scatter_kernel, piece=piece, per_dev=per...  11.5 us
    all_to_all x1, starting transfers between devices, local(): got = lax.all_to_all(sent, ('chan', 'lat'), 0, 0, tiled=True)  11.1 us
    all_to_all x1, starting transfers between devices, local(): returned = lax.all_to_all(leaving, ('chan', 'lat'), 0, 0, tiled=True)  9.52 us
    convert_element_type x1, other arithmetic, local(): initial = flat[:, :, :, n * period:(n + 1) * period].astype(jnp.float32)  7.23 us
  transfers between devices with their start and end apart: 2, of which 1 were waited for; matrix products, arithmetic and copies ran while one was open for 6% of the time, Pallas kernels for 0%

profile of v3, /device:TPU:0, one launch (start us, length us, event | category | flops | bytes accessed | tf_op | source)
XLA Modules:
  0.0 141.8 jit_solution(14010579776459789739)
XLA Ops:
  0.0 0.7 broadcast_multiply_fusion.1
  1.2 2.4 %fusion.32 = (f32[128,4,128]{2,1,0:T(4,128)S(1)}, f32[128,4,128]{2,1,0:T(4,128)S(1)}) fusion(s32[128,4]{1,0:T(8,128)S(1)} %copy.28), kind=kLoop, calls=%fused_computation.49 | loop fusion | flops 917504 | bytes 526336 | tf_op jit(solution)/shard_map/cos | solution.py:163
  4.4 2.5 %multiply_convert_fusion = bf16[128,2,4,8,128]{4,3,2,1,0:T(8,128)(2,1)S(1)} fusion(f32[128,4,128]{2,1,0:T(4,128)S(1)} %get-tuple-element.21, f32[128,2,4,8]{3,2,1,0:T(4,128)S(1)} %copy.29, f32[128,4,128]{2,1,0:T(4,128)S(1)} %get-tuple-element.20, f32[128,2,4,8]{3,2,1,0:T(4,128)S(1)} %copy.27), kind=kLoop, calls=%fused_computation.5 | loop fusion | flops 5242880 | bytes 2686976 | tf_op jit(solution)/shard_map/convert_element_type | solution.py:165
  6.9 0.6 copy.45
  7.5 0.8 copy.30
  8.3 1.6 %subtract_convert_fusion = (bf16[768,1024]{1,0:T(8,128)(2,1)S(1)}, bf16[768,1024]{1,0:T(8,128)(2,1)S(1)}) fusion(bf16[768,4096]{1,0:T(8,128)(2,1)S(1)} %bitcast.61), kind=kLoop, calls=%fused_computation.9 | loop fusion | flops 8650752 | bytes 9437184 | tf_op jit(solution)/shard_map/convert_element_type | solution.py:179
  9.9 4.6 %fusion.17 = bf16[128,8,768]{2,1,0:T(8,128)(2,1)} fusion(bf16[768,1024]{1,0:T(8,128)(2,1)S(1)} %get-tuple-element.5, bf16[768,1024]{1,0:T(8,128)(2,1)S(1)} %get-tuple-element.6, bf16[1024,1024]{1,0:T(8,128)(2,1)S(1)} %bitcast.67), kind=kOutput, calls=%fused_computation.29 | convolution fusion | flops 3236691968 | bytes 6815744 | tf_op jit(solution)/shard_map/dot_general | solution.py:181
  14.5 11.1 %all-to-all-start = ((bf16[128,8,768]{2,1,0:T(8,128)(2,1)}), bf16[128,8,768]{2,1,0:T(8,128)(2,1)S(1)}, u32[]{:S(2)}, u32[]{:S(2)}) async-start(bf16[128,8,768]{2,1,0:T(8,128)(2,1)} %fusion.17), calls=%async_computation | async-start | bytes 3145728 | tf_op jit(solution)/shard_map/all_to_all | solution.py:187
  26.2 26.0 %all_gather.3 = f32[32,2048]{1,0:T(8,128)S(1)} all-gather(f32[8,2048]{1,0:T(8,128)S(1)} %copy-done.5), channel_id=1, replica_groups=mesh['lat'=32,'chan'=4] {'chan'}, dimensions={0}, use_global_device_ids=true | all-gather | bytes 327680 | tf_op jit(solution)/shard_map/all_gather | solution.py:203
  52.5 0.4 copy.35
  53.4 13.0 %shard_map.73 = bf16[4,2,3,2,32,512]{5,4,3,2,1,0:T(8,128)(2,1)S(1)} custom-call(bf16[4,8,32,768]{3,2,1,0:T(8,128)(2,1)S(1)} %bitcast.59, bf16[64,64]{1,0:T(8,128)(2,1)S(1)} %copy.33.mix_ref), custom_call_target="tpu_custom_call" | custom-call | tf_op jit(solution)/shard_map/pallas_call | solution.py:194
  66.6 13.0 %shard_map.74.back_ref = bf16[4,2,192,512]{3,2,1,0:T(8,128)(2,1)S(1)} custom-call(s32[4]{0:T(128)S(1)} %dynamic_slice.3.modes_ref, s32[1]{0:T(128)} %bitcast.2.base_ref, bf16[4,2,192,512]{3,2,1,0:T(8,128)(2,1)S(1)} %bitcast.57, bf16[2,16,512,1024]{3,2,1,0:T(8,128)(2,1)} %leg_ref.1, f32[2,192,1024]{2,1,0:T(8,128)S(1)} %bitcast.58), custom_call_target="tpu_custom_call" | custom-call | flops 3221225472 | bytes 13107200 | tf_op jit(solution)/shard_map/pallas_call | solution.py:124
  79.7 11.5 %shard_map.75 = bf16[4,8,32,768]{3,2,1,0:T(8,128)(2,1)S(1)} custom-call(bf16[4,2,192,512]{3,2,1,0:T(8,128)(2,1)S(1)} %shard_map.74.back_ref), custom_call_target="tpu_custom_call" | custom-call | tf_op jit(solution)/shard_map/pallas_call | solution.py:214
  91.2 2.0 %copy.36 = bf16[4,32,8,768]{3,2,1,0:T(8,128)(2,1)} copy(bf16[4,32,8,768]{3,1,2,0:T(8,128)(2,1)S(1)} %bitcast.60) | data formatting | bytes 3145728 | tf_op jit(solution)/shard_map/transpose | solution.py:219
  93.2 9.5 %all-to-all-start.1 = ((bf16[128,8,768]{2,1,0:T(8,128)(2,1)}), bf16[128,8,768]{2,1,0:T(8,128)(2,1)}, u32[]{:S(2)}, u32[]{:S(2)}) async-start(bf16[128,8,768]{2,1,0:T(8,128)(2,1)} %bitcast.15), calls=%async_computation.1 | async-start | bytes 3145728 | tf_op jit(solution)/shard_map/all_to_all | solution.py:220
  102.7 7.2 %slice_convert_fusion.3 = (f32[8,3,32,1024]{3,2,1,0:T(8,128)S(1)}, f32[8,3,32,1024]{3,2,1,0:T(8,128)}, f32[8,3,32,1024]{3,2,1,0:T(8,128)}, f32[8,3,32,1024]{3,2,1,0:T(8,128)}) fusion(bf16[8,3,32,4096]{3,2,1,0:T(8,128)(2,1)} %bitcast.62), kind=kLoop, calls=%fused_computation.26 | loop fusion | flops 3145728 | bytes 18874368 | tf_op jit(solution)/shard_map/convert_element_type | solution.py:235
  110.0 17.0 %all-to-all-done.1 = bf16[128,8,768]{2,1,0:T(8,128)(2,1)} async-done(((bf16[128,8,768]{2,1,0:T(8,128)(2,1)}), bf16[128,8,768]{2,1,0:T(8,128)(2,1)}, u32[]{:S(2)}, u32[]{:S(2)}) %all-to-all-start.1) | async-done | bytes 1572896 | tf_op jit(solution)/shard_map/all_to_all | solution.py:220
  127.0 4.0 %convolution_multiply_fusion = f32[768,1024]{1,0:T(8,128)S(1)} fusion(bf16[1024,1024]{1,0:T(8,128)(2,1)} %bitcast.68, bf16[128,8,768]{2,1,0:T(8,128)(2,1)} %all-to-all-done.1), kind=kOutput, calls=%fused_computation.21 | convolution fusion | flops 1611399168 | bytes 6815744 | tf_op jit(solution)/shard_map/dot_general | solution.py:223
  131.0 0.4 copy.37
  131.4 1.5 %copy-done.1 = f32[8,3,32,1024]{3,2,1,0:T(8,128)S(1)} copy-done((f32[8,3,32,1024]{3,2,1,0:T(8,128)S(1)}, f32[8,3,32,1024]{3,2,1,0:T(8,128)}, u32[]{:S(2)}) %copy-start.1) | copy-done | bytes 3145752
  132.9 1.0 copy-done.2
  133.9 1.7 %fusion.25 = (bf16[8,1,32,1024]{3,2,1,0:T(8,128)(2,1)S(1)}, bf16[8,1,32,1024]{3,2,1,0:T(8,128)(2,1)S(1)}, bf16[8,1,32,1024]{3,2,1,0:T(8,128)(2,1)}, bf16[8,1,32,1024]{3,2,1,0:T(8,128)(2,1)}, f32[8,32,1024]{2,1,0:T(8,128)S(1)}) fusion(f32[8,3,32,1024]{3,2,1,0:T(8,128)S(1)} %get-tuple-element.7, f32[8,3,32,1024]{3,2,1,0:T(8,128)S(1)} %bitcast.63, ...), kind=kLoop, calls=%fused_computation.37 | loop fusion | flops 4194304 | bytes 8388608 | tf_op jit(solution)/shard_map/convert.16
  135.6 1.7 %fusion.10 = (bf16[8,2,32,1024]{3,2,1,0:T(8,128)(2,1)S(1)}, bf16[8,2,32,1024]{3,2,1,0:T(8,128)(2,1)S(1)}, bf16[8,2,32,1024]{3,2,1,0:T(8,128)(2,1)S(1)}, bf16[8,2,32,1024]{3,2,1,0:T(8,128)(2,1)S(1)}) fusion(f32[8,3,32,1024]{3,2,1,0:T(8,128)S(1)} %get-tuple-element.7, f32[8,3,32,1024]{3,2,1,0:T(8,128)S(1)} %bitcast.64, ...), kind=kLoop, calls=%fused_computation.20 | loop fusion | flops 4718592 | bytes 15728640 | tf_op jit(solution)/shard_map/convert.15
  137.2 4.6 %maximum_maximum_fusion = bf16[8,3,2,16,4096]{4,3,2,1,0:T(8,128)(2,1)} fusion(bf16[8,2,2,16,1024]{4,3,2,1,0:T(8,128)(2,1)S(1)} %bitcast.74, bf16[8,1,2,16,1024]{4,3,2,1,0:T(8,128)(2,1)} %bitcast.78, bf16[8,2,2,16,1024]{4,3,2,1,0:T(8,128)(2,1)S(1)} %bitcast.73, bf16[8,1,2,16,1024]{4,3,2,1,0:T(8,128)(2,1)} %bitcast.77, ...), kind=kLoop, calls=%fused_computation | loop fusion | flops 50331648 | bytes 12582912 | tf_op jit(solution)/shard_map/concatenate | solution.py:239
  (36 shorter events, 2.7 us)
Async XLA Ops:
  4.4 3.1 %copy-start = (bf16[8,3,2,16,4096]{4,3,2,1,0:T(8,128)(2,1)S(1)}, bf16[8,3,2,16,4096]{4,3,2,1,0:T(8,128)(2,1)}, u32[]{:S(2)}) copy-start(bf16[8,3,2,16,4096]{4,3,2,1,0:T(8,128)(2,1)} %param.7) | copy-start | bytes 18874372
  7.5 2.4 %copy-start.4 = (bf16[128,8,8,128]{3,1,2,0:T(8,128)(2,1)}, bf16[128,8,8,128]{3,1,2,0:T(8,128)(2,1)S(1)}, u32[]{:S(2)}) copy-start(bf16[128,8,8,128]{3,1,2,0:T(8,128)(2,1)S(1)} %copy.45) | copy-start | bytes 6291460
  14.5 11.2 %copy-start.6 = (bf16[32,32]{1,0:T(8,128)(2,1)S(1)}, bf16[32,32]{1,0:T(8,128)(2,1)}, u32[]{:S(2)}) copy-start(bf16[32,32]{1,0:T(8,128)(2,1)} %param.8) | copy-start | bytes 6148
  14.5 11.3 %copy-start.7 = (f32[2,2]{0,1:T(2,128)S(1)}, f32[2,2]{0,1:T(2,128)}, u32[]{:S(2)}) copy-start(f32[2,2]{0,1:T(2,128)} %constant.57.clone) | copy-start | bytes 52
  14.5 11.7 %copy-start.5 = (f32[8,2048]{1,0:T(8,128)S(1)}, f32[8,2048]{1,0:T(8,128)}, u32[]{:S(2)}) copy-start(f32[8,2048]{1,0:T(8,128)} %param.9) | copy-start | bytes 196612
  14.5 38.6 %all-to-all-start = ((bf16[128,8,768]{2,1,0:T(8,128)(2,1)}), bf16[128,8,768]{2,1,0:T(8,128)(2,1)S(1)}, u32[]{:S(2)}, u32[]{:S(2)}) async-start(bf16[128,8,768]{2,1,0:T(8,128)(2,1)} %fusion.17), calls=%async_computation | async-start | bytes 3145728 | tf_op jit(solution)/shard_map/all_to_all | solution.py:187
  93.2 33.7 %all-to-all-start.1 = ((bf16[128,8,768]{2,1,0:T(8,128)(2,1)}), bf16[128,8,768]{2,1,0:T(8,128)(2,1)}, u32[]{:S(2)}, u32[]{:S(2)}) async-start(bf16[128,8,768]{2,1,0:T(8,128)(2,1)} %bitcast.15), calls=%async_computation.1 | async-start | bytes 3145728 | tf_op jit(solution)/shard_map/all_to_all | solution.py:220
  126.9 4.5 %copy-start.3 = (f32[8,3,32,1024]{3,2,1,0:T(8,128)S(1)}, f32[8,3,32,1024]{3,2,1,0:T(8,128)}, u32[]{:S(2)}) copy-start(f32[8,3,32,1024]{3,2,1,0:T(8,128)} %get-tuple-element.10) | copy-start | bytes 9437188
  131.0 1.9 %copy-start.1 = (f32[8,3,32,1024]{3,2,1,0:T(8,128)S(1)}, f32[8,3,32,1024]{3,2,1,0:T(8,128)}, u32[]{:S(2)}) copy-start(f32[8,3,32,1024]{3,2,1,0:T(8,128)} %get-tuple-element.8) | copy-start | bytes 9437188
  131.0 2.8 %copy-start.2 = (f32[8,3,32,1024]{3,2,1,0:T(8,128)S(1)}, f32[8,3,32,1024]{3,2,1,0:T(8,128)}, u32[]{:S(2)}) copy-start(f32[8,3,32,1024]{3,2,1,0:T(8,128)} %get-tuple-element.9) | copy-start | bytes 9437188

commit v4 on v3

--- a/solution.py
+++ b/solution.py
@@ -10,17 +10,25 @@
 
 
 def block_swap(x, piece):
-    rows, width = x.shape
-    group = 128 // piece
-    row = lax.broadcasted_iota(jnp.int32, x.shape, 0) % group
-    blk = (lax.broadcasted_iota(jnp.int32, x.shape, 1) % 128) // piece
-    out = jnp.zeros_like(x)
-    for d in range(1 - group, group):
-        moved = x if d == 0 else pltpu.roll(x, (-piece * d) % width, 1)
-        keep = (blk == row) & (row + d >= 0) & (row + d < group)
-        moved = jnp.where(keep, moved, 0.0)
-        out = out + (moved if d == 0 else pltpu.roll(moved, d % rows, 0))
+    group, width = x.shape[1], x.shape[2]
+    row = lax.broadcasted_iota(jnp.int32, x.shape, 1)
+    blk = lax.broadcasted_iota(jnp.int32, x.shape, 2) // piece
+    out = jnp.where(blk == row, x, 0.0)
+    for d in range(1, group):
+        moved = pltpu.roll(x, (-piece * d) % width, 2)
+        moved = jnp.where(blk == row, moved, 0.0)
+        out = out + pltpu.roll(moved, d, 1)
     return out
+
+
+def tiles_of(x, group):
+    return jnp.stack(
+        [
+            x[i * group : (i + 1) * group, j * 128 : (j + 1) * 128]
+            for i in range(x.shape[0] // group)
+            for j in range(x.shape[1] // 128)
+        ]
+    )
 
 
 def gather_kernel(got_ref, mix_ref, out_ref, stage_ref, *, piece, per_dev, pairs):
@@ -30,11 +38,11 @@
 
     def one(qs, carry):
         for c in range(n_chan):
-            swapped = block_swap(got_ref[c, qs].astype(jnp.float32), piece)
-            for th in range(pairs):
-                for tile in range(lat_rows // group):
+            swapped = block_swap(tiles_of(got_ref[c, qs].astype(jnp.float32), group), piece)
+            for tile in range(lat_rows // group):
+                for th in range(pairs):
                     stage_ref[qs, th // 2, c, th % 2, :, tile * 128 : (tile + 1) * 128] = swapped[
-                        tile * group : (tile + 1) * group, th * 128 : (th + 1) * 128
+                        tile * pairs + th
                     ]
         q = qs // per_dev
         s = qs % per_dev
@@ -63,15 +71,12 @@
             for h in range(2):
                 start = (t * 2 + q) * chans
                 part = back_ref[s, h, pl.ds(pl.multiple_of(start, 8), chans)].astype(jnp.float32)
-                swapped = block_swap(part, piece)
+                swapped = block_swap(tiles_of(part, group), piece)
                 th = t * 2 + h
+                lane_tiles = part.shape[1] // 128
                 for c in range(n_chan):
                     column = jnp.concatenate(
-                        [
-                            swapped[c * group : (c + 1) * group, tile * 128 : (tile + 1) * 128]
-                            for tile in range(lat_rows // group)
-                        ],
-                        axis=0,
+                        [swapped[c * lane_tiles + tile] for tile in range(lat_rows // group)], axis=0
                     )
                     out_ref[c, qs, :, th * 128 : (th + 1) * 128] = column.astype(out_ref.dtype)
         return carry

time: 142 us -> 127 us (0.89)
  Pallas kernels: 37.6 us -> 21.8 us
    pallas_call x1, Pallas kernels: 13 us -> 5.01 us  [local(): pl.pallas_call(functools.partial(gather_kernel, piece=piece, per_dev=per_...]
    pallas_call x1, Pallas kernels: 11.5 us -> 3.78 us  [local(): pl.pallas_call(functools.partial(scatter_kernel, piece=piece, per_dev=per...]
  transfers between devices with their start and end apart: 2 -> 2, of which waited for: 1 -> 1; matrix products, arithmetic and copies ran while one was open for 6% -> 7% of each run, Pallas kernels for 0% -> 0%
where the time goes in v4:
time: 127 us; the launch traced here: 126 us
  blocking collectives  26 us (20%)
  other arithmetic  22.7 us (18%)
  Pallas kernels  21.8 us (17%)
  starting transfers between devices  20.3 us (16%)
  waiting for transfers between devices  17.2 us (14%)
  local copies, waits for them, and re-layouts  8.99 us (7%)
  matrix products  8.66 us (7%)
    all_gather x1, blocking collectives, local(): all_gain = lax.all_gather(spectral_gain, 'chan', axis=0, tiled=True)  26 us
    all_to_all x1, waiting for transfers between devices, local(): returned = lax.all_to_all(leaving, ('chan', 'lat'), 0, 0, tiled=True)  17.2 us
    pallas_call x1, Pallas kernels, legendre_stage(): pl.pallas_call(functools.partial(legendre_kernel, block=block), grid_spec...  13.1 us
    all_to_all x1, starting transfers between devices, local(): got = lax.all_to_all(sent, ('chan', 'lat'), 0, 0, tiled=True)  11.1 us
    all_to_all x1, starting transfers between devices, local(): returned = lax.all_to_all(leaving, ('chan', 'lat'), 0, 0, tiled=True)  9.13 us
    convert_element_type x1, other arithmetic, local(): initial = flat[:, :, :, n * period:(n + 1) * period].astype(jnp.float32)  7.23 us
    pallas_call x1, Pallas kernels, local(): pl.pallas_call(functools.partial(gather_kernel, piece=piece, per_dev=per_...  5.01 us
    dot_general x1, matrix products, local(): lax.dot_general(jnp.concatenate([fwd, fwd], axis=1), rows, (((1,), (1,)),...  4.61 us
  transfers between devices with their start and end apart: 2, of which 1 were waited for; matrix products, arithmetic and copies ran while one was open for 7% of the time, Pallas kernels for 0%

profile of v4, /device:TPU:0, one launch (start us, length us, event | category | flops | bytes accessed | tf_op | source)
XLA Modules:
  0.0 125.9 jit_solution(9135683891875769639)
XLA Ops:
  0.0 0.7 broadcast_multiply_fusion.1
  1.2 2.4 %fusion.32 = (f32[128,4,128]{2,1,0:T(4,128)S(1)}, f32[128,4,128]{2,1,0:T(4,128)S(1)}) fusion(s32[128,4]{1,0:T(8,128)S(1)} %copy.28), kind=kLoop, calls=%fused_computation.49 | loop fusion | flops 917504 | bytes 526336 | tf_op jit(solution)/shard_map/cos | solution.py:168
  4.4 2.5 %multiply_convert_fusion = bf16[128,2,4,8,128]{4,3,2,1,0:T(8,128)(2,1)S(1)} fusion(f32[128,4,128]{2,1,0:T(4,128)S(1)} %get-tuple-element.21, f32[128,2,4,8]{3,2,1,0:T(4,128)S(1)} %copy.29, f32[128,4,128]{2,1,0:T(4,128)S(1)} %get-tuple-element.20, f32[128,2,4,8]{3,2,1,0:T(4,128)S(1)} %copy.27), kind=kLoop, calls=%fused_computation.5 | loop fusion | flops 5242880 | bytes 2686976 | tf_op jit(solution)/shard_map/convert_element_type | solution.py:170
  6.9 0.6 copy.45
  7.5 0.8 copy.30
  8.3 1.6 %subtract_convert_fusion = (bf16[768,1024]{1,0:T(8,128)(2,1)S(1)}, bf16[768,1024]{1,0:T(8,128)(2,1)S(1)}) fusion(bf16[768,4096]{1,0:T(8,128)(2,1)S(1)} %bitcast.61), kind=kLoop, calls=%fused_computation.9 | loop fusion | flops 8650752 | bytes 9437184 | tf_op jit(solution)/shard_map/convert_element_type | solution.py:184
  9.9 4.6 %fusion.17 = bf16[128,8,768]{2,1,0:T(8,128)(2,1)} fusion(bf16[768,1024]{1,0:T(8,128)(2,1)S(1)} %get-tuple-element.5, bf16[768,1024]{1,0:T(8,128)(2,1)S(1)} %get-tuple-element.6, bf16[1024,1024]{1,0:T(8,128)(2,1)S(1)} %bitcast.67), kind=kOutput, calls=%fused_computation.29 | convolution fusion | flops 3236691968 | bytes 6815744 | tf_op jit(solution)/shard_map/dot_general | solution.py:186
  14.5 11.1 %all-to-all-start = ((bf16[128,8,768]{2,1,0:T(8,128)(2,1)}), bf16[128,8,768]{2,1,0:T(8,128)(2,1)S(1)}, u32[]{:S(2)}, u32[]{:S(2)}) async-start(bf16[128,8,768]{2,1,0:T(8,128)(2,1)} %fusion.17), calls=%async_computation | async-start | bytes 3145728 | tf_op jit(solution)/shard_map/all_to_all | solution.py:192
  26.2 26.0 %all_gather.3 = f32[32,2048]{1,0:T(8,128)S(1)} all-gather(f32[8,2048]{1,0:T(8,128)S(1)} %copy-done.5), channel_id=1, replica_groups=mesh['lat'=32,'chan'=4] {'chan'}, dimensions={0}, use_global_device_ids=true | all-gather | bytes 327680 | tf_op jit(solution)/shard_map/all_gather | solution.py:208
  52.5 0.4 copy.35
  53.4 5.0 %shard_map.73 = bf16[4,2,3,2,32,512]{5,4,3,2,1,0:T(8,128)(2,1)S(1)} custom-call(bf16[4,8,32,768]{3,2,1,0:T(8,128)(2,1)S(1)} %bitcast.59, bf16[64,64]{1,0:T(8,128)(2,1)S(1)} %copy.33.mix_ref), custom_call_target="tpu_custom_call" | custom-call | tf_op jit(solution)/shard_map/pallas_call | solution.py:199
  58.6 13.1 %shard_map.74.back_ref = bf16[4,2,192,512]{3,2,1,0:T(8,128)(2,1)S(1)} custom-call(s32[4]{0:T(128)S(1)} %dynamic_slice.3.modes_ref, s32[1]{0:T(128)} %bitcast.2.base_ref, bf16[4,2,192,512]{3,2,1,0:T(8,128)(2,1)S(1)} %bitcast.57, bf16[2,16,512,1024]{3,2,1,0:T(8,128)(2,1)} %leg_ref.1, f32[2,192,1024]{2,1,0:T(8,128)S(1)} %bitcast.58), custom_call_target="tpu_custom_call" | custom-call | flops 3221225472 | bytes 13107200 | tf_op jit(solution)/shard_map/pallas_call | solution.py:129
  71.7 3.8 %shard_map.75 = bf16[4,8,32,768]{3,2,1,0:T(8,128)(2,1)S(1)} custom-call(bf16[4,2,192,512]{3,2,1,0:T(8,128)(2,1)S(1)} %shard_map.74.back_ref), custom_call_target="tpu_custom_call" | custom-call | tf_op jit(solution)/shard_map/pallas_call | solution.py:219
  75.5 2.0 %copy.36 = bf16[4,32,8,768]{3,2,1,0:T(8,128)(2,1)} copy(bf16[4,32,8,768]{3,1,2,0:T(8,128)(2,1)S(1)} %bitcast.60) | data formatting | bytes 3145728 | tf_op jit(solution)/shard_map/transpose | solution.py:224
  77.5 9.1 %all-to-all-start.1 = ((bf16[128,8,768]{2,1,0:T(8,128)(2,1)}), bf16[128,8,768]{2,1,0:T(8,128)(2,1)}, u32[]{:S(2)}, u32[]{:S(2)}) async-start(bf16[128,8,768]{2,1,0:T(8,128)(2,1)} %bitcast.15), calls=%async_computation.1 | async-start | bytes 3145728 | tf_op jit(solution)/shard_map/all_to_all | solution.py:225
  86.6 7.2 %slice_convert_fusion.3 = (f32[8,3,32,1024]{3,2,1,0:T(8,128)S(1)}, f32[8,3,32,1024]{3,2,1,0:T(8,128)}, f32[8,3,32,1024]{3,2,1,0:T(8,128)}, f32[8,3,32,1024]{3,2,1,0:T(8,128)}) fusion(bf16[8,3,32,4096]{3,2,1,0:T(8,128)(2,1)} %bitcast.62), kind=kLoop, calls=%fused_computation.26 | loop fusion | flops 3145728 | bytes 18874368 | tf_op jit(solution)/shard_map/convert_element_type | solution.py:240
  93.9 17.2 %all-to-all-done.1 = bf16[128,8,768]{2,1,0:T(8,128)(2,1)} async-done(((bf16[128,8,768]{2,1,0:T(8,128)(2,1)}), bf16[128,8,768]{2,1,0:T(8,128)(2,1)}, u32[]{:S(2)}, u32[]{:S(2)}) %all-to-all-start.1) | async-done | bytes 1572896 | tf_op jit(solution)/shard_map/all_to_all | solution.py:225
  111.1 4.0 %convolution_multiply_fusion = f32[768,1024]{1,0:T(8,128)S(1)} fusion(bf16[1024,1024]{1,0:T(8,128)(2,1)} %bitcast.68, bf16[128,8,768]{2,1,0:T(8,128)(2,1)} %all-to-all-done.1), kind=kOutput, calls=%fused_computation.21 | convolution fusion | flops 1611399168 | bytes 6815744 | tf_op jit(solution)/shard_map/dot_general | solution.py:228
  115.1 0.4 copy.37
  115.5 1.5 %copy-done.1 = f32[8,3,32,1024]{3,2,1,0:T(8,128)S(1)} copy-done((f32[8,3,32,1024]{3,2,1,0:T(8,128)S(1)}, f32[8,3,32,1024]{3,2,1,0:T(8,128)}, u32[]{:S(2)}) %copy-start.1) | copy-done | bytes 3145752
  117.0 1.0 copy-done.2
  118.0 1.7 %fusion.25 = (bf16[8,1,32,1024]{3,2,1,0:T(8,128)(2,1)S(1)}, bf16[8,1,32,1024]{3,2,1,0:T(8,128)(2,1)S(1)}, bf16[8,1,32,1024]{3,2,1,0:T(8,128)(2,1)}, bf16[8,1,32,1024]{3,2,1,0:T(8,128)(2,1)}, f32[8,32,1024]{2,1,0:T(8,128)S(1)}) fusion(f32[8,3,32,1024]{3,2,1,0:T(8,128)S(1)} %get-tuple-element.7, f32[8,3,32,1024]{3,2,1,0:T(8,128)S(1)} %bitcast.63, ...), kind=kLoop, calls=%fused_computation.37 | loop fusion | flops 4194304 | bytes 8388608 | tf_op jit(solution)/shard_map/convert.16
  119.7 1.7 %fusion.10 = (bf16[8,2,32,1024]{3,2,1,0:T(8,128)(2,1)S(1)}, bf16[8,2,32,1024]{3,2,1,0:T(8,128)(2,1)S(1)}, bf16[8,2,32,1024]{3,2,1,0:T(8,128)(2,1)S(1)}, bf16[8,2,32,1024]{3,2,1,0:T(8,128)(2,1)S(1)}) fusion(f32[8,3,32,1024]{3,2,1,0:T(8,128)S(1)} %get-tuple-element.7, f32[8,3,32,1024]{3,2,1,0:T(8,128)S(1)} %bitcast.64, ...), kind=kLoop, calls=%fused_computation.20 | loop fusion | flops 4718592 | bytes 15728640 | tf_op jit(solution)/shard_map/convert.15
  121.4 4.6 %maximum_maximum_fusion = bf16[8,3,2,16,4096]{4,3,2,1,0:T(8,128)(2,1)} fusion(bf16[8,2,2,16,1024]{4,3,2,1,0:T(8,128)(2,1)S(1)} %bitcast.74, bf16[8,1,2,16,1024]{4,3,2,1,0:T(8,128)(2,1)} %bitcast.78, bf16[8,2,2,16,1024]{4,3,2,1,0:T(8,128)(2,1)S(1)} %bitcast.73, bf16[8,1,2,16,1024]{4,3,2,1,0:T(8,128)(2,1)} %bitcast.77, ...), kind=kLoop, calls=%fused_computation | loop fusion | flops 50331648 | bytes 12582912 | tf_op jit(solution)/shard_map/concatenate | solution.py:244
  (36 shorter events, 2.7 us)
Async XLA Ops:
  4.4 3.1 %copy-start = (bf16[8,3,2,16,4096]{4,3,2,1,0:T(8,128)(2,1)S(1)}, bf16[8,3,2,16,4096]{4,3,2,1,0:T(8,128)(2,1)}, u32[]{:S(2)}) copy-start(bf16[8,3,2,16,4096]{4,3,2,1,0:T(8,128)(2,1)} %param.7) | copy-start | bytes 18874372
  7.5 2.4 %copy-start.4 = (bf16[128,8,8,128]{3,1,2,0:T(8,128)(2,1)}, bf16[128,8,8,128]{3,1,2,0:T(8,128)(2,1)S(1)}, u32[]{:S(2)}) copy-start(bf16[128,8,8,128]{3,1,2,0:T(8,128)(2,1)S(1)} %copy.45) | copy-start | bytes 6291460
  14.5 11.2 %copy-start.6 = (bf16[32,32]{1,0:T(8,128)(2,1)S(1)}, bf16[32,32]{1,0:T(8,128)(2,1)}, u32[]{:S(2)}) copy-start(bf16[32,32]{1,0:T(8,128)(2,1)} %param.8) | copy-start | bytes 6148
  14.5 11.3 %copy-start.7 = (f32[2,2]{0,1:T(2,128)S(1)}, f32[2,2]{0,1:T(2,128)}, u32[]{:S(2)}) copy-start(f32[2,2]{0,1:T(2,128)} %constant.57.clone) | copy-start | bytes 52
  14.5 11.7 %copy-start.5 = (f32[8,2048]{1,0:T(8,128)S(1)}, f32[8,2048]{1,0:T(8,128)}, u32[]{:S(2)}) copy-start(f32[8,2048]{1,0:T(8,128)} %param.9) | copy-start | bytes 196612
  14.5 38.6 %all-to-all-start = ((bf16[128,8,768]{2,1,0:T(8,128)(2,1)}), bf16[128,8,768]{2,1,0:T(8,128)(2,1)S(1)}, u32[]{:S(2)}, u32[]{:S(2)}) async-start(bf16[128,8,768]{2,1,0:T(8,128)(2,1)} %fusion.17), calls=%async_computation | async-start | bytes 3145728 | tf_op jit(solution)/shard_map/all_to_all | solution.py:192
  77.5 33.6 %all-to-all-start.1 = ((bf16[128,8,768]{2,1,0:T(8,128)(2,1)}), bf16[128,8,768]{2,1,0:T(8,128)(2,1)}, u32[]{:S(2)}, u32[]{:S(2)}) async-start(bf16[128,8,768]{2,1,0:T(8,128)(2,1)} %bitcast.15), calls=%async_computation.1 | async-start | bytes 3145728 | tf_op jit(solution)/shard_map/all_to_all | solution.py:225
  111.1 4.5 %copy-start.3 = (f32[8,3,32,1024]{3,2,1,0:T(8,128)S(1)}, f32[8,3,32,1024]{3,2,1,0:T(8,128)}, u32[]{:S(2)}) copy-start(f32[8,3,32,1024]{3,2,1,0:T(8,128)} %get-tuple-element.10) | copy-start | bytes 9437188
  115.1 1.9 %copy-start.1 = (f32[8,3,32,1024]{3,2,1,0:T(8,128)S(1)}, f32[8,3,32,1024]{3,2,1,0:T(8,128)}, u32[]{:S(2)}) copy-start(f32[8,3,32,1024]{3,2,1,0:T(8,128)} %get-tuple-element.8) | copy-start | bytes 9437188
  115.1 2.8 %copy-start.2 = (f32[8,3,32,1024]{3,2,1,0:T(8,128)S(1)}, f32[8,3,32,1024]{3,2,1,0:T(8,128)}, u32[]{:S(2)}) copy-start(f32[8,3,32,1024]{3,2,1,0:T(8,128)} %get-tuple-element.9) | copy-start | bytes 9437188

commit v5 on v4

--- a/solution.py
+++ b/solution.py
@@ -93,7 +93,7 @@
     syn = []
     for p in range(2):
         lhs = folded_ref[0, p]
-        acc = jnp.zeros((rows, north), jnp.float32)
+        acc = jnp.zeros((north, rows), jnp.float32)
         for b in range(half_deg // block):
             def step(acc, p=p, b=b):
                 table = leg_ref[p, 0, :, b * block : (b + 1) * block]
@@ -102,14 +102,12 @@
                 kept = jnp.where(
                     degree >= mode, gain_ref[p, :, b * block : (b + 1) * block] * coef, 0.0
                 ).astype(jnp.bfloat16)
-                return acc + lax.dot_general(
-                    kept, table, (((1,), (1,)), ((), ())), preferred_element_type=jnp.float32
-                )
+                return acc + jnp.dot(table, kept.T, preferred_element_type=jnp.float32)
             top = 2 * ((b + 1) * block - 1) + p
             acc = lax.cond(top >= mode, step, lambda a: a, acc)
         syn.append(acc)
-    out_ref[0, 0] = (syn[0] + syn[1]).astype(out_ref.dtype)
-    out_ref[0, 1] = (syn[0] - syn[1]).astype(out_ref.dtype)
+    out_ref[0, 0] = (syn[0] + syn[1]).T.astype(out_ref.dtype)
+    out_ref[0, 1] = (syn[0] - syn[1]).T.astype(out_ref.dtype)
 
 
 def legendre_stage(folded, legendre, gain_rows, own_modes, base, block=256):

time: 127 us -> 130 us (1.024)
  Pallas kernels: 21.8 us -> 25 us
    pallas_call x1, Pallas kernels: 13.1 us -> 16.2 us  [legendre_stage(): pl.pallas_call(functools.partial(legendre_kernel, block=block), grid_spec...]
where the time goes in v5:
time: 130 us; the launch traced here: 129 us
  blocking collectives  26 us (20%)
  Pallas kernels  25 us (19%)
  other arithmetic  22.7 us (17%)
  starting transfers between devices  20.7 us (16%)
  waiting for transfers between devices  17 us (13%)
  local copies, waits for them, and re-layouts  8.99 us (7%)
  matrix products  8.66 us (7%)
    all_gather x1, blocking collectives, local(): all_gain = lax.all_gather(spectral_gain, 'chan', axis=0, tiled=True)  26 us
    all_to_all x1, waiting for transfers between devices, local(): returned = lax.all_to_all(leaving, ('chan', 'lat'), 0, 0, tiled=True)  17 us
    pallas_call x1, Pallas kernels, legendre_stage(): pl.pallas_call(functools.partial(legendre_kernel, block=block), grid_spec...  16.2 us
    all_to_all x1, starting transfers between devices, local(): got = lax.all_to_all(sent, ('chan', 'lat'), 0, 0, tiled=True)  11.1 us
    all_to_all x1, starting transfers between devices, local(): returned = lax.all_to_all(leaving, ('chan', 'lat'), 0, 0, tiled=True)  9.52 us
    convert_element_type x1, other arithmetic, local(): initial = flat[:, :, :, n * period:(n + 1) * period].astype(jnp.float32)  7.23 us
    pallas_call x1, Pallas kernels, local(): pl.pallas_call(functools.partial(gather_kernel, piece=piece, per_dev=per_...  5.01 us
    dot_general x1, matrix products, local(): lax.dot_general(jnp.concatenate([fwd, fwd], axis=1), rows, (((1,), (1,)),...  4.61 us
  transfers between devices with their start and end apart: 2, of which 1 were waited for; matrix products, arithmetic and copies ran while one was open for 7% of the time, Pallas kernels for 0%

profile of v5, /device:TPU:0, one launch (start us, length us, event | category | flops | bytes accessed | tf_op | source)
XLA Modules:
  0.0 129.3 jit_solution(6436776026503669211)
XLA Ops:
  0.0 0.7 broadcast_multiply_fusion.1
  1.2 2.4 %fusion.32 = (f32[128,4,128]{2,1,0:T(4,128)S(1)}, f32[128,4,128]{2,1,0:T(4,128)S(1)}) fusion(s32[128,4]{1,0:T(8,128)S(1)} %copy.28), kind=kLoop, calls=%fused_computation.49 | loop fusion | flops 917504 | bytes 526336 | tf_op jit(solution)/shard_map/cos | solution.py:166
  4.4 2.5 %multiply_convert_fusion = bf16[128,2,4,8,128]{4,3,2,1,0:T(8,128)(2,1)S(1)} fusion(f32[128,4,128]{2,1,0:T(4,128)S(1)} %get-tuple-element.21, f32[128,2,4,8]{3,2,1,0:T(4,128)S(1)} %copy.29, f32[128,4,128]{2,1,0:T(4,128)S(1)} %get-tuple-element.20, f32[128,2,4,8]{3,2,1,0:T(4,128)S(1)} %copy.27), kind=kLoop, calls=%fused_computation.5 | loop fusion | flops 5242880 | bytes 2686976 | tf_op jit(solution)/shard_map/convert_element_type | solution.py:168
  6.9 0.6 copy.45
  7.5 0.8 copy.30
  8.3 1.6 %subtract_convert_fusion = (bf16[768,1024]{1,0:T(8,128)(2,1)S(1)}, bf16[768,1024]{1,0:T(8,128)(2,1)S(1)}) fusion(bf16[768,4096]{1,0:T(8,128)(2,1)S(1)} %bitcast.61), kind=kLoop, calls=%fused_computation.9 | loop fusion | flops 8650752 | bytes 9437184 | tf_op jit(solution)/shard_map/convert_element_type | solution.py:182
  9.9 4.6 %fusion.17 = bf16[128,8,768]{2,1,0:T(8,128)(2,1)} fusion(bf16[768,1024]{1,0:T(8,128)(2,1)S(1)} %get-tuple-element.5, bf16[768,1024]{1,0:T(8,128)(2,1)S(1)} %get-tuple-element.6, bf16[1024,1024]{1,0:T(8,128)(2,1)S(1)} %bitcast.67), kind=kOutput, calls=%fused_computation.29 | convolution fusion | flops 3236691968 | bytes 6815744 | tf_op jit(solution)/shard_map/dot_general | solution.py:184
  14.5 11.1 %all-to-all-start = ((bf16[128,8,768]{2,1,0:T(8,128)(2,1)}), bf16[128,8,768]{2,1,0:T(8,128)(2,1)S(1)}, u32[]{:S(2)}, u32[]{:S(2)}) async-start(bf16[128,8,768]{2,1,0:T(8,128)(2,1)} %fusion.17), calls=%async_computation | async-start | bytes 3145728 | tf_op jit(solution)/shard_map/all_to_all | solution.py:190
  26.2 26.0 %all_gather.3 = f32[32,2048]{1,0:T(8,128)S(1)} all-gather(f32[8,2048]{1,0:T(8,128)S(1)} %copy-done.5), channel_id=1, replica_groups=mesh['lat'=32,'chan'=4] {'chan'}, dimensions={0}, use_global_device_ids=true | all-gather | bytes 327680 | tf_op jit(solution)/shard_map/all_gather | solution.py:206
  52.5 0.4 copy.35
  53.4 5.0 %shard_map.73 = bf16[4,2,3,2,32,512]{5,4,3,2,1,0:T(8,128)(2,1)S(1)} custom-call(bf16[4,8,32,768]{3,2,1,0:T(8,128)(2,1)S(1)} %bitcast.59, bf16[64,64]{1,0:T(8,128)(2,1)S(1)} %copy.33.mix_ref), custom_call_target="tpu_custom_call" | custom-call | tf_op jit(solution)/shard_map/pallas_call | solution.py:197
  58.6 16.2 %shard_map.74.back_ref = bf16[4,2,192,512]{3,2,1,0:T(8,128)(2,1)S(1)} custom-call(s32[4]{0:T(128)S(1)} %dynamic_slice.3.modes_ref, s32[1]{0:T(128)} %bitcast.2.base_ref, bf16[4,2,192,512]{3,2,1,0:T(8,128)(2,1)S(1)} %bitcast.57, bf16[2,16,512,1024]{3,2,1,0:T(8,128)(2,1)} %leg_ref.1, f32[2,192,1024]{2,1,0:T(8,128)S(1)} %bitcast.58), custom_call_target="tpu_custom_call" | custom-call | flops 3221225472 | bytes 13107200 | tf_op jit(solution)/shard_map/pallas_call | solution.py:127
  74.9 3.8 %shard_map.75 = bf16[4,8,32,768]{3,2,1,0:T(8,128)(2,1)S(1)} custom-call(bf16[4,2,192,512]{3,2,1,0:T(8,128)(2,1)S(1)} %shard_map.74.back_ref), custom_call_target="tpu_custom_call" | custom-call | tf_op jit(solution)/shard_map/pallas_call | solution.py:217
  78.6 2.0 %copy.36 = bf16[4,32,8,768]{3,2,1,0:T(8,128)(2,1)} copy(bf16[4,32,8,768]{3,1,2,0:T(8,128)(2,1)S(1)} %bitcast.60) | data formatting | bytes 3145728 | tf_op jit(solution)/shard_map/transpose | solution.py:222
  80.7 9.5 %all-to-all-start.1 = ((bf16[128,8,768]{2,1,0:T(8,128)(2,1)}), bf16[128,8,768]{2,1,0:T(8,128)(2,1)}, u32[]{:S(2)}, u32[]{:S(2)}) async-start(bf16[128,8,768]{2,1,0:T(8,128)(2,1)} %bitcast.15), calls=%async_computation.1 | async-start | bytes 3145728 | tf_op jit(solution)/shard_map/all_to_all | solution.py:223
  90.2 7.2 %slice_convert_fusion.3 = (f32[8,3,32,1024]{3,2,1,0:T(8,128)S(1)}, f32[8,3,32,1024]{3,2,1,0:T(8,128)}, f32[8,3,32,1024]{3,2,1,0:T(8,128)}, f32[8,3,32,1024]{3,2,1,0:T(8,128)}) fusion(bf16[8,3,32,4096]{3,2,1,0:T(8,128)(2,1)} %bitcast.62), kind=kLoop, calls=%fused_computation.26 | loop fusion | flops 3145728 | bytes 18874368 | tf_op jit(solution)/shard_map/convert_element_type | solution.py:238
  97.4 17.0 %all-to-all-done.1 = bf16[128,8,768]{2,1,0:T(8,128)(2,1)} async-done(((bf16[128,8,768]{2,1,0:T(8,128)(2,1)}), bf16[128,8,768]{2,1,0:T(8,128)(2,1)}, u32[]{:S(2)}, u32[]{:S(2)}) %all-to-all-start.1) | async-done | bytes 1572896 | tf_op jit(solution)/shard_map/all_to_all | solution.py:223
  114.4 4.1 %convolution_multiply_fusion = f32[768,1024]{1,0:T(8,128)S(1)} fusion(bf16[1024,1024]{1,0:T(8,128)(2,1)} %bitcast.68, bf16[128,8,768]{2,1,0:T(8,128)(2,1)} %all-to-all-done.1), kind=kOutput, calls=%fused_computation.21 | convolution fusion | flops 1611399168 | bytes 6815744 | tf_op jit(solution)/shard_map/dot_general | solution.py:226
  118.5 0.4 copy.37
  118.9 1.5 %copy-done.1 = f32[8,3,32,1024]{3,2,1,0:T(8,128)S(1)} copy-done((f32[8,3,32,1024]{3,2,1,0:T(8,128)S(1)}, f32[8,3,32,1024]{3,2,1,0:T(8,128)}, u32[]{:S(2)}) %copy-start.1) | copy-done | bytes 3145752
  120.4 1.0 copy-done.2
  121.3 1.7 %fusion.25 = (bf16[8,1,32,1024]{3,2,1,0:T(8,128)(2,1)S(1)}, bf16[8,1,32,1024]{3,2,1,0:T(8,128)(2,1)S(1)}, bf16[8,1,32,1024]{3,2,1,0:T(8,128)(2,1)}, bf16[8,1,32,1024]{3,2,1,0:T(8,128)(2,1)}, f32[8,32,1024]{2,1,0:T(8,128)S(1)}) fusion(f32[8,3,32,1024]{3,2,1,0:T(8,128)S(1)} %get-tuple-element.7, f32[8,3,32,1024]{3,2,1,0:T(8,128)S(1)} %bitcast.63, ...), kind=kLoop, calls=%fused_computation.37 | loop fusion | flops 4194304 | bytes 8388608 | tf_op jit(solution)/shard_map/convert.16
  123.1 1.7 %fusion.10 = (bf16[8,2,32,1024]{3,2,1,0:T(8,128)(2,1)S(1)}, bf16[8,2,32,1024]{3,2,1,0:T(8,128)(2,1)S(1)}, bf16[8,2,32,1024]{3,2,1,0:T(8,128)(2,1)S(1)}, bf16[8,2,32,1024]{3,2,1,0:T(8,128)(2,1)S(1)}) fusion(f32[8,3,32,1024]{3,2,1,0:T(8,128)S(1)} %get-tuple-element.7, f32[8,3,32,1024]{3,2,1,0:T(8,128)S(1)} %bitcast.64, ...), kind=kLoop, calls=%fused_computation.20 | loop fusion | flops 4718592 | bytes 15728640 | tf_op jit(solution)/shard_map/convert.15
  124.7 4.6 %maximum_maximum_fusion = bf16[8,3,2,16,4096]{4,3,2,1,0:T(8,128)(2,1)} fusion(bf16[8,2,2,16,1024]{4,3,2,1,0:T(8,128)(2,1)S(1)} %bitcast.74, bf16[8,1,2,16,1024]{4,3,2,1,0:T(8,128)(2,1)} %bitcast.78, bf16[8,2,2,16,1024]{4,3,2,1,0:T(8,128)(2,1)S(1)} %bitcast.73, bf16[8,1,2,16,1024]{4,3,2,1,0:T(8,128)(2,1)} %bitcast.77, ...), kind=kLoop, calls=%fused_computation | loop fusion | flops 50331648 | bytes 12582912 | tf_op jit(solution)/shard_map/concatenate | solution.py:242
  (36 shorter events, 2.7 us)
Async XLA Ops:
  4.4 3.1 %copy-start = (bf16[8,3,2,16,4096]{4,3,2,1,0:T(8,128)(2,1)S(1)}, bf16[8,3,2,16,4096]{4,3,2,1,0:T(8,128)(2,1)}, u32[]{:S(2)}) copy-start(bf16[8,3,2,16,4096]{4,3,2,1,0:T(8,128)(2,1)} %param.7) | copy-start | bytes 18874372
  7.5 2.4 %copy-start.4 = (bf16[128,8,8,128]{3,1,2,0:T(8,128)(2,1)}, bf16[128,8,8,128]{3,1,2,0:T(8,128)(2,1)S(1)}, u32[]{:S(2)}) copy-start(bf16[128,8,8,128]{3,1,2,0:T(8,128)(2,1)S(1)} %copy.45) | copy-start | bytes 6291460
  14.5 11.2 %copy-start.6 = (bf16[32,32]{1,0:T(8,128)(2,1)S(1)}, bf16[32,32]{1,0:T(8,128)(2,1)}, u32[]{:S(2)}) copy-start(bf16[32,32]{1,0:T(8,128)(2,1)} %param.8) | copy-start | bytes 6148
  14.5 11.3 %copy-start.7 = (f32[2,2]{0,1:T(2,128)S(1)}, f32[2,2]{0,1:T(2,128)}, u32[]{:S(2)}) copy-start(f32[2,2]{0,1:T(2,128)} %constant.57.clone) | copy-start | bytes 52
  14.5 11.7 %copy-start.5 = (f32[8,2048]{1,0:T(8,128)S(1)}, f32[8,2048]{1,0:T(8,128)}, u32[]{:S(2)}) copy-start(f32[8,2048]{1,0:T(8,128)} %param.9) | copy-start | bytes 196612
  14.5 38.6 %all-to-all-start = ((bf16[128,8,768]{2,1,0:T(8,128)(2,1)}), bf16[128,8,768]{2,1,0:T(8,128)(2,1)S(1)}, u32[]{:S(2)}, u32[]{:S(2)}) async-start(bf16[128,8,768]{2,1,0:T(8,128)(2,1)} %fusion.17), calls=%async_computation | async-start | bytes 3145728 | tf_op jit(solution)/shard_map/all_to_all | solution.py:190
  80.7 33.7 %all-to-all-start.1 = ((bf16[128,8,768]{2,1,0:T(8,128)(2,1)}), bf16[128,8,768]{2,1,0:T(8,128)(2,1)}, u32[]{:S(2)}, u32[]{:S(2)}) async-start(bf16[128,8,768]{2,1,0:T(8,128)(2,1)} %bitcast.15), calls=%async_computation.1 | async-start | bytes 3145728 | tf_op jit(solution)/shard_map/all_to_all | solution.py:223
  114.4 4.5 %copy-start.3 = (f32[8,3,32,1024]{3,2,1,0:T(8,128)S(1)}, f32[8,3,32,1024]{3,2,1,0:T(8,128)}, u32[]{:S(2)}) copy-start(f32[8,3,32,1024]{3,2,1,0:T(8,128)} %get-tuple-element.10) | copy-start | bytes 9437188
  118.5 1.9 %copy-start.1 = (f32[8,3,32,1024]{3,2,1,0:T(8,128)S(1)}, f32[8,3,32,1024]{3,2,1,0:T(8,128)}, u32[]{:S(2)}) copy-start(f32[8,3,32,1024]{3,2,1,0:T(8,128)} %get-tuple-element.8) | copy-start | bytes 9437188
  118.5 2.8 %copy-start.2 = (f32[8,3,32,1024]{3,2,1,0:T(8,128)S(1)}, f32[8,3,32,1024]{3,2,1,0:T(8,128)}, u32[]{:S(2)}) copy-start(f32[8,3,32,1024]{3,2,1,0:T(8,128)} %get-tuple-element.9) | copy-start | bytes 9437188

commit v6 on v4

--- a/solution.py
+++ b/solution.py
@@ -112,7 +112,7 @@
     out_ref[0, 1] = (syn[0] - syn[1]).astype(out_ref.dtype)
 
 
-def legendre_stage(folded, legendre, gain_rows, own_modes, base, block=256):
+def legendre_stage(folded, legendre, gain_rows, own_modes, base, block=512):
     per_dev, _, rows, north = folded.shape
     half_deg = legendre.shape[-1]
     grid_spec = pltpu.PrefetchScalarGridSpec(

time: 127 us -> 123 us (0.969)
  Pallas kernels: 21.8 us -> 18.3 us
    pallas_call x1, Pallas kernels: 13.1 us -> 9.5 us  [legendre_stage(): pl.pallas_call(functools.partial(legendre_kernel, block=block), grid_spec...]
where the time goes in v6:
time: 123 us; the launch traced here: 122 us
  blocking collectives  26 us (21%)
  other arithmetic  22.7 us (18%)
  starting transfers between devices  20.3 us (17%)
  Pallas kernels  18.3 us (15%)
  waiting for transfers between devices  17.2 us (14%)
  local copies, waits for them, and re-layouts  8.99 us (7%)
  matrix products  8.66 us (7%)
    all_gather x1, blocking collectives, local(): all_gain = lax.all_gather(spectral_gain, 'chan', axis=0, tiled=True)  26 us
    all_to_all x1, waiting for transfers between devices, local(): returned = lax.all_to_all(leaving, ('chan', 'lat'), 0, 0, tiled=True)  17.2 us
    all_to_all x1, starting transfers between devices, local(): got = lax.all_to_all(sent, ('chan', 'lat'), 0, 0, tiled=True)  11.1 us
    pallas_call x1, Pallas kernels, legendre_stage(): pl.pallas_call(functools.partial(legendre_kernel, block=block), grid_spec...  9.5 us
    all_to_all x1, starting transfers between devices, local(): returned = lax.all_to_all(leaving, ('chan', 'lat'), 0, 0, tiled=True)  9.13 us
    convert_element_type x1, other arithmetic, local(): initial = flat[:, :, :, n * period:(n + 1) * period].astype(jnp.float32)  7.23 us
    pallas_call x1, Pallas kernels, local(): pl.pallas_call(functools.partial(gather_kernel, piece=piece, per_dev=per_...  5.01 us
    dot_general x1, matrix products, local(): lax.dot_general(jnp.concatenate([fwd, fwd], axis=1), rows, (((1,), (1,)),...  4.61 us
  transfers between devices with their start and end apart: 2, of which 1 were waited for; matrix products, arithmetic and copies ran while one was open for 7% of the time, Pallas kernels for 0%

profile of v6, /device:TPU:0, one launch (start us, length us, event | category | flops | bytes accessed | tf_op | source)
XLA Modules:
  0.0 122.4 jit_solution(4737446056506357263)
XLA Ops:
  0.0 0.7 broadcast_multiply_fusion.1
  1.2 2.4 %fusion.32 = (f32[128,4,128]{2,1,0:T(4,128)S(1)}, f32[128,4,128]{2,1,0:T(4,128)S(1)}) fusion(s32[128,4]{1,0:T(8,128)S(1)} %copy.28), kind=kLoop, calls=%fused_computation.49 | loop fusion | flops 917504 | bytes 526336 | tf_op jit(solution)/shard_map/cos | solution.py:168
  4.4 2.5 %multiply_convert_fusion = bf16[128,2,4,8,128]{4,3,2,1,0:T(8,128)(2,1)S(1)} fusion(f32[128,4,128]{2,1,0:T(4,128)S(1)} %get-tuple-element.21, f32[128,2,4,8]{3,2,1,0:T(4,128)S(1)} %copy.29, f32[128,4,128]{2,1,0:T(4,128)S(1)} %get-tuple-element.20, f32[128,2,4,8]{3,2,1,0:T(4,128)S(1)} %copy.27), kind=kLoop, calls=%fused_computation.5 | loop fusion | flops 5242880 | bytes 2686976 | tf_op jit(solution)/shard_map/convert_element_type | solution.py:170
  6.9 0.6 copy.45
  7.5 0.8 copy.30
  8.3 1.6 %subtract_convert_fusion = (bf16[768,1024]{1,0:T(8,128)(2,1)S(1)}, bf16[768,1024]{1,0:T(8,128)(2,1)S(1)}) fusion(bf16[768,4096]{1,0:T(8,128)(2,1)S(1)} %bitcast.61), kind=kLoop, calls=%fused_computation.9 | loop fusion | flops 8650752 | bytes 9437184 | tf_op jit(solution)/shard_map/convert_element_type | solution.py:184
  9.9 4.6 %fusion.17 = bf16[128,8,768]{2,1,0:T(8,128)(2,1)} fusion(bf16[768,1024]{1,0:T(8,128)(2,1)S(1)} %get-tuple-element.5, bf16[768,1024]{1,0:T(8,128)(2,1)S(1)} %get-tuple-element.6, bf16[1024,1024]{1,0:T(8,128)(2,1)S(1)} %bitcast.67), kind=kOutput, calls=%fused_computation.29 | convolution fusion | flops 3236691968 | bytes 6815744 | tf_op jit(solution)/shard_map/dot_general | solution.py:186
  14.5 11.1 %all-to-all-start = ((bf16[128,8,768]{2,1,0:T(8,128)(2,1)}), bf16[128,8,768]{2,1,0:T(8,128)(2,1)S(1)}, u32[]{:S(2)}, u32[]{:S(2)}) async-start(bf16[128,8,768]{2,1,0:T(8,128)(2,1)} %fusion.17), calls=%async_computation | async-start | bytes 3145728 | tf_op jit(solution)/shard_map/all_to_all | solution.py:192
  26.2 26.0 %all_gather.3 = f32[32,2048]{1,0:T(8,128)S(1)} all-gather(f32[8,2048]{1,0:T(8,128)S(1)} %copy-done.5), channel_id=1, replica_groups=mesh['lat'=32,'chan'=4] {'chan'}, dimensions={0}, use_global_device_ids=true | all-gather | bytes 327680 | tf_op jit(solution)/shard_map/all_gather | solution.py:208
  52.5 0.4 copy.35
  53.4 5.0 %shard_map.73 = bf16[4,2,3,2,32,512]{5,4,3,2,1,0:T(8,128)(2,1)S(1)} custom-call(bf16[4,8,32,768]{3,2,1,0:T(8,128)(2,1)S(1)} %bitcast.59, bf16[64,64]{1,0:T(8,128)(2,1)S(1)} %copy.33.mix_ref), custom_call_target="tpu_custom_call" | custom-call | tf_op jit(solution)/shard_map/pallas_call | solution.py:199
  58.6 9.5 %shard_map.74.back_ref = bf16[4,2,192,512]{3,2,1,0:T(8,128)(2,1)S(1)} custom-call(s32[4]{0:T(128)S(1)} %dynamic_slice.3.modes_ref, s32[1]{0:T(128)} %bitcast.2.base_ref, bf16[4,2,192,512]{3,2,1,0:T(8,128)(2,1)S(1)} %bitcast.57, bf16[2,16,512,1024]{3,2,1,0:T(8,128)(2,1)} %leg_ref.1, f32[2,192,1024]{2,1,0:T(8,128)S(1)} %bitcast.58), custom_call_target="tpu_custom_call" | custom-call | flops 3221225472 | bytes 13107200 | tf_op jit(solution)/shard_map/pallas_call | solution.py:129
  68.1 3.8 %shard_map.75 = bf16[4,8,32,768]{3,2,1,0:T(8,128)(2,1)S(1)} custom-call(bf16[4,2,192,512]{3,2,1,0:T(8,128)(2,1)S(1)} %shard_map.74.back_ref), custom_call_target="tpu_custom_call" | custom-call | tf_op jit(solution)/shard_map/pallas_call | solution.py:219
  71.9 2.0 %copy.36 = bf16[4,32,8,768]{3,2,1,0:T(8,128)(2,1)} copy(bf16[4,32,8,768]{3,1,2,0:T(8,128)(2,1)S(1)} %bitcast.60) | data formatting | bytes 3145728 | tf_op jit(solution)/shard_map/transpose | solution.py:224
  73.9 9.1 %all-to-all-start.1 = ((bf16[128,8,768]{2,1,0:T(8,128)(2,1)}), bf16[128,8,768]{2,1,0:T(8,128)(2,1)}, u32[]{:S(2)}, u32[]{:S(2)}) async-start(bf16[128,8,768]{2,1,0:T(8,128)(2,1)} %bitcast.15), calls=%async_computation.1 | async-start | bytes 3145728 | tf_op jit(solution)/shard_map/all_to_all | solution.py:225
  83.1 7.2 %slice_convert_fusion.3 = (f32[8,3,32,1024]{3,2,1,0:T(8,128)S(1)}, f32[8,3,32,1024]{3,2,1,0:T(8,128)}, f32[8,3,32,1024]{3,2,1,0:T(8,128)}, f32[8,3,32,1024]{3,2,1,0:T(8,128)}) fusion(bf16[8,3,32,4096]{3,2,1,0:T(8,128)(2,1)} %bitcast.62), kind=kLoop, calls=%fused_computation.26 | loop fusion | flops 3145728 | bytes 18874368 | tf_op jit(solution)/shard_map/convert_element_type | solution.py:240
  90.3 17.2 %all-to-all-done.1 = bf16[128,8,768]{2,1,0:T(8,128)(2,1)} async-done(((bf16[128,8,768]{2,1,0:T(8,128)(2,1)}), bf16[128,8,768]{2,1,0:T(8,128)(2,1)}, u32[]{:S(2)}, u32[]{:S(2)}) %all-to-all-start.1) | async-done | bytes 1572896 | tf_op jit(solution)/shard_map/all_to_all | solution.py:225
  107.5 4.1 %convolution_multiply_fusion = f32[768,1024]{1,0:T(8,128)S(1)} fusion(bf16[1024,1024]{1,0:T(8,128)(2,1)} %bitcast.68, bf16[128,8,768]{2,1,0:T(8,128)(2,1)} %all-to-all-done.1), kind=kOutput, calls=%fused_computation.21 | convolution fusion | flops 1611399168 | bytes 6815744 | tf_op jit(solution)/shard_map/dot_general | solution.py:228
  111.6 0.4 copy.37
  112.0 1.5 %copy-done.1 = f32[8,3,32,1024]{3,2,1,0:T(8,128)S(1)} copy-done((f32[8,3,32,1024]{3,2,1,0:T(8,128)S(1)}, f32[8,3,32,1024]{3,2,1,0:T(8,128)}, u32[]{:S(2)}) %copy-start.1) | copy-done | bytes 3145752
  113.5 1.0 copy-done.2
  114.4 1.7 %fusion.25 = (bf16[8,1,32,1024]{3,2,1,0:T(8,128)(2,1)S(1)}, bf16[8,1,32,1024]{3,2,1,0:T(8,128)(2,1)S(1)}, bf16[8,1,32,1024]{3,2,1,0:T(8,128)(2,1)}, bf16[8,1,32,1024]{3,2,1,0:T(8,128)(2,1)}, f32[8,32,1024]{2,1,0:T(8,128)S(1)}) fusion(f32[8,3,32,1024]{3,2,1,0:T(8,128)S(1)} %get-tuple-element.7, f32[8,3,32,1024]{3,2,1,0:T(8,128)S(1)} %bitcast.63, ...), kind=kLoop, calls=%fused_computation.37 | loop fusion | flops 4194304 | bytes 8388608 | tf_op jit(solution)/shard_map/convert.16
  116.1 1.7 %fusion.10 = (bf16[8,2,32,1024]{3,2,1,0:T(8,128)(2,1)S(1)}, bf16[8,2,32,1024]{3,2,1,0:T(8,128)(2,1)S(1)}, bf16[8,2,32,1024]{3,2,1,0:T(8,128)(2,1)S(1)}, bf16[8,2,32,1024]{3,2,1,0:T(8,128)(2,1)S(1)}) fusion(f32[8,3,32,1024]{3,2,1,0:T(8,128)S(1)} %get-tuple-element.7, f32[8,3,32,1024]{3,2,1,0:T(8,128)S(1)} %bitcast.64, ...), kind=kLoop, calls=%fused_computation.20 | loop fusion | flops 4718592 | bytes 15728640 | tf_op jit(solution)/shard_map/convert.15
  117.8 4.6 %maximum_maximum_fusion = bf16[8,3,2,16,4096]{4,3,2,1,0:T(8,128)(2,1)} fusion(bf16[8,2,2,16,1024]{4,3,2,1,0:T(8,128)(2,1)S(1)} %bitcast.74, bf16[8,1,2,16,1024]{4,3,2,1,0:T(8,128)(2,1)} %bitcast.78, bf16[8,2,2,16,1024]{4,3,2,1,0:T(8,128)(2,1)S(1)} %bitcast.73, bf16[8,1,2,16,1024]{4,3,2,1,0:T(8,128)(2,1)} %bitcast.77, ...), kind=kLoop, calls=%fused_computation | loop fusion | flops 50331648 | bytes 12582912 | tf_op jit(solution)/shard_map/concatenate | solution.py:244
  (36 shorter events, 2.7 us)
Async XLA Ops:
  4.4 3.1 %copy-start = (bf16[8,3,2,16,4096]{4,3,2,1,0:T(8,128)(2,1)S(1)}, bf16[8,3,2,16,4096]{4,3,2,1,0:T(8,128)(2,1)}, u32[]{:S(2)}) copy-start(bf16[8,3,2,16,4096]{4,3,2,1,0:T(8,128)(2,1)} %param.7) | copy-start | bytes 18874372
  7.5 2.4 %copy-start.4 = (bf16[128,8,8,128]{3,1,2,0:T(8,128)(2,1)}, bf16[128,8,8,128]{3,1,2,0:T(8,128)(2,1)S(1)}, u32[]{:S(2)}) copy-start(bf16[128,8,8,128]{3,1,2,0:T(8,128)(2,1)S(1)} %copy.45) | copy-start | bytes 6291460
  14.5 11.2 %copy-start.6 = (bf16[32,32]{1,0:T(8,128)(2,1)S(1)}, bf16[32,32]{1,0:T(8,128)(2,1)}, u32[]{:S(2)}) copy-start(bf16[32,32]{1,0:T(8,128)(2,1)} %param.8) | copy-start | bytes 6148
  14.5 11.3 %copy-start.7 = (f32[2,2]{0,1:T(2,128)S(1)}, f32[2,2]{0,1:T(2,128)}, u32[]{:S(2)}) copy-start(f32[2,2]{0,1:T(2,128)} %constant.57.clone) | copy-start | bytes 52
  14.5 11.7 %copy-start.5 = (f32[8,2048]{1,0:T(8,128)S(1)}, f32[8,2048]{1,0:T(8,128)}, u32[]{:S(2)}) copy-start(f32[8,2048]{1,0:T(8,128)} %param.9) | copy-start | bytes 196612
  14.5 38.6 %all-to-all-start = ((bf16[128,8,768]{2,1,0:T(8,128)(2,1)}), bf16[128,8,768]{2,1,0:T(8,128)(2,1)S(1)}, u32[]{:S(2)}, u32[]{:S(2)}) async-start(bf16[128,8,768]{2,1,0:T(8,128)(2,1)} %fusion.17), calls=%async_computation | async-start | bytes 3145728 | tf_op jit(solution)/shard_map/all_to_all | solution.py:192
  73.9 33.6 %all-to-all-start.1 = ((bf16[128,8,768]{2,1,0:T(8,128)(2,1)}), bf16[128,8,768]{2,1,0:T(8,128)(2,1)}, u32[]{:S(2)}, u32[]{:S(2)}) async-start(bf16[128,8,768]{2,1,0:T(8,128)(2,1)} %bitcast.15), calls=%async_computation.1 | async-start | bytes 3145728 | tf_op jit(solution)/shard_map/all_to_all | solution.py:225
  107.5 4.5 %copy-start.3 = (f32[8,3,32,1024]{3,2,1,0:T(8,128)S(1)}, f32[8,3,32,1024]{3,2,1,0:T(8,128)}, u32[]{:S(2)}) copy-start(f32[8,3,32,1024]{3,2,1,0:T(8,128)} %get-tuple-element.10) | copy-start | bytes 9437188
  111.6 1.9 %copy-start.1 = (f32[8,3,32,1024]{3,2,1,0:T(8,128)S(1)}, f32[8,3,32,1024]{3,2,1,0:T(8,128)}, u32[]{:S(2)}) copy-start(f32[8,3,32,1024]{3,2,1,0:T(8,128)} %get-tuple-element.8) | copy-start | bytes 9437188
  111.6 2.8 %copy-start.2 = (f32[8,3,32,1024]{3,2,1,0:T(8,128)S(1)}, f32[8,3,32,1024]{3,2,1,0:T(8,128)}, u32[]{:S(2)}) copy-start(f32[8,3,32,1024]{3,2,1,0:T(8,128)} %get-tuple-element.9) | copy-start | bytes 9437188

commit v7 on v6

--- a/solution.py
+++ b/solution.py
@@ -112,7 +112,7 @@
     out_ref[0, 1] = (syn[0] - syn[1]).astype(out_ref.dtype)
 
 
-def legendre_stage(folded, legendre, gain_rows, own_modes, base, block=512):
+def legendre_stage(folded, legendre, gain_rows, own_modes, base, block=1024):
     per_dev, _, rows, north = folded.shape
     half_deg = legendre.shape[-1]
     grid_spec = pltpu.PrefetchScalarGridSpec(

time: 123 us -> 122 us (level)
  no operation moved by 1% of the time
where the time goes in v7:
time: 122 us
  blocking collectives  26 us (21%)
  other arithmetic  22.7 us (19%)
  starting transfers between devices  20.4 us (17%)
  Pallas kernels  17.4 us (14%)
  waiting for transfers between devices  17.2 us (14%)
  local copies, waits for them, and re-layouts  8.99 us (7%)
  matrix products  8.66 us (7%)
    all_gather x1, blocking collectives, local(): all_gain = lax.all_gather(spectral_gain, 'chan', axis=0, tiled=True)  26 us
    all_to_all x1, waiting for transfers between devices, local(): returned = lax.all_to_all(leaving, ('chan', 'lat'), 0, 0, tiled=True)  17.2 us
    all_to_all x1, starting transfers between devices, local(): got = lax.all_to_all(sent, ('chan', 'lat'), 0, 0, tiled=True)  11.1 us
    all_to_all x1, starting transfers between devices, local(): returned = lax.all_to_all(leaving, ('chan', 'lat'), 0, 0, tiled=True)  9.31 us
    pallas_call x1, Pallas kernels, legendre_stage(): pl.pallas_call(functools.partial(legendre_kernel, block=block), grid_spec...  8.62 us
    convert_element_type x1, other arithmetic, local(): initial = flat[:, :, :, n * period:(n + 1) * period].astype(jnp.float32)  7.23 us
    pallas_call x1, Pallas kernels, local(): pl.pallas_call(functools.partial(gather_kernel, piece=piece, per_dev=per_...  5.01 us
    dot_general x1, matrix products, local(): lax.dot_general(jnp.concatenate([fwd, fwd], axis=1), rows, (((1,), (1,)),...  4.61 us
  transfers between devices with their start and end apart: 2, of which 1 were waited for; matrix products, arithmetic and copies ran while one was open for 7% of the time, Pallas kernels for 0%

profile of v7, /device:TPU:0, one launch (start us, length us, event | category | flops | bytes accessed | tf_op | source)
XLA Modules:
  0.0 121.7 jit_solution(14734500448166759220)
XLA Ops:
  0.0 0.7 broadcast_multiply_fusion.1
  1.2 2.4 %fusion.32 = (f32[128,4,128]{2,1,0:T(4,128)S(1)}, f32[128,4,128]{2,1,0:T(4,128)S(1)}) fusion(s32[128,4]{1,0:T(8,128)S(1)} %copy.28), kind=kLoop, calls=%fused_computation.49 | loop fusion | flops 917504 | bytes 526336 | tf_op jit(solution)/shard_map/cos | solution.py:168
  4.4 2.5 %multiply_convert_fusion = bf16[128,2,4,8,128]{4,3,2,1,0:T(8,128)(2,1)S(1)} fusion(f32[128,4,128]{2,1,0:T(4,128)S(1)} %get-tuple-element.21, f32[128,2,4,8]{3,2,1,0:T(4,128)S(1)} %copy.29, f32[128,4,128]{2,1,0:T(4,128)S(1)} %get-tuple-element.20, f32[128,2,4,8]{3,2,1,0:T(4,128)S(1)} %copy.27), kind=kLoop, calls=%fused_computation.5 | loop fusion | flops 5242880 | bytes 2686976 | tf_op jit(solution)/shard_map/convert_element_type | solution.py:170
  6.9 0.6 copy.45
  7.5 0.8 copy.30
  8.3 1.6 %subtract_convert_fusion = (bf16[768,1024]{1,0:T(8,128)(2,1)S(1)}, bf16[768,1024]{1,0:T(8,128)(2,1)S(1)}) fusion(bf16[768,4096]{1,0:T(8,128)(2,1)S(1)} %bitcast.61), kind=kLoop, calls=%fused_computation.9 | loop fusion | flops 8650752 | bytes 9437184 | tf_op jit(solution)/shard_map/convert_element_type | solution.py:184
  9.9 4.6 %fusion.17 = bf16[128,8,768]{2,1,0:T(8,128)(2,1)} fusion(bf16[768,1024]{1,0:T(8,128)(2,1)S(1)} %get-tuple-element.5, bf16[768,1024]{1,0:T(8,128)(2,1)S(1)} %get-tuple-element.6, bf16[1024,1024]{1,0:T(8,128)(2,1)S(1)} %bitcast.67), kind=kOutput, calls=%fused_computation.29 | convolution fusion | flops 3236691968 | bytes 6815744 | tf_op jit(solution)/shard_map/dot_general | solution.py:186
  14.5 11.1 %all-to-all-start = ((bf16[128,8,768]{2,1,0:T(8,128)(2,1)}), bf16[128,8,768]{2,1,0:T(8,128)(2,1)S(1)}, u32[]{:S(2)}, u32[]{:S(2)}) async-start(bf16[128,8,768]{2,1,0:T(8,128)(2,1)} %fusion.17), calls=%async_computation | async-start | bytes 3145728 | tf_op jit(solution)/shard_map/all_to_all | solution.py:192
  26.2 26.0 %all_gather.3 = f32[32,2048]{1,0:T(8,128)S(1)} all-gather(f32[8,2048]{1,0:T(8,128)S(1)} %copy-done.5), channel_id=1, replica_groups=mesh['lat'=32,'chan'=4] {'chan'}, dimensions={0}, use_global_device_ids=true | all-gather | bytes 327680 | tf_op jit(solution)/shard_map/all_gather | solution.py:208
  52.5 0.4 copy.35
  53.4 5.0 %shard_map.73 = bf16[4,2,3,2,32,512]{5,4,3,2,1,0:T(8,128)(2,1)S(1)} custom-call(bf16[4,8,32,768]{3,2,1,0:T(8,128)(2,1)S(1)} %bitcast.59, bf16[64,64]{1,0:T(8,128)(2,1)S(1)} %copy.33.mix_ref), custom_call_target="tpu_custom_call" | custom-call | tf_op jit(solution)/shard_map/pallas_call | solution.py:199
  58.6 8.6 %shard_map.74.back_ref = bf16[4,2,192,512]{3,2,1,0:T(8,128)(2,1)S(1)} custom-call(s32[4]{0:T(128)S(1)} %dynamic_slice.3.modes_ref, s32[1]{0:T(128)} %bitcast.2.base_ref, bf16[4,2,192,512]{3,2,1,0:T(8,128)(2,1)S(1)} %bitcast.57, bf16[2,16,512,1024]{3,2,1,0:T(8,128)(2,1)} %leg_ref.1, f32[2,192,1024]{2,1,0:T(8,128)S(1)} %bitcast.58), custom_call_target="tpu_custom_call" | custom-call | flops 3221225472 | bytes 13107200 | tf_op jit(solution)/shard_map/pallas_call | solution.py:129
  67.2 3.8 %shard_map.75 = bf16[4,8,32,768]{3,2,1,0:T(8,128)(2,1)S(1)} custom-call(bf16[4,2,192,512]{3,2,1,0:T(8,128)(2,1)S(1)} %shard_map.74.back_ref), custom_call_target="tpu_custom_call" | custom-call | tf_op jit(solution)/shard_map/pallas_call | solution.py:219
  71.0 2.0 %copy.36 = bf16[4,32,8,768]{3,2,1,0:T(8,128)(2,1)} copy(bf16[4,32,8,768]{3,1,2,0:T(8,128)(2,1)S(1)} %bitcast.60) | data formatting | bytes 3145728 | tf_op jit(solution)/shard_map/transpose | solution.py:224
  73.1 9.3 %all-to-all-start.1 = ((bf16[128,8,768]{2,1,0:T(8,128)(2,1)}), bf16[128,8,768]{2,1,0:T(8,128)(2,1)}, u32[]{:S(2)}, u32[]{:S(2)}) async-start(bf16[128,8,768]{2,1,0:T(8,128)(2,1)} %bitcast.15), calls=%async_computation.1 | async-start | bytes 3145728 | tf_op jit(solution)/shard_map/all_to_all | solution.py:225
  82.4 7.2 %slice_convert_fusion.3 = (f32[8,3,32,1024]{3,2,1,0:T(8,128)S(1)}, f32[8,3,32,1024]{3,2,1,0:T(8,128)}, f32[8,3,32,1024]{3,2,1,0:T(8,128)}, f32[8,3,32,1024]{3,2,1,0:T(8,128)}) fusion(bf16[8,3,32,4096]{3,2,1,0:T(8,128)(2,1)} %bitcast.62), kind=kLoop, calls=%fused_computation.26 | loop fusion | flops 3145728 | bytes 18874368 | tf_op jit(solution)/shard_map/convert_element_type | solution.py:240
  89.6 17.2 %all-to-all-done.1 = bf16[128,8,768]{2,1,0:T(8,128)(2,1)} async-done(((bf16[128,8,768]{2,1,0:T(8,128)(2,1)}), bf16[128,8,768]{2,1,0:T(8,128)(2,1)}, u32[]{:S(2)}, u32[]{:S(2)}) %all-to-all-start.1) | async-done | bytes 1572896 | tf_op jit(solution)/shard_map/all_to_all | solution.py:225
  106.8 4.1 %convolution_multiply_fusion = f32[768,1024]{1,0:T(8,128)S(1)} fusion(bf16[1024,1024]{1,0:T(8,128)(2,1)} %bitcast.68, bf16[128,8,768]{2,1,0:T(8,128)(2,1)} %all-to-all-done.1), kind=kOutput, calls=%fused_computation.21 | convolution fusion | flops 1611399168 | bytes 6815744 | tf_op jit(solution)/shard_map/dot_general | solution.py:228
  110.9 0.4 copy.37
  111.3 1.5 %copy-done.1 = f32[8,3,32,1024]{3,2,1,0:T(8,128)S(1)} copy-done((f32[8,3,32,1024]{3,2,1,0:T(8,128)S(1)}, f32[8,3,32,1024]{3,2,1,0:T(8,128)}, u32[]{:S(2)}) %copy-start.1) | copy-done | bytes 3145752
  112.8 1.0 copy-done.2
  113.7 1.7 %fusion.25 = (bf16[8,1,32,1024]{3,2,1,0:T(8,128)(2,1)S(1)}, bf16[8,1,32,1024]{3,2,1,0:T(8,128)(2,1)S(1)}, bf16[8,1,32,1024]{3,2,1,0:T(8,128)(2,1)}, bf16[8,1,32,1024]{3,2,1,0:T(8,128)(2,1)}, f32[8,32,1024]{2,1,0:T(8,128)S(1)}) fusion(f32[8,3,32,1024]{3,2,1,0:T(8,128)S(1)} %get-tuple-element.7, f32[8,3,32,1024]{3,2,1,0:T(8,128)S(1)} %bitcast.63, ...), kind=kLoop, calls=%fused_computation.37 | loop fusion | flops 4194304 | bytes 8388608 | tf_op jit(solution)/shard_map/convert.16
  115.4 1.7 %fusion.10 = (bf16[8,2,32,1024]{3,2,1,0:T(8,128)(2,1)S(1)}, bf16[8,2,32,1024]{3,2,1,0:T(8,128)(2,1)S(1)}, bf16[8,2,32,1024]{3,2,1,0:T(8,128)(2,1)S(1)}, bf16[8,2,32,1024]{3,2,1,0:T(8,128)(2,1)S(1)}) fusion(f32[8,3,32,1024]{3,2,1,0:T(8,128)S(1)} %get-tuple-element.7, f32[8,3,32,1024]{3,2,1,0:T(8,128)S(1)} %bitcast.64, ...), kind=kLoop, calls=%fused_computation.20 | loop fusion | flops 4718592 | bytes 15728640 | tf_op jit(solution)/shard_map/convert.15
  117.1 4.6 %maximum_maximum_fusion = bf16[8,3,2,16,4096]{4,3,2,1,0:T(8,128)(2,1)} fusion(bf16[8,2,2,16,1024]{4,3,2,1,0:T(8,128)(2,1)S(1)} %bitcast.74, bf16[8,1,2,16,1024]{4,3,2,1,0:T(8,128)(2,1)} %bitcast.78, bf16[8,2,2,16,1024]{4,3,2,1,0:T(8,128)(2,1)S(1)} %bitcast.73, bf16[8,1,2,16,1024]{4,3,2,1,0:T(8,128)(2,1)} %bitcast.77, ...), kind=kLoop, calls=%fused_computation | loop fusion | flops 50331648 | bytes 12582912 | tf_op jit(solution)/shard_map/concatenate | solution.py:244
  (36 shorter events, 2.7 us)
Async XLA Ops:
  4.4 3.1 %copy-start = (bf16[8,3,2,16,4096]{4,3,2,1,0:T(8,128)(2,1)S(1)}, bf16[8,3,2,16,4096]{4,3,2,1,0:T(8,128)(2,1)}, u32[]{:S(2)}) copy-start(bf16[8,3,2,16,4096]{4,3,2,1,0:T(8,128)(2,1)} %param.7) | copy-start | bytes 18874372
  7.5 2.4 %copy-start.4 = (bf16[128,8,8,128]{3,1,2,0:T(8,128)(2,1)}, bf16[128,8,8,128]{3,1,2,0:T(8,128)(2,1)S(1)}, u32[]{:S(2)}) copy-start(bf16[128,8,8,128]{3,1,2,0:T(8,128)(2,1)S(1)} %copy.45) | copy-start | bytes 6291460
  14.5 11.2 %copy-start.6 = (bf16[32,32]{1,0:T(8,128)(2,1)S(1)}, bf16[32,32]{1,0:T(8,128)(2,1)}, u32[]{:S(2)}) copy-start(bf16[32,32]{1,0:T(8,128)(2,1)} %param.8) | copy-start | bytes 6148
  14.5 11.3 %copy-start.7 = (f32[2,2]{0,1:T(2,128)S(1)}, f32[2,2]{0,1:T(2,128)}, u32[]{:S(2)}) copy-start(f32[2,2]{0,1:T(2,128)} %constant.57.clone) | copy-start | bytes 52
  14.5 11.7 %copy-start.5 = (f32[8,2048]{1,0:T(8,128)S(1)}, f32[8,2048]{1,0:T(8,128)}, u32[]{:S(2)}) copy-start(f32[8,2048]{1,0:T(8,128)} %param.9) | copy-start | bytes 196612
  14.5 38.6 %all-to-all-start = ((bf16[128,8,768]{2,1,0:T(8,128)(2,1)}), bf16[128,8,768]{2,1,0:T(8,128)(2,1)S(1)}, u32[]{:S(2)}, u32[]{:S(2)}) async-start(bf16[128,8,768]{2,1,0:T(8,128)(2,1)} %fusion.17), calls=%async_computation | async-start | bytes 3145728 | tf_op jit(solution)/shard_map/all_to_all | solution.py:192
  73.1 33.7 %all-to-all-start.1 = ((bf16[128,8,768]{2,1,0:T(8,128)(2,1)}), bf16[128,8,768]{2,1,0:T(8,128)(2,1)}, u32[]{:S(2)}, u32[]{:S(2)}) async-start(bf16[128,8,768]{2,1,0:T(8,128)(2,1)} %bitcast.15), calls=%async_computation.1 | async-start | bytes 3145728 | tf_op jit(solution)/shard_map/all_to_all | solution.py:225
  106.8 4.5 %copy-start.3 = (f32[8,3,32,1024]{3,2,1,0:T(8,128)S(1)}, f32[8,3,32,1024]{3,2,1,0:T(8,128)}, u32[]{:S(2)}) copy-start(f32[8,3,32,1024]{3,2,1,0:T(8,128)} %get-tuple-element.10) | copy-start | bytes 9437188
  110.9 1.9 %copy-start.1 = (f32[8,3,32,1024]{3,2,1,0:T(8,128)S(1)}, f32[8,3,32,1024]{3,2,1,0:T(8,128)}, u32[]{:S(2)}) copy-start(f32[8,3,32,1024]{3,2,1,0:T(8,128)} %get-tuple-element.8) | copy-start | bytes 9437188
  110.9 2.8 %copy-start.2 = (f32[8,3,32,1024]{3,2,1,0:T(8,128)S(1)}, f32[8,3,32,1024]{3,2,1,0:T(8,128)}, u32[]{:S(2)}) copy-start(f32[8,3,32,1024]{3,2,1,0:T(8,128)} %get-tuple-element.9) | copy-start | bytes 9437188

commit v8 on v7

--- a/solution.py
+++ b/solution.py
@@ -82,6 +82,23 @@
         return carry
 
     lax.fori_loop(0, out_ref.shape[1], one, 0)
+
+
+def epilogue_kernel(wave_ref, field_ref, out_ref, *, period):
+    fields = wave_ref.shape[0]
+    primal_h = wave_ref[0, :, 0]
+    sigmoid_h = 1.0 / (1.0 + jnp.exp(-primal_h))
+    slope_h = sigmoid_h * (1.0 + primal_h * (1.0 - sigmoid_h))
+    gain_h = primal_h * sigmoid_h
+    for n in range(field_ref.shape[-1] // period):
+        cols = slice(n * period, (n + 1) * period)
+        out_ref[0, 0, :, :, cols] = (
+            field_ref[0, 0, :, :, cols].astype(jnp.float32) + gain_h
+        ).astype(out_ref.dtype)
+        for t in range(1, fields):
+            out_ref[0, t, :, :, cols] = (
+                field_ref[0, t, :, :, cols].astype(jnp.float32) + slope_h * wave_ref[t, :, 0]
+            ).astype(out_ref.dtype)
 
 
 def legendre_kernel(modes_ref, base_ref, folded_ref, leg_ref, gain_ref, out_ref, *, block):
@@ -228,21 +245,19 @@
     waveform = lax.dot_general(
         returned, inv, (((0,), (0,)), ((), ())), preferred_element_type=jnp.float32
     ) * ratio
-    waveform = jnp.transpose(waveform.reshape(fields, 2, chans, cycles, period), (2, 0, 1, 3, 4))
-    waveform = waveform.reshape(chans, fields, -1, period)
-    primal_h = waveform[:, 0]
-    sigmoid_h = jax.nn.sigmoid(primal_h)
-    slope_h = sigmoid_h * (1.0 + primal_h * (1.0 - sigmoid_h))
-    gain_h = primal_h * sigmoid_h
-    flat = field.reshape(chans, fields, -1, points)
-    pieces = []
-    for n in range(points // period):
-        initial = flat[:, :, :, n * period : (n + 1) * period].astype(jnp.float32)
-        primal = initial[:, 0] + gain_h
-        tangents = initial[:, 1:] + slope_h[:, None] * waveform[:, 1:]
-        pieces.append(jnp.concatenate([primal[:, None], tangents], axis=1).astype(jnp.bfloat16))
-    out = jnp.concatenate(pieces, axis=3)
-    return out.reshape(field.shape)
+    waveform = waveform.reshape(fields, 2, chans, cycles, period)
+    block = (1,) + field.shape[1:]
+    return pl.pallas_call(
+        functools.partial(epilogue_kernel, period=period),
+        grid=(chans,),
+        in_specs=[
+            pl.BlockSpec((fields, 2, 1, cycles, period), lambda c: (0, 0, c, 0, 0)),
+            pl.BlockSpec(block, lambda c: (c, 0, 0, 0, 0)),
+        ],
+        out_specs=pl.BlockSpec(block, lambda c: (c, 0, 0, 0, 0)),
+        out_shape=jax.ShapeDtypeStruct(field.shape, field.dtype),
+        compiler_params=pltpu.CompilerParams(vmem_limit_bytes=48 * 1024 * 1024),
+    )(waveform, field)
 
 
 def solution(mesh):

time: 122 us -> 118 us (0.967)
  blocking collectives: 26 us -> 58.9 us
  waiting for transfers between devices: 17.2 us -> 0.01 us
  other arithmetic: 22.7 us -> 7.56 us
  starting transfers between devices: 20.4 us -> 11.6 us
  Pallas kernels: 17.4 us -> 25.8 us
  local copies, waits for them, and re-layouts: 8.99 us -> 6.4 us
  matrix products: 8.66 us -> 6.43 us
    all_to_all x0 -> x1, blocking collectives: none -> 33.4 us  [local(): returned = lax.all_to_all(leaving, ('chan', 'lat'), 0, 0, tiled=True)]
    all_to_all x1 -> x0, waiting for transfers between devices: 17.2 us -> none  [local(): returned = lax.all_to_all(leaving, ('chan', 'lat'), 0, 0, tiled=True)]
    all_to_all x1 -> x0, starting transfers between devices: 9.31 us -> none  [local(): returned = lax.all_to_all(leaving, ('chan', 'lat'), 0, 0, tiled=True)]
    pallas_call x0 -> x1, Pallas kernels: none -> 8.39 us  [local(): pl.pallas_call(functools.partial(epilogue_kernel, period=period), grid=(c...]
    convert_element_type x1 -> x0, other arithmetic: 7.23 us -> none  [local(): initial = flat[:, :, :, n * period:(n + 1) * period].astype(jnp.float32)]
    concatenate x1 -> x0, other arithmetic: 4.58 us -> none  [local(): out = jnp.concatenate(pieces, axis=3)]
    another operation x3 -> x1, other arithmetic: 3.39 us -> 0.01 us
    unnamed x19 -> x11, local copies, waits for them, and re-layouts: 3.95 us -> 1.51 us
  transfers between devices with their start and end apart: 2 -> 1, of which waited for: 1 -> 0; matrix products, arithmetic and copies ran while one was open for 7% -> 1% of each run, Pallas kernels for 0% -> 0%
where the time goes in v8:
time: 118 us; the launch traced here: 117 us
  blocking collectives  58.9 us (50%)
  Pallas kernels  25.8 us (22%)
  starting transfers between devices  11.6 us (10%)
  other arithmetic  7.56 us (6%)
  matrix products  6.43 us (5%)
  local copies, waits for them, and re-layouts  6.4 us (5%)
    all_to_all x1, blocking collectives, local(): returned = lax.all_to_all(leaving, ('chan', 'lat'), 0, 0, tiled=True)  33.4 us
    all_gather x1, blocking collectives, local(): all_gain = lax.all_gather(spectral_gain, 'chan', axis=0, tiled=True)  25.5 us
    all_to_all x1, starting transfers between devices, local(): got = lax.all_to_all(sent, ('chan', 'lat'), 0, 0, tiled=True)  11.6 us
    pallas_call x1, Pallas kernels, legendre_stage(): pl.pallas_call(functools.partial(legendre_kernel, block=block), grid_spec...  8.62 us
    pallas_call x1, Pallas kernels, local(): pl.pallas_call(functools.partial(epilogue_kernel, period=period), grid=(c...  8.39 us
    pallas_call x1, Pallas kernels, local(): pl.pallas_call(functools.partial(gather_kernel, piece=piece, per_dev=per_...  5.01 us
    dot_general x1, matrix products, local(): lax.dot_general(jnp.concatenate([fwd, fwd], axis=1), rows, (((1,), (1,)),...  4.61 us
    pallas_call x1, Pallas kernels, local(): pl.pallas_call(functools.partial(scatter_kernel, piece=piece, per_dev=per...  3.78 us
  transfers between devices with their start and end apart: 1, of which 0 were waited for; matrix products, arithmetic and copies ran while one was open for 1% of the time, Pallas kernels for 0%

profile of v8, /device:TPU:0, one launch (start us, length us, event | category | flops | bytes accessed | tf_op | source)
XLA Modules:
  0.0 117.0 jit_solution(13961311294274119118)
XLA Ops:
  0.0 0.7 broadcast_multiply_fusion.1
  0.7 0.1 reshape.113
  1.2 0.2 fusion.28
  1.4 0.3 copy.22
  1.7 0.3 copy.24
  2.0 2.4 %fusion.23 = (f32[128,4,128]{2,1,0:T(4,128)S(1)}, f32[128,4,128]{2,1,0:T(4,128)S(1)}) fusion(s32[128,4]{1,0:T(8,128)S(1)} %copy.23), kind=kLoop, calls=%fused_computation.24 | loop fusion | flops 917504 | bytes 526336 | tf_op jit(solution)/shard_map/cos | solution.py:185
  4.4 2.5 %multiply_convert_fusion = bf16[128,2,4,8,128]{4,3,2,1,0:T(8,128)(2,1)S(1)} fusion(f32[128,4,128]{2,1,0:T(4,128)S(1)} %get-tuple-element.8, f32[128,2,4,8]{3,2,1,0:T(4,128)S(1)} %copy.24, f32[128,4,128]{2,1,0:T(4,128)S(1)} %get-tuple-element.7, f32[128,2,4,8]{3,2,1,0:T(4,128)S(1)} %copy.22), kind=kLoop, calls=%fused_computation.4 | loop fusion | flops 5242880 | bytes 2686976 | tf_op jit(solution)/shard_map/convert_element_type | solution.py:187
  6.9 0.6 copy.35
  7.6 0.8 copy.25
  8.4 1.5 %subtract_convert_fusion = (bf16[768,1024]{1,0:T(8,128)(2,1)S(1)}, bf16[768,1024]{1,0:T(8,128)(2,1)S(1)}) fusion(bf16[768,4096]{1,0:T(8,128)(2,1)S(1)} %bitcast.40), kind=kLoop, calls=%fused_computation.8 | loop fusion | flops 8650752 | bytes 9437184 | tf_op jit(solution)/shard_map/convert_element_type | solution.py:201
  9.9 4.6 %fusion.13 = bf16[128,8,768]{2,1,0:T(8,128)(2,1)} fusion(bf16[768,1024]{1,0:T(8,128)(2,1)S(1)} %get-tuple-element.5, bf16[768,1024]{1,0:T(8,128)(2,1)S(1)} %get-tuple-element.6, bf16[1024,1024]{1,0:T(8,128)(2,1)S(1)} %bitcast.42), kind=kOutput, calls=%fused_computation.15 | convolution fusion | flops 3236691968 | bytes 6815744 | tf_op jit(solution)/shard_map/dot_general | solution.py:203
  14.5 11.6 %all-to-all-start = ((bf16[128,8,768]{2,1,0:T(8,128)(2,1)}), bf16[128,8,768]{2,1,0:T(8,128)(2,1)}, u32[]{:S(2)}, u32[]{:S(2)}) async-start(bf16[128,8,768]{2,1,0:T(8,128)(2,1)} %fusion.13), calls=%async_computation | async-start | bytes 3145728 | tf_op jit(solution)/shard_map/all_to_all | solution.py:209
  26.7 25.5 %all_gather.3 = f32[32,2048]{1,0:T(8,128)S(1)} all-gather(f32[8,2048]{1,0:T(8,128)S(1)} %copy-done.1), channel_id=1, replica_groups=mesh['lat'=32,'chan'=4] {'chan'}, dimensions={0}, use_global_device_ids=true | all-gather | bytes 327680 | tf_op jit(solution)/shard_map/all_gather | solution.py:225
  52.2 0.3 copy.29
  52.6 0.4 copy.30
  53.1 1.7 %copy.36 = bf16[4,32,8,768]{3,1,2,0:T(8,128)(2,1)S(1)} copy(bf16[4,32,8,768]{3,2,1,0:T(8,128)(2,1)} %bitcast.6) | data formatting | bytes 3145728 | tf_op jit(solution)/shard_map/reshape | solution.py:210
  54.9 5.0 %shard_map.73 = bf16[4,2,3,2,32,512]{5,4,3,2,1,0:T(8,128)(2,1)S(1)} custom-call(bf16[4,8,32,768]{3,2,1,0:T(8,128)(2,1)S(1)} %bitcast.38, bf16[64,64]{1,0:T(8,128)(2,1)S(1)} %copy.28.mix_ref), custom_call_target="tpu_custom_call" | custom-call | tf_op jit(solution)/shard_map/pallas_call | solution.py:216
  59.9 0.2 tile.4
  60.1 8.6 %shard_map.74.back_ref = bf16[4,2,192,512]{3,2,1,0:T(8,128)(2,1)S(1)} custom-call(s32[4]{0:T(128)S(1)} %dynamic_slice.3.modes_ref, s32[1]{0:T(128)} %bitcast.1.base_ref, bf16[4,2,192,512]{3,2,1,0:T(8,128)(2,1)S(1)} %bitcast.36, bf16[2,16,512,1024]{3,2,1,0:T(8,128)(2,1)} %leg_ref.1, f32[2,192,1024]{2,1,0:T(8,128)S(1)} %bitcast.37), custom_call_target="tpu_custom_call" | custom-call | flops 3221225472 | bytes 13107200 | tf_op jit(solution)/shard_map/pallas_call | solution.py:146
  68.7 3.8 %shard_map.75 = bf16[4,8,32,768]{3,2,1,0:T(8,128)(2,1)S(1)} custom-call(bf16[4,2,192,512]{3,2,1,0:T(8,128)(2,1)S(1)} %shard_map.74.back_ref), custom_call_target="tpu_custom_call" | custom-call | tf_op jit(solution)/shard_map/pallas_call | solution.py:236
  72.5 0.9 copy.31
  73.3 33.4 %all_to_all.10 = bf16[128,8,768]{2,1,0:T(8,128)(2,1)S(1)} all-to-all(bf16[128,8,768]{2,1,0:T(8,128)(2,1)S(1)} %bitcast.44), channel_id=1, replica_groups=mesh['lat'=32,'chan'=4] {'chan','lat'}, dimensions={0} | all-to-all | bytes 3145728 | tf_op jit(solution)/shard_map/all_to_all | solution.py:242
  106.7 1.8 %convolution_multiply_fusion = f32[768,1024]{1,0:T(8,128)S(1)} fusion(bf16[1024,1024]{1,0:T(8,128)(2,1)S(1)} %bitcast.43, bf16[128,8,768]{2,1,0:T(8,128)(2,1)S(1)} %all_to_all.10), kind=kOutput, calls=%fused_computation.11 | convolution fusion | flops 1611399168 | bytes 6815744 | tf_op jit(solution)/shard_map/dot_general | solution.py:245
  108.6 8.4 %shard_map.76 = bf16[8,3,2,16,4096]{4,3,2,1,0:T(8,128)(2,1)} custom-call(f32[3,2,8,16,1024]{4,3,2,1,0:T(8,128)S(1)} %bitcast.35, bf16[8,3,2,16,4096]{4,3,2,1,0:T(8,128)(2,1)} %field_ref.1), custom_call_target="tpu_custom_call" | custom-call | tf_op jit(solution)/shard_map/pallas_call | solution.py:250
  (23 shorter events, 1.0 us)
Async XLA Ops:
  4.4 3.2 %copy-start = (bf16[8,3,2,16,4096]{4,3,2,1,0:T(8,128)(2,1)S(1)}, bf16[8,3,2,16,4096]{4,3,2,1,0:T(8,128)(2,1)}, u32[]{:S(2)}) copy-start(bf16[8,3,2,16,4096]{4,3,2,1,0:T(8,128)(2,1)} %field_ref.1) | copy-start | bytes 18874372
  14.5 11.8 %copy-start.2 = (bf16[32,32]{1,0:T(8,128)(2,1)S(1)}, bf16[32,32]{1,0:T(8,128)(2,1)}, u32[]{:S(2)}) copy-start(bf16[32,32]{1,0:T(8,128)(2,1)} %param.8) | copy-start | bytes 6148
  14.5 11.9 %copy-start.3 = (f32[2,2]{0,1:T(2,128)S(1)}, f32[2,2]{0,1:T(2,128)}, u32[]{:S(2)}) copy-start(f32[2,2]{0,1:T(2,128)} %constant.55.clone) | copy-start | bytes 52
  14.5 12.2 %copy-start.1 = (f32[8,2048]{1,0:T(8,128)S(1)}, f32[8,2048]{1,0:T(8,128)}, u32[]{:S(2)}) copy-start(f32[8,2048]{1,0:T(8,128)} %param.9) | copy-start | bytes 196612
  14.5 38.6 %all-to-all-start = ((bf16[128,8,768]{2,1,0:T(8,128)(2,1)}), bf16[128,8,768]{2,1,0:T(8,128)(2,1)}, u32[]{:S(2)}, u32[]{:S(2)}) async-start(bf16[128,8,768]{2,1,0:T(8,128)(2,1)} %fusion.13), calls=%async_computation | async-start | bytes 3145728 | tf_op jit(solution)/shard_map/all_to_all | solution.py:209

commit v9 on v8

--- a/solution.py
+++ b/solution.py
@@ -193,6 +193,8 @@
         inv = (basis * math.sqrt(1.0 / total_modes)).astype(jnp.bfloat16)
         ratio = 1.0
 
+    all_gain = lax.all_gather(spectral_gain, "chan", axis=0, tiled=True)
+    all_gain, field = lax.optimization_barrier((all_gain, field))
     flat = jnp.transpose(field, (1, 2, 0, 3, 4)).reshape(-1, points)
     summed = flat[:, :period].astype(jnp.float32)
     for n in range(1, points // period):
@@ -222,7 +224,6 @@
         compiler_params=pltpu.CompilerParams(vmem_limit_bytes=48 * 1024 * 1024),
     )(got, mix_fold)
 
-    all_gain = lax.all_gather(spectral_gain, "chan", axis=0, tiled=True)
     gain_par = jnp.transpose(all_gain.reshape(-1, half_deg, 2), (2, 0, 1))
     own_modes = lax.dynamic_slice_in_dim(
         modes.reshape(-1), (chan_index * n_lat + lat_index) * per_dev, per_dev, 0

time: 118 us -> 123 us (1.042)
  waiting for transfers between devices: 0.01 us -> 23 us
  blocking collectives: 58.9 us -> 41.8 us
    all_to_all x1, waiting for transfers between devices: 0.01 us -> 23 us  [local(): got = lax.all_to_all(sent, ('chan', 'lat'), 0, 0, tiled=True)]
    all_gather x1, blocking collectives: 25.5 us -> 12.7 us  [local(): all_gain = lax.all_gather(spectral_gain, 'chan', axis=0, tiled=True)]
    all_to_all x1, blocking collectives: 33.4 us -> 29.1 us  [local(): returned = lax.all_to_all(leaving, ('chan', 'lat'), 0, 0, tiled=True)]
  transfers between devices with their start and end apart: 1 -> 1, of which waited for: 0 -> 1; matrix products, arithmetic and copies ran while one was open for 1% -> 1% of each run, Pallas kernels for 0% -> 0%
where the time goes in v9:
time: 123 us; the launch traced here: 122 us
  blocking collectives  41.8 us (34%)
  Pallas kernels  25.8 us (21%)
  waiting for transfers between devices  23 us (19%)
  starting transfers between devices  10.9 us (9%)
  other arithmetic  7.51 us (6%)
  matrix products  6.46 us (5%)
  local copies, waits for them, and re-layouts  6.4 us (5%)
    all_to_all x1, blocking collectives, local(): returned = lax.all_to_all(leaving, ('chan', 'lat'), 0, 0, tiled=True)  29.1 us
    all_to_all x1, waiting for transfers between devices, local(): got = lax.all_to_all(sent, ('chan', 'lat'), 0, 0, tiled=True)  23 us
    all_gather x1, blocking collectives, local(): all_gain = lax.all_gather(spectral_gain, 'chan', axis=0, tiled=True)  12.7 us
    all_to_all x1, starting transfers between devices, local(): got = lax.all_to_all(sent, ('chan', 'lat'), 0, 0, tiled=True)  10.9 us
    pallas_call x1, Pallas kernels, legendre_stage(): pl.pallas_call(functools.partial(legendre_kernel, block=block), grid_spec...  8.62 us
    pallas_call x1, Pallas kernels, local(): pl.pallas_call(functools.partial(epilogue_kernel, period=period), grid=(c...  8.39 us
    pallas_call x1, Pallas kernels, local(): pl.pallas_call(functools.partial(gather_kernel, piece=piece, per_dev=per_...  5.01 us
    dot_general x1, matrix products, local(): lax.dot_general(jnp.concatenate([fwd, fwd], axis=1), rows, (((1,), (1,)),...  4.61 us
  transfers between devices with their start and end apart: 1, of which 1 were waited for; matrix products, arithmetic and copies ran while one was open for 1% of the time, Pallas kernels for 0%

profile of v9, /device:TPU:0, one launch (start us, length us, event | category | flops | bytes accessed | tf_op | source)
XLA Modules:
  0.0 122.1 jit_solution(13797004295941252489)
XLA Ops:
  0.0 0.7 broadcast_multiply_fusion.1
  1.1 2.4 %fusion.23 = (f32[128,4,128]{2,1,0:T(4,128)S(1)}, f32[128,4,128]{2,1,0:T(4,128)S(1)}) fusion(s32[128,4]{1,0:T(8,128)S(1)} %copy.23), kind=kLoop, calls=%fused_computation.24 | loop fusion | flops 917504 | bytes 526336 | tf_op jit(solution)/shard_map/cos | solution.py:185
  3.6 0.2 fusion.28
  3.8 0.3 copy.24
  4.1 0.3 copy.22
  4.4 2.5 %multiply_convert_fusion = bf16[128,2,4,8,128]{4,3,2,1,0:T(8,128)(2,1)S(1)} fusion(f32[128,4,128]{2,1,0:T(4,128)S(1)} %get-tuple-element.12, f32[128,2,4,8]{3,2,1,0:T(4,128)S(1)} %copy.24, f32[128,4,128]{2,1,0:T(4,128)S(1)} %get-tuple-element.11, f32[128,2,4,8]{3,2,1,0:T(4,128)S(1)} %copy.22), kind=kLoop, calls=%fused_computation.4 | loop fusion | flops 5242880 | bytes 2686976 | tf_op jit(solution)/shard_map/convert_element_type | solution.py:187
  6.9 0.6 copy.35
  7.5 12.7 %all_gather.3 = f32[32,2048]{1,0:T(8,128)S(1)} all-gather(f32[8,2048]{1,0:T(8,128)S(1)} %copy-done.1), channel_id=1, replica_groups=mesh['lat'=32,'chan'=4] {'chan'}, dimensions={0}, use_global_device_ids=true | all-gather | bytes 327680 | tf_op jit(solution)/shard_map/all_gather | solution.py:196
  20.2 0.8 copy.25
  21.0 1.5 %subtract_convert_fusion = (bf16[768,1024]{1,0:T(8,128)(2,1)S(1)}, bf16[768,1024]{1,0:T(8,128)(2,1)S(1)}) fusion(bf16[768,4096]{1,0:T(8,128)(2,1)S(1)} %bitcast.40), kind=kLoop, calls=%fused_computation.8 | loop fusion | flops 8650752 | bytes 9437184 | tf_op jit(solution)/shard_map/convert_element_type | solution.py:203
  22.6 4.6 %fusion.13 = bf16[128,8,768]{2,1,0:T(8,128)(2,1)} fusion(bf16[768,1024]{1,0:T(8,128)(2,1)S(1)} %get-tuple-element.9, bf16[768,1024]{1,0:T(8,128)(2,1)S(1)} %get-tuple-element.10, bf16[1024,1024]{1,0:T(8,128)(2,1)S(1)} %bitcast.42), kind=kOutput, calls=%fused_computation.15 | convolution fusion | flops 3236691968 | bytes 6815744 | tf_op jit(solution)/shard_map/dot_general | solution.py:205
  27.2 10.9 %all-to-all-start = ((bf16[128,8,768]{2,1,0:T(8,128)(2,1)}), bf16[128,8,768]{2,1,0:T(8,128)(2,1)}, u32[]{:S(2)}, u32[]{:S(2)}) async-start(bf16[128,8,768]{2,1,0:T(8,128)(2,1)} %fusion.13), calls=%async_computation | async-start | bytes 3145728 | tf_op jit(solution)/shard_map/all_to_all | solution.py:211
  38.7 0.3 copy.29
  39.0 0.4 copy.30
  39.5 23.0 %all-to-all-done = bf16[128,8,768]{2,1,0:T(8,128)(2,1)} async-done(((bf16[128,8,768]{2,1,0:T(8,128)(2,1)}), bf16[128,8,768]{2,1,0:T(8,128)(2,1)}, u32[]{:S(2)}, u32[]{:S(2)}) %all-to-all-start) | async-done | bytes 1572896 | tf_op jit(solution)/shard_map/all_to_all | solution.py:211
  62.6 1.7 %copy.36 = bf16[4,32,8,768]{3,1,2,0:T(8,128)(2,1)S(1)} copy(bf16[4,32,8,768]{3,2,1,0:T(8,128)(2,1)} %bitcast.6) | data formatting | bytes 3145728 | tf_op jit(solution)/shard_map/reshape | solution.py:212
  64.3 5.0 %shard_map.73 = bf16[4,2,3,2,32,512]{5,4,3,2,1,0:T(8,128)(2,1)S(1)} custom-call(bf16[4,8,32,768]{3,2,1,0:T(8,128)(2,1)S(1)} %bitcast.38, bf16[64,64]{1,0:T(8,128)(2,1)S(1)} %copy.28.mix_ref), custom_call_target="tpu_custom_call" | custom-call | tf_op jit(solution)/shard_map/pallas_call | solution.py:218
  69.3 0.2 tile.4
  69.5 8.6 %shard_map.74.back_ref = bf16[4,2,192,512]{3,2,1,0:T(8,128)(2,1)S(1)} custom-call(s32[4]{0:T(128)S(1)} %dynamic_slice.3.modes_ref, s32[1]{0:T(128)} %bitcast.1.base_ref, bf16[4,2,192,512]{3,2,1,0:T(8,128)(2,1)S(1)} %bitcast.36, bf16[2,16,512,1024]{3,2,1,0:T(8,128)(2,1)} %leg_ref.1, f32[2,192,1024]{2,1,0:T(8,128)S(1)} %bitcast.37), custom_call_target="tpu_custom_call" | custom-call | flops 3221225472 | bytes 13107200 | tf_op jit(solution)/shard_map/pallas_call | solution.py:146
  78.2 3.8 %shard_map.75 = bf16[4,8,32,768]{3,2,1,0:T(8,128)(2,1)S(1)} custom-call(bf16[4,2,192,512]{3,2,1,0:T(8,128)(2,1)S(1)} %shard_map.74.back_ref), custom_call_target="tpu_custom_call" | custom-call | tf_op jit(solution)/shard_map/pallas_call | solution.py:237
  81.9 0.9 copy.31
  82.8 29.1 %all_to_all.10 = bf16[128,8,768]{2,1,0:T(8,128)(2,1)S(1)} all-to-all(bf16[128,8,768]{2,1,0:T(8,128)(2,1)S(1)} %bitcast.44), channel_id=1, replica_groups=mesh['lat'=32,'chan'=4] {'chan','lat'}, dimensions={0} | all-to-all | bytes 3145728 | tf_op jit(solution)/shard_map/all_to_all | solution.py:243
  111.9 1.8 %convolution_multiply_fusion = f32[768,1024]{1,0:T(8,128)S(1)} fusion(bf16[1024,1024]{1,0:T(8,128)(2,1)S(1)} %bitcast.43, bf16[128,8,768]{2,1,0:T(8,128)(2,1)S(1)} %all_to_all.10), kind=kOutput, calls=%fused_computation.11 | convolution fusion | flops 1611399168 | bytes 6815744 | tf_op jit(solution)/shard_map/dot_general | solution.py:246
  113.7 8.4 %shard_map.76 = bf16[8,3,2,16,4096]{4,3,2,1,0:T(8,128)(2,1)} custom-call(f32[3,2,8,16,1024]{4,3,2,1,0:T(8,128)S(1)} %bitcast.35, bf16[8,3,2,16,4096]{4,3,2,1,0:T(8,128)(2,1)} %field_ref), custom_call_target="tpu_custom_call" | custom-call | tf_op jit(solution)/shard_map/pallas_call | solution.py:251
  (23 shorter events, 1.1 us)
Async XLA Ops:
  4.4 3.1 %copy-start.1 = (f32[8,2048]{1,0:T(8,128)S(1)}, f32[8,2048]{1,0:T(8,128)}, u32[]{:S(2)}) copy-start(f32[8,2048]{1,0:T(8,128)} %param.9) | copy-start | bytes 196612
  4.4 15.8 %copy-start = (bf16[8,3,2,16,4096]{4,3,2,1,0:T(8,128)(2,1)S(1)}, bf16[8,3,2,16,4096]{4,3,2,1,0:T(8,128)(2,1)}, u32[]{:S(2)}) copy-start(bf16[8,3,2,16,4096]{4,3,2,1,0:T(8,128)(2,1)} %field_ref) | copy-start | bytes 18874372
  27.2 11.1 %copy-start.2 = (bf16[32,32]{1,0:T(8,128)(2,1)S(1)}, bf16[32,32]{1,0:T(8,128)(2,1)}, u32[]{:S(2)}) copy-start(bf16[32,32]{1,0:T(8,128)(2,1)} %param.8) | copy-start | bytes 6148
  27.2 11.2 %copy-start.3 = (f32[2,2]{0,1:T(2,128)S(1)}, f32[2,2]{0,1:T(2,128)}, u32[]{:S(2)}) copy-start(f32[2,2]{0,1:T(2,128)} %constant.55.clone) | copy-start | bytes 52
  27.2 35.4 %all-to-all-start = ((bf16[128,8,768]{2,1,0:T(8,128)(2,1)}), bf16[128,8,768]{2,1,0:T(8,128)(2,1)}, u32[]{:S(2)}, u32[]{:S(2)}) async-start(bf16[128,8,768]{2,1,0:T(8,128)(2,1)} %fusion.13), calls=%async_computation | async-start | bytes 3145728 | tf_op jit(solution)/shard_map/all_to_all | solution.py:211

commit v10 on v8

--- a/solution.py
+++ b/solution.py
@@ -86,19 +86,20 @@
 
 def epilogue_kernel(wave_ref, field_ref, out_ref, *, period):
     fields = wave_ref.shape[0]
-    primal_h = wave_ref[0, :, 0]
-    sigmoid_h = 1.0 / (1.0 + jnp.exp(-primal_h))
-    slope_h = sigmoid_h * (1.0 + primal_h * (1.0 - sigmoid_h))
-    gain_h = primal_h * sigmoid_h
-    for n in range(field_ref.shape[-1] // period):
-        cols = slice(n * period, (n + 1) * period)
-        out_ref[0, 0, :, :, cols] = (
-            field_ref[0, 0, :, :, cols].astype(jnp.float32) + gain_h
-        ).astype(out_ref.dtype)
-        for t in range(1, fields):
-            out_ref[0, t, :, :, cols] = (
-                field_ref[0, t, :, :, cols].astype(jnp.float32) + slope_h * wave_ref[t, :, 0]
+    for c in range(field_ref.shape[0]):
+        primal_h = wave_ref[0, :, c]
+        sigmoid_h = 1.0 / (1.0 + jnp.exp(-primal_h))
+        slope_h = sigmoid_h * (1.0 + primal_h * (1.0 - sigmoid_h))
+        gain_h = primal_h * sigmoid_h
+        for n in range(field_ref.shape[-1] // period):
+            cols = slice(n * period, (n + 1) * period)
+            out_ref[c, 0, :, :, cols] = (
+                field_ref[c, 0, :, :, cols].astype(jnp.float32) + gain_h
             ).astype(out_ref.dtype)
+            for t in range(1, fields):
+                out_ref[c, t, :, :, cols] = (
+                    field_ref[c, t, :, :, cols].astype(jnp.float32) + slope_h * wave_ref[t, :, c]
+                ).astype(out_ref.dtype)
 
 
 def legendre_kernel(modes_ref, base_ref, folded_ref, leg_ref, gain_ref, out_ref, *, block):
@@ -246,12 +247,13 @@
         returned, inv, (((0,), (0,)), ((), ())), preferred_element_type=jnp.float32
     ) * ratio
     waveform = waveform.reshape(fields, 2, chans, cycles, period)
-    block = (1,) + field.shape[1:]
+    per_step = 2 if chans % 2 == 0 else 1
+    block = (per_step,) + field.shape[1:]
     return pl.pallas_call(
         functools.partial(epilogue_kernel, period=period),
-        grid=(chans,),
+        grid=(chans // per_step,),
         in_specs=[
-            pl.BlockSpec((fields, 2, 1, cycles, period), lambda c: (0, 0, c, 0, 0)),
+            pl.BlockSpec((fields, 2, per_step, cycles, period), lambda c: (0, 0, c, 0, 0)),
             pl.BlockSpec(block, lambda c: (c, 0, 0, 0, 0)),
         ],
         out_specs=pl.BlockSpec(block, lambda c: (c, 0, 0, 0, 0)),

time: 118 us -> 116 us (0.983)
  Pallas kernels: 25.8 us -> 23.9 us
    pallas_call x1, Pallas kernels: 8.39 us -> 6.47 us  [local(): pl.pallas_call(functools.partial(epilogue_kernel, period=period), grid=(c...]
where the time goes in v10:
time: 116 us; the launch traced here: 115 us
  blocking collectives  58.9 us (51%)
  Pallas kernels  23.9 us (21%)
  starting transfers between devices  11.6 us (10%)
  other arithmetic  7.56 us (7%)
  matrix products  6.44 us (6%)
  local copies, waits for them, and re-layouts  6.4 us (6%)
    all_to_all x1, blocking collectives, local(): returned = lax.all_to_all(leaving, ('chan', 'lat'), 0, 0, tiled=True)  33.4 us
    all_gather x1, blocking collectives, local(): all_gain = lax.all_gather(spectral_gain, 'chan', axis=0, tiled=True)  25.5 us
    all_to_all x1, starting transfers between devices, local(): got = lax.all_to_all(sent, ('chan', 'lat'), 0, 0, tiled=True)  11.6 us
    pallas_call x1, Pallas kernels, legendre_stage(): pl.pallas_call(functools.partial(legendre_kernel, block=block), grid_spec...  8.62 us
    pallas_call x1, Pallas kernels, local(): pl.pallas_call(functools.partial(epilogue_kernel, period=period), grid=(c...  6.47 us
    pallas_call x1, Pallas kernels, local(): pl.pallas_call(functools.partial(gather_kernel, piece=piece, per_dev=per_...  5.01 us
    dot_general x1, matrix products, local(): lax.dot_general(jnp.concatenate([fwd, fwd], axis=1), rows, (((1,), (1,)),...  4.61 us
    pallas_call x1, Pallas kernels, local(): pl.pallas_call(functools.partial(scatter_kernel, piece=piece, per_dev=per...  3.78 us
  transfers between devices with their start and end apart: 1, of which 0 were waited for; matrix products, arithmetic and copies ran while one was open for 1% of the time, Pallas kernels for 0%

profile of v10, /device:TPU:0, one launch (start us, length us, event | category | flops | bytes accessed | tf_op | source)
XLA Modules:
  0.0 115.0 jit_solution(7410272611720595950)
XLA Ops:
  0.0 0.7 broadcast_multiply_fusion.1
  0.7 0.1 reshape.113
  1.2 0.2 fusion.28
  1.4 0.3 copy.22
  1.7 0.3 copy.24
  2.0 2.4 %fusion.23 = (f32[128,4,128]{2,1,0:T(4,128)S(1)}, f32[128,4,128]{2,1,0:T(4,128)S(1)}) fusion(s32[128,4]{1,0:T(8,128)S(1)} %copy.23), kind=kLoop, calls=%fused_computation.24 | loop fusion | flops 917504 | bytes 526336 | tf_op jit(solution)/shard_map/cos | solution.py:186
  4.4 2.5 %multiply_convert_fusion = bf16[128,2,4,8,128]{4,3,2,1,0:T(8,128)(2,1)S(1)} fusion(f32[128,4,128]{2,1,0:T(4,128)S(1)} %get-tuple-element.8, f32[128,2,4,8]{3,2,1,0:T(4,128)S(1)} %copy.24, f32[128,4,128]{2,1,0:T(4,128)S(1)} %get-tuple-element.7, f32[128,2,4,8]{3,2,1,0:T(4,128)S(1)} %copy.22), kind=kLoop, calls=%fused_computation.4 | loop fusion | flops 5242880 | bytes 2686976 | tf_op jit(solution)/shard_map/convert_element_type | solution.py:188
  6.9 0.6 copy.35
  7.6 0.8 copy.25
  8.4 1.5 %subtract_convert_fusion = (bf16[768,1024]{1,0:T(8,128)(2,1)S(1)}, bf16[768,1024]{1,0:T(8,128)(2,1)S(1)}) fusion(bf16[768,4096]{1,0:T(8,128)(2,1)S(1)} %bitcast.40), kind=kLoop, calls=%fused_computation.8 | loop fusion | flops 8650752 | bytes 9437184 | tf_op jit(solution)/shard_map/convert_element_type | solution.py:202
  9.9 4.6 %fusion.13 = bf16[128,8,768]{2,1,0:T(8,128)(2,1)} fusion(bf16[768,1024]{1,0:T(8,128)(2,1)S(1)} %get-tuple-element.5, bf16[768,1024]{1,0:T(8,128)(2,1)S(1)} %get-tuple-element.6, bf16[1024,1024]{1,0:T(8,128)(2,1)S(1)} %bitcast.42), kind=kOutput, calls=%fused_computation.15 | convolution fusion | flops 3236691968 | bytes 6815744 | tf_op jit(solution)/shard_map/dot_general | solution.py:204
  14.5 11.6 %all-to-all-start = ((bf16[128,8,768]{2,1,0:T(8,128)(2,1)}), bf16[128,8,768]{2,1,0:T(8,128)(2,1)}, u32[]{:S(2)}, u32[]{:S(2)}) async-start(bf16[128,8,768]{2,1,0:T(8,128)(2,1)} %fusion.13), calls=%async_computation | async-start | bytes 3145728 | tf_op jit(solution)/shard_map/all_to_all | solution.py:210
  26.7 25.5 %all_gather.3 = f32[32,2048]{1,0:T(8,128)S(1)} all-gather(f32[8,2048]{1,0:T(8,128)S(1)} %copy-done.1), channel_id=1, replica_groups=mesh['lat'=32,'chan'=4] {'chan'}, dimensions={0}, use_global_device_ids=true | all-gather | bytes 327680 | tf_op jit(solution)/shard_map/all_gather | solution.py:226
  52.2 0.3 copy.29
  52.6 0.4 copy.30
  53.1 1.7 %copy.36 = bf16[4,32,8,768]{3,1,2,0:T(8,128)(2,1)S(1)} copy(bf16[4,32,8,768]{3,2,1,0:T(8,128)(2,1)} %bitcast.6) | data formatting | bytes 3145728 | tf_op jit(solution)/shard_map/reshape | solution.py:211
  54.8 5.0 %shard_map.73 = bf16[4,2,3,2,32,512]{5,4,3,2,1,0:T(8,128)(2,1)S(1)} custom-call(bf16[4,8,32,768]{3,2,1,0:T(8,128)(2,1)S(1)} %bitcast.38, bf16[64,64]{1,0:T(8,128)(2,1)S(1)} %copy.28.mix_ref), custom_call_target="tpu_custom_call" | custom-call | tf_op jit(solution)/shard_map/pallas_call | solution.py:217
  59.9 0.2 tile.4
  60.1 8.6 %shard_map.74.back_ref = bf16[4,2,192,512]{3,2,1,0:T(8,128)(2,1)S(1)} custom-call(s32[4]{0:T(128)S(1)} %dynamic_slice.3.modes_ref, s32[1]{0:T(128)} %bitcast.1.base_ref, bf16[4,2,192,512]{3,2,1,0:T(8,128)(2,1)S(1)} %bitcast.36, bf16[2,16,512,1024]{3,2,1,0:T(8,128)(2,1)} %leg_ref.1, f32[2,192,1024]{2,1,0:T(8,128)S(1)} %bitcast.37), custom_call_target="tpu_custom_call" | custom-call | flops 3221225472 | bytes 13107200 | tf_op jit(solution)/shard_map/pallas_call | solution.py:147
  68.7 3.8 %shard_map.75 = bf16[4,8,32,768]{3,2,1,0:T(8,128)(2,1)S(1)} custom-call(bf16[4,2,192,512]{3,2,1,0:T(8,128)(2,1)S(1)} %shard_map.74.back_ref), custom_call_target="tpu_custom_call" | custom-call | tf_op jit(solution)/shard_map/pallas_call | solution.py:237
  72.5 0.9 copy.31
  73.3 33.4 %all_to_all.10 = bf16[128,8,768]{2,1,0:T(8,128)(2,1)S(1)} all-to-all(bf16[128,8,768]{2,1,0:T(8,128)(2,1)S(1)} %bitcast.44), channel_id=1, replica_groups=mesh['lat'=32,'chan'=4] {'chan','lat'}, dimensions={0} | all-to-all | bytes 3145728 | tf_op jit(solution)/shard_map/all_to_all | solution.py:243
  106.7 1.8 %convolution_multiply_fusion = f32[768,1024]{1,0:T(8,128)S(1)} fusion(bf16[1024,1024]{1,0:T(8,128)(2,1)S(1)} %bitcast.43, bf16[128,8,768]{2,1,0:T(8,128)(2,1)S(1)} %all_to_all.10), kind=kOutput, calls=%fused_computation.11 | convolution fusion | flops 1611399168 | bytes 6815744 | tf_op jit(solution)/shard_map/dot_general | solution.py:246
  108.6 6.5 %shard_map.76 = bf16[8,3,2,16,4096]{4,3,2,1,0:T(8,128)(2,1)} custom-call(f32[3,2,8,16,1024]{4,3,2,1,0:T(8,128)S(1)} %bitcast.35, bf16[8,3,2,16,4096]{4,3,2,1,0:T(8,128)(2,1)} %field_ref.1), custom_call_target="tpu_custom_call" | custom-call | tf_op jit(solution)/shard_map/pallas_call | solution.py:252
  (23 shorter events, 1.0 us)
Async XLA Ops:
  4.4 3.2 %copy-start = (bf16[8,3,2,16,4096]{4,3,2,1,0:T(8,128)(2,1)S(1)}, bf16[8,3,2,16,4096]{4,3,2,1,0:T(8,128)(2,1)}, u32[]{:S(2)}) copy-start(bf16[8,3,2,16,4096]{4,3,2,1,0:T(8,128)(2,1)} %field_ref.1) | copy-start | bytes 18874372
  14.5 11.8 %copy-start.2 = (bf16[32,32]{1,0:T(8,128)(2,1)S(1)}, bf16[32,32]{1,0:T(8,128)(2,1)}, u32[]{:S(2)}) copy-start(bf16[32,32]{1,0:T(8,128)(2,1)} %param.8) | copy-start | bytes 6148
  14.5 11.9 %copy-start.3 = (f32[2,2]{0,1:T(2,128)S(1)}, f32[2,2]{0,1:T(2,128)}, u32[]{:S(2)}) copy-start(f32[2,2]{0,1:T(2,128)} %constant.55.clone) | copy-start | bytes 52
  14.5 12.1 %copy-start.1 = (f32[8,2048]{1,0:T(8,128)S(1)}, f32[8,2048]{1,0:T(8,128)}, u32[]{:S(2)}) copy-start(f32[8,2048]{1,0:T(8,128)} %param.9) | copy-start | bytes 196612
  14.5 38.6 %all-to-all-start = ((bf16[128,8,768]{2,1,0:T(8,128)(2,1)}), bf16[128,8,768]{2,1,0:T(8,128)(2,1)}, u32[]{:S(2)}, u32[]{:S(2)}) async-start(bf16[128,8,768]{2,1,0:T(8,128)(2,1)} %fusion.13), calls=%async_computation | async-start | bytes 3145728 | tf_op jit(solution)/shard_map/all_to_all | solution.py:210

commit v11 on v10

--- a/solution.py
+++ b/solution.py
@@ -247,7 +247,7 @@
         returned, inv, (((0,), (0,)), ((), ())), preferred_element_type=jnp.float32
     ) * ratio
     waveform = waveform.reshape(fields, 2, chans, cycles, period)
-    per_step = 2 if chans % 2 == 0 else 1
+    per_step = 4 if chans % 4 == 0 else 1
     block = (per_step,) + field.shape[1:]
     return pl.pallas_call(
         functools.partial(epilogue_kernel, period=period),

time: 116 us -> 115 us (level)
  no operation moved by 1% of the time
where the time goes in v11:
time: 115 us; the launch traced here: 114 us
  blocking collectives  58.9 us (51%)
  Pallas kernels  22.9 us (20%)
  starting transfers between devices  11.6 us (10%)
  other arithmetic  7.56 us (7%)
  matrix products  6.44 us (6%)
  local copies, waits for them, and re-layouts  6.4 us (6%)
    all_to_all x1, blocking collectives, local(): returned = lax.all_to_all(leaving, ('chan', 'lat'), 0, 0, tiled=True)  33.4 us
    all_gather x1, blocking collectives, local(): all_gain = lax.all_gather(spectral_gain, 'chan', axis=0, tiled=True)  25.5 us
    all_to_all x1, starting transfers between devices, local(): got = lax.all_to_all(sent, ('chan', 'lat'), 0, 0, tiled=True)  11.6 us
    pallas_call x1, Pallas kernels, legendre_stage(): pl.pallas_call(functools.partial(legendre_kernel, block=block), grid_spec...  8.62 us
    pallas_call x1, Pallas kernels, local(): pl.pallas_call(functools.partial(epilogue_kernel, period=period), grid=(c...  5.46 us
    pallas_call x1, Pallas kernels, local(): pl.pallas_call(functools.partial(gather_kernel, piece=piece, per_dev=per_...  5.01 us
    dot_general x1, matrix products, local(): lax.dot_general(jnp.concatenate([fwd, fwd], axis=1), rows, (((1,), (1,)),...  4.61 us
    pallas_call x1, Pallas kernels, local(): pl.pallas_call(functools.partial(scatter_kernel, piece=piece, per_dev=per...  3.78 us
  transfers between devices with their start and end apart: 1, of which 0 were waited for; matrix products, arithmetic and copies ran while one was open for 1% of the time, Pallas kernels for 0%

profile of v11, /device:TPU:0, one launch (start us, length us, event | category | flops | bytes accessed | tf_op | source)
XLA Modules:
  0.0 114.0 jit_solution(10037895514387200371)
XLA Ops:
  0.0 0.7 broadcast_multiply_fusion.1
  0.7 0.1 reshape.113
  1.2 0.2 fusion.28
  1.4 0.3 copy.22
  1.7 0.3 copy.24
  2.0 2.4 %fusion.23 = (f32[128,4,128]{2,1,0:T(4,128)S(1)}, f32[128,4,128]{2,1,0:T(4,128)S(1)}) fusion(s32[128,4]{1,0:T(8,128)S(1)} %copy.23), kind=kLoop, calls=%fused_computation.24 | loop fusion | flops 917504 | bytes 526336 | tf_op jit(solution)/shard_map/cos | solution.py:186
  4.4 2.5 %multiply_convert_fusion = bf16[128,2,4,8,128]{4,3,2,1,0:T(8,128)(2,1)S(1)} fusion(f32[128,4,128]{2,1,0:T(4,128)S(1)} %get-tuple-element.8, f32[128,2,4,8]{3,2,1,0:T(4,128)S(1)} %copy.24, f32[128,4,128]{2,1,0:T(4,128)S(1)} %get-tuple-element.7, f32[128,2,4,8]{3,2,1,0:T(4,128)S(1)} %copy.22), kind=kLoop, calls=%fused_computation.4 | loop fusion | flops 5242880 | bytes 2686976 | tf_op jit(solution)/shard_map/convert_element_type | solution.py:188
  6.9 0.6 copy.35
  7.6 0.8 copy.25
  8.4 1.5 %subtract_convert_fusion = (bf16[768,1024]{1,0:T(8,128)(2,1)S(1)}, bf16[768,1024]{1,0:T(8,128)(2,1)S(1)}) fusion(bf16[768,4096]{1,0:T(8,128)(2,1)S(1)} %bitcast.40), kind=kLoop, calls=%fused_computation.8 | loop fusion | flops 8650752 | bytes 9437184 | tf_op jit(solution)/shard_map/convert_element_type | solution.py:202
  9.9 4.6 %fusion.13 = bf16[128,8,768]{2,1,0:T(8,128)(2,1)} fusion(bf16[768,1024]{1,0:T(8,128)(2,1)S(1)} %get-tuple-element.5, bf16[768,1024]{1,0:T(8,128)(2,1)S(1)} %get-tuple-element.6, bf16[1024,1024]{1,0:T(8,128)(2,1)S(1)} %bitcast.42), kind=kOutput, calls=%fused_computation.15 | convolution fusion | flops 3236691968 | bytes 6815744 | tf_op jit(solution)/shard_map/dot_general | solution.py:204
  14.5 11.6 %all-to-all-start = ((bf16[128,8,768]{2,1,0:T(8,128)(2,1)}), bf16[128,8,768]{2,1,0:T(8,128)(2,1)}, u32[]{:S(2)}, u32[]{:S(2)}) async-start(bf16[128,8,768]{2,1,0:T(8,128)(2,1)} %fusion.13), calls=%async_computation | async-start | bytes 3145728 | tf_op jit(solution)/shard_map/all_to_all | solution.py:210
  26.7 25.5 %all_gather.3 = f32[32,2048]{1,0:T(8,128)S(1)} all-gather(f32[8,2048]{1,0:T(8,128)S(1)} %copy-done.1), channel_id=1, replica_groups=mesh['lat'=32,'chan'=4] {'chan'}, dimensions={0}, use_global_device_ids=true | all-gather | bytes 327680 | tf_op jit(solution)/shard_map/all_gather | solution.py:226
  52.2 0.3 copy.29
  52.6 0.4 copy.30
  53.1 1.7 %copy.36 = bf16[4,32,8,768]{3,1,2,0:T(8,128)(2,1)S(1)} copy(bf16[4,32,8,768]{3,2,1,0:T(8,128)(2,1)} %bitcast.6) | data formatting | bytes 3145728 | tf_op jit(solution)/shard_map/reshape | solution.py:211
  54.8 5.0 %shard_map.73 = bf16[4,2,3,2,32,512]{5,4,3,2,1,0:T(8,128)(2,1)S(1)} custom-call(bf16[4,8,32,768]{3,2,1,0:T(8,128)(2,1)S(1)} %bitcast.38, bf16[64,64]{1,0:T(8,128)(2,1)S(1)} %copy.28.mix_ref), custom_call_target="tpu_custom_call" | custom-call | tf_op jit(solution)/shard_map/pallas_call | solution.py:217
  59.9 0.2 tile.4
  60.1 8.6 %shard_map.74.back_ref = bf16[4,2,192,512]{3,2,1,0:T(8,128)(2,1)S(1)} custom-call(s32[4]{0:T(128)S(1)} %dynamic_slice.3.modes_ref, s32[1]{0:T(128)} %bitcast.1.base_ref, bf16[4,2,192,512]{3,2,1,0:T(8,128)(2,1)S(1)} %bitcast.36, bf16[2,16,512,1024]{3,2,1,0:T(8,128)(2,1)} %leg_ref.1, f32[2,192,1024]{2,1,0:T(8,128)S(1)} %bitcast.37), custom_call_target="tpu_custom_call" | custom-call | flops 3221225472 | bytes 13107200 | tf_op jit(solution)/shard_map/pallas_call | solution.py:147
  68.7 3.8 %shard_map.75 = bf16[4,8,32,768]{3,2,1,0:T(8,128)(2,1)S(1)} custom-call(bf16[4,2,192,512]{3,2,1,0:T(8,128)(2,1)S(1)} %shard_map.74.back_ref), custom_call_target="tpu_custom_call" | custom-call | tf_op jit(solution)/shard_map/pallas_call | solution.py:237
  72.5 0.9 copy.31
  73.3 33.4 %all_to_all.10 = bf16[128,8,768]{2,1,0:T(8,128)(2,1)S(1)} all-to-all(bf16[128,8,768]{2,1,0:T(8,128)(2,1)S(1)} %bitcast.44), channel_id=1, replica_groups=mesh['lat'=32,'chan'=4] {'chan','lat'}, dimensions={0} | all-to-all | bytes 3145728 | tf_op jit(solution)/shard_map/all_to_all | solution.py:243
  106.7 1.8 %convolution_multiply_fusion = f32[768,1024]{1,0:T(8,128)S(1)} fusion(bf16[1024,1024]{1,0:T(8,128)(2,1)S(1)} %bitcast.43, bf16[128,8,768]{2,1,0:T(8,128)(2,1)S(1)} %all_to_all.10), kind=kOutput, calls=%fused_computation.11 | convolution fusion | flops 1611399168 | bytes 6815744 | tf_op jit(solution)/shard_map/dot_general | solution.py:246
  108.6 5.5 %shard_map.76 = bf16[8,3,2,16,4096]{4,3,2,1,0:T(8,128)(2,1)} custom-call(f32[3,2,8,16,1024]{4,3,2,1,0:T(8,128)S(1)} %bitcast.35, bf16[8,3,2,16,4096]{4,3,2,1,0:T(8,128)(2,1)} %field_ref.1), custom_call_target="tpu_custom_call" | custom-call | tf_op jit(solution)/shard_map/pallas_call | solution.py:252
  (23 shorter events, 1.0 us)
Async XLA Ops:
  4.4 3.2 %copy-start = (bf16[8,3,2,16,4096]{4,3,2,1,0:T(8,128)(2,1)S(1)}, bf16[8,3,2,16,4096]{4,3,2,1,0:T(8,128)(2,1)}, u32[]{:S(2)}) copy-start(bf16[8,3,2,16,4096]{4,3,2,1,0:T(8,128)(2,1)} %field_ref.1) | copy-start | bytes 18874372
  14.5 11.8 %copy-start.2 = (bf16[32,32]{1,0:T(8,128)(2,1)S(1)}, bf16[32,32]{1,0:T(8,128)(2,1)}, u32[]{:S(2)}) copy-start(bf16[32,32]{1,0:T(8,128)(2,1)} %param.8) | copy-start | bytes 6148
  14.5 11.9 %copy-start.3 = (f32[2,2]{0,1:T(2,128)S(1)}, f32[2,2]{0,1:T(2,128)}, u32[]{:S(2)}) copy-start(f32[2,2]{0,1:T(2,128)} %constant.55.clone) | copy-start | bytes 52
  14.5 12.1 %copy-start.1 = (f32[8,2048]{1,0:T(8,128)S(1)}, f32[8,2048]{1,0:T(8,128)}, u32[]{:S(2)}) copy-start(f32[8,2048]{1,0:T(8,128)} %param.9) | copy-start | bytes 196612
  14.5 38.6 %all-to-all-start = ((bf16[128,8,768]{2,1,0:T(8,128)(2,1)}), bf16[128,8,768]{2,1,0:T(8,128)(2,1)}, u32[]{:S(2)}, u32[]{:S(2)}) async-start(bf16[128,8,768]{2,1,0:T(8,128)(2,1)} %fusion.13), calls=%async_computation | async-start | bytes 3145728 | tf_op jit(solution)/shard_map/all_to_all | solution.py:210

commit v12 on v11

--- a/solution.py
+++ b/solution.py
@@ -123,8 +123,11 @@
                 return acc + lax.dot_general(
                     kept, table, (((1,), (1,)), ((), ())), preferred_element_type=jnp.float32
                 )
-            top = 2 * ((b + 1) * block - 1) + p
-            acc = lax.cond(top >= mode, step, lambda a: a, acc)
+            if half_deg // block == 1:
+                acc = step(acc)
+            else:
+                top = 2 * ((b + 1) * block - 1) + p
+                acc = lax.cond(top >= mode, step, lambda a: a, acc)
         syn.append(acc)
     out_ref[0, 0] = (syn[0] + syn[1]).astype(out_ref.dtype)
     out_ref[0, 1] = (syn[0] - syn[1]).astype(out_ref.dtype)

time: 115 us -> 114 us (level)
  no operation moved by 1% of the time
where the time goes in v12:
time: 114 us; the launch traced here: 113 us
  blocking collectives  58.9 us (52%)
  Pallas kernels  21.9 us (19%)
  starting transfers between devices  11.6 us (10%)
  other arithmetic  7.56 us (7%)
  matrix products  6.44 us (6%)
  local copies, waits for them, and re-layouts  6.4 us (6%)
    all_to_all x1, blocking collectives, local(): returned = lax.all_to_all(leaving, ('chan', 'lat'), 0, 0, tiled=True)  33.4 us
    all_gather x1, blocking collectives, local(): all_gain = lax.all_gather(spectral_gain, 'chan', axis=0, tiled=True)  25.5 us
    all_to_all x1, starting transfers between devices, local(): got = lax.all_to_all(sent, ('chan', 'lat'), 0, 0, tiled=True)  11.6 us
    pallas_call x1, Pallas kernels, legendre_stage(): pl.pallas_call(functools.partial(legendre_kernel, block=block), grid_spec...  7.69 us
    pallas_call x1, Pallas kernels, local(): pl.pallas_call(functools.partial(epilogue_kernel, period=period), grid=(c...  5.46 us
    pallas_call x1, Pallas kernels, local(): pl.pallas_call(functools.partial(gather_kernel, piece=piece, per_dev=per_...  5.01 us
    dot_general x1, matrix products, local(): lax.dot_general(jnp.concatenate([fwd, fwd], axis=1), rows, (((1,), (1,)),...  4.61 us
    pallas_call x1, Pallas kernels, local(): pl.pallas_call(functools.partial(scatter_kernel, piece=piece, per_dev=per...  3.78 us
  transfers between devices with their start and end apart: 1, of which 0 were waited for; matrix products, arithmetic and copies ran while one was open for 1% of the time, Pallas kernels for 0%

profile of v12, /device:TPU:0, one launch (start us, length us, event | category | flops | bytes accessed | tf_op | source)
XLA Modules:
  0.0 113.1 jit_solution(5426336433194125148)
XLA Ops:
  0.0 0.7 broadcast_multiply_fusion.1
  0.7 0.1 reshape.113
  1.2 0.2 fusion.28
  1.4 0.3 copy.22
  1.7 0.3 copy.24
  2.0 2.4 %fusion.23 = (f32[128,4,128]{2,1,0:T(4,128)S(1)}, f32[128,4,128]{2,1,0:T(4,128)S(1)}) fusion(s32[128,4]{1,0:T(8,128)S(1)} %copy.23), kind=kLoop, calls=%fused_computation.24 | loop fusion | flops 917504 | bytes 526336 | tf_op jit(solution)/shard_map/cos | solution.py:189
  4.4 2.5 %multiply_convert_fusion = bf16[128,2,4,8,128]{4,3,2,1,0:T(8,128)(2,1)S(1)} fusion(f32[128,4,128]{2,1,0:T(4,128)S(1)} %get-tuple-element.8, f32[128,2,4,8]{3,2,1,0:T(4,128)S(1)} %copy.24, f32[128,4,128]{2,1,0:T(4,128)S(1)} %get-tuple-element.7, f32[128,2,4,8]{3,2,1,0:T(4,128)S(1)} %copy.22), kind=kLoop, calls=%fused_computation.4 | loop fusion | flops 5242880 | bytes 2686976 | tf_op jit(solution)/shard_map/convert_element_type | solution.py:191
  6.9 0.6 copy.35
  7.6 0.8 copy.25
  8.4 1.5 %subtract_convert_fusion = (bf16[768,1024]{1,0:T(8,128)(2,1)S(1)}, bf16[768,1024]{1,0:T(8,128)(2,1)S(1)}) fusion(bf16[768,4096]{1,0:T(8,128)(2,1)S(1)} %bitcast.40), kind=kLoop, calls=%fused_computation.8 | loop fusion | flops 8650752 | bytes 9437184 | tf_op jit(solution)/shard_map/convert_element_type | solution.py:205
  9.9 4.6 %fusion.13 = bf16[128,8,768]{2,1,0:T(8,128)(2,1)} fusion(bf16[768,1024]{1,0:T(8,128)(2,1)S(1)} %get-tuple-element.5, bf16[768,1024]{1,0:T(8,128)(2,1)S(1)} %get-tuple-element.6, bf16[1024,1024]{1,0:T(8,128)(2,1)S(1)} %bitcast.42), kind=kOutput, calls=%fused_computation.15 | convolution fusion | flops 3236691968 | bytes 6815744 | tf_op jit(solution)/shard_map/dot_general | solution.py:207
  14.5 11.6 %all-to-all-start = ((bf16[128,8,768]{2,1,0:T(8,128)(2,1)}), bf16[128,8,768]{2,1,0:T(8,128)(2,1)}, u32[]{:S(2)}, u32[]{:S(2)}) async-start(bf16[128,8,768]{2,1,0:T(8,128)(2,1)} %fusion.13), calls=%async_computation | async-start | bytes 3145728 | tf_op jit(solution)/shard_map/all_to_all | solution.py:213
  26.7 25.5 %all_gather.3 = f32[32,2048]{1,0:T(8,128)S(1)} all-gather(f32[8,2048]{1,0:T(8,128)S(1)} %copy-done.1), channel_id=1, replica_groups=mesh['lat'=32,'chan'=4] {'chan'}, dimensions={0}, use_global_device_ids=true | all-gather | bytes 327680 | tf_op jit(solution)/shard_map/all_gather | solution.py:229
  52.2 0.3 copy.29
  52.6 0.4 copy.30
  53.1 1.7 %copy.36 = bf16[4,32,8,768]{3,1,2,0:T(8,128)(2,1)S(1)} copy(bf16[4,32,8,768]{3,2,1,0:T(8,128)(2,1)} %bitcast.6) | data formatting | bytes 3145728 | tf_op jit(solution)/shard_map/reshape | solution.py:214
  54.8 5.0 %shard_map.73 = bf16[4,2,3,2,32,512]{5,4,3,2,1,0:T(8,128)(2,1)S(1)} custom-call(bf16[4,8,32,768]{3,2,1,0:T(8,128)(2,1)S(1)} %bitcast.38, bf16[64,64]{1,0:T(8,128)(2,1)S(1)} %copy.28.mix_ref), custom_call_target="tpu_custom_call" | custom-call | tf_op jit(solution)/shard_map/pallas_call | solution.py:220
  59.9 0.2 tile.4
  60.1 7.7 %shard_map.74.back_ref = bf16[4,2,192,512]{3,2,1,0:T(8,128)(2,1)S(1)} custom-call(s32[4]{0:T(128)S(1)} %dynamic_slice.3.modes_ref, s32[1]{0:T(128)} %bitcast.1.base_ref, bf16[4,2,192,512]{3,2,1,0:T(8,128)(2,1)S(1)} %bitcast.36, bf16[2,16,512,1024]{3,2,1,0:T(8,128)(2,1)} %leg_ref.1, f32[2,192,1024]{2,1,0:T(8,128)S(1)} %bitcast.37), custom_call_target="tpu_custom_call" | custom-call | flops 3221225472 | bytes 13107200 | tf_op jit(solution)/shard_map/pallas_call | solution.py:150
  67.7 3.8 %shard_map.75 = bf16[4,8,32,768]{3,2,1,0:T(8,128)(2,1)S(1)} custom-call(bf16[4,2,192,512]{3,2,1,0:T(8,128)(2,1)S(1)} %shard_map.74.back_ref), custom_call_target="tpu_custom_call" | custom-call | tf_op jit(solution)/shard_map/pallas_call | solution.py:240
  71.5 0.9 copy.31
  72.4 33.4 %all_to_all.10 = bf16[128,8,768]{2,1,0:T(8,128)(2,1)S(1)} all-to-all(bf16[128,8,768]{2,1,0:T(8,128)(2,1)S(1)} %bitcast.44), channel_id=1, replica_groups=mesh['lat'=32,'chan'=4] {'chan','lat'}, dimensions={0} | all-to-all | bytes 3145728 | tf_op jit(solution)/shard_map/all_to_all | solution.py:246
  105.8 1.8 %convolution_multiply_fusion = f32[768,1024]{1,0:T(8,128)S(1)} fusion(bf16[1024,1024]{1,0:T(8,128)(2,1)S(1)} %bitcast.43, bf16[128,8,768]{2,1,0:T(8,128)(2,1)S(1)} %all_to_all.10), kind=kOutput, calls=%fused_computation.11 | convolution fusion | flops 1611399168 | bytes 6815744 | tf_op jit(solution)/shard_map/dot_general | solution.py:249
  107.6 5.5 %shard_map.76 = bf16[8,3,2,16,4096]{4,3,2,1,0:T(8,128)(2,1)} custom-call(f32[3,2,8,16,1024]{4,3,2,1,0:T(8,128)S(1)} %bitcast.35, bf16[8,3,2,16,4096]{4,3,2,1,0:T(8,128)(2,1)} %field_ref.1), custom_call_target="tpu_custom_call" | custom-call | tf_op jit(solution)/shard_map/pallas_call | solution.py:255
  (23 shorter events, 1.0 us)
Async XLA Ops:
  4.4 3.2 %copy-start = (bf16[8,3,2,16,4096]{4,3,2,1,0:T(8,128)(2,1)S(1)}, bf16[8,3,2,16,4096]{4,3,2,1,0:T(8,128)(2,1)}, u32[]{:S(2)}) copy-start(bf16[8,3,2,16,4096]{4,3,2,1,0:T(8,128)(2,1)} %field_ref.1) | copy-start | bytes 18874372
  14.5 11.8 %copy-start.2 = (bf16[32,32]{1,0:T(8,128)(2,1)S(1)}, bf16[32,32]{1,0:T(8,128)(2,1)}, u32[]{:S(2)}) copy-start(bf16[32,32]{1,0:T(8,128)(2,1)} %param.8) | copy-start | bytes 6148
  14.5 11.9 %copy-start.3 = (f32[2,2]{0,1:T(2,128)S(1)}, f32[2,2]{0,1:T(2,128)}, u32[]{:S(2)}) copy-start(f32[2,2]{0,1:T(2,128)} %constant.55.clone) | copy-start | bytes 52
  14.5 12.1 %copy-start.1 = (f32[8,2048]{1,0:T(8,128)S(1)}, f32[8,2048]{1,0:T(8,128)}, u32[]{:S(2)}) copy-start(f32[8,2048]{1,0:T(8,128)} %param.9) | copy-start | bytes 196612
  14.5 38.6 %all-to-all-start = ((bf16[128,8,768]{2,1,0:T(8,128)(2,1)}), bf16[128,8,768]{2,1,0:T(8,128)(2,1)}, u32[]{:S(2)}, u32[]{:S(2)}) async-start(bf16[128,8,768]{2,1,0:T(8,128)(2,1)} %fusion.13), calls=%async_computation | async-start | bytes 3145728 | tf_op jit(solution)/shard_map/all_to_all | solution.py:213
